TPU v7x, 128 devices: a whole 4x4x4 slice. The times are simulated.
128 devices in a mesh: dp: 2 (over x_hi), seq: 8 (over z, core), expert: 8 (over x_lo, y).
Axes of the slice: x: 4 (x_hi: 2, x_lo: 2; x = x_hi * 2 + x_lo), y: 4, z: 4, core: 2. Of those that a mesh axis runs over, the one named last changes fastest.
Arguments:
- tokens: bfloat16 [32768, 2048], P(('dp', 'seq', 'expert')), may hold values from -6 to 6
- grad_out: bfloat16 [32768, 2048], P(('dp', 'seq', 'expert')), may hold values from -6 to 6
- route_weights: bfloat16 [32768, 2], P(('dp', 'seq', 'expert')), may hold values from 0.099609375 to 1
- expert_ids: int32 [32768, 2], P(('dp', 'seq', 'expert')), may hold values from 0 to 63, as said below
- route_slots: int32 [32768, 2], P(('dp', 'seq', 'expert')), may hold values from 0 to 7, as said below
- w_gate: bfloat16 [64, 2048, 1024], P(('seq', 'expert')), may hold values from -0.125 to 0.125
- w_up: bfloat16 [64, 2048, 1024], P(('seq', 'expert')), may hold values from -0.125 to 0.125
- w_down: bfloat16 [64, 2048, 1024], P(('seq', 'expert')), may hold values from -0.1875 to 0.1875
Outputs:
- grad_tokens: bfloat16 [32768, 2048], P(('dp', 'seq', 'expert'))
- grad_gate: bfloat16 [64, 2048, 1024], P(('seq', 'expert'), 'dp')
- grad_up: bfloat16 [64, 2048, 1024], P(('seq', 'expert'), 'dp')
- grad_down: bfloat16 [64, 2048, 1024], P(('seq', 'expert'), 'dp')
Inputs may be any that keep to these rules, and one draw needn't show every extreme that they name: `expert_ids`: in every block of 256 cells, a cell's two experts differ, each expert is named by exactly 8 of the block's routes, and the experts fall into two halves drawn from the seed with each cell naming one expert of each half. `route_slots`: within a block the routes to one expert take the slots 0 to 7, each once.
All inputs are finite; a program needn't handle non-finite values.
Results may differ from a plain program's by a relative error of at most 0.0065.
Values may be sent and summed in bfloat16 or wider, within the bound.
No kernel may reach another device: no remote copies, remote signals or barrier semaphores. Data moves between devices by JAX's collectives and lax.ppermute only.
A program may use at most 128 MiB of HBM per device.

v0:
```python
import jax
import jax.numpy as jnp
from jax import lax
from jax.sharding import PartitionSpec as P

E = 64


def per_device(tokens, grad_out, route_weights, expert_ids, route_slots, w_gate, w_up, w_down):
    seq_count = lax.axis_size("seq")
    exp_count = lax.axis_size("expert")
    group = seq_count * exp_count
    exp_local = w_gate.shape[0]
    cell_count = tokens.shape[0]
    width = tokens.shape[1]
    slot_count = 2 * cell_count // E
    position = expert_ids * slot_count + route_slots
    cells = jnp.arange(cell_count, dtype=jnp.int32)
    table = (
        jnp.zeros((E * slot_count,), jnp.int32)
        .at[position]
        .set(jnp.broadcast_to(cells[:, None], (cell_count, 2)))
    )
    weight_table = jnp.zeros((E * slot_count,), jnp.bfloat16).at[position].set(route_weights)
    send_x = tokens[table].reshape(group, exp_local, slot_count, width)
    send_g = grad_out[table].reshape(group, exp_local, slot_count, width)
    send_c = weight_table.reshape(group, exp_local, slot_count)
    recv_x, recv_g, recv_c = (
        lax.all_to_all(send_x, ("seq", "expert"), split_axis=0, concat_axis=0, tiled=True),
        lax.all_to_all(send_g, ("seq", "expert"), split_axis=0, concat_axis=0, tiled=True),
        lax.all_to_all(send_c, ("seq", "expert"), split_axis=0, concat_axis=0, tiled=True),
    )
    gate_pre = jnp.einsum("gesd,edf->gesf", recv_x, w_gate, preferred_element_type=jnp.float32)
    up_pre = jnp.einsum("gesd,edf->gesf", recv_x, w_up, preferred_element_type=jnp.float32)
    gate_sig = jax.nn.sigmoid(gate_pre)
    silu_g = gate_pre * gate_sig
    act = (silu_g * up_pre).astype(jnp.bfloat16)
    route_grad = (recv_c.astype(jnp.float32)[..., None] * recv_g.astype(jnp.float32)).astype(
        jnp.bfloat16
    )
    act_grad = jnp.einsum("gesd,edf->gesf", route_grad, w_down, preferred_element_type=jnp.float32)
    gate_grad = (act_grad * up_pre * gate_sig * (1.0 + gate_pre * (1.0 - gate_sig))).astype(
        jnp.bfloat16
    )
    up_grad = (act_grad * silu_g).astype(jnp.bfloat16)
    acc_gate = jnp.einsum("gesd,gesf->edf", recv_x, gate_grad, preferred_element_type=jnp.float32)
    acc_up = jnp.einsum("gesd,gesf->edf", recv_x, up_grad, preferred_element_type=jnp.float32)
    acc_down = jnp.einsum("gesd,gesf->edf", route_grad, act, preferred_element_type=jnp.float32)
    back = jnp.einsum("gesf,edf->gesd", gate_grad, w_gate, preferred_element_type=jnp.float32)
    back = (
        back + jnp.einsum("gesf,edf->gesd", up_grad, w_up, preferred_element_type=jnp.float32)
    ).astype(jnp.bfloat16)
    returned = lax.all_to_all(back, ("seq", "expert"), split_axis=0, concat_axis=0, tiled=True)
    returned = returned.reshape(E * slot_count, width)
    grad_tokens = (
        returned[position[:, 0]].astype(jnp.float32) + returned[position[:, 1]].astype(jnp.float32)
    ).astype(jnp.bfloat16)
    grad_gate, grad_up, grad_down = (
        lax.psum_scatter(
            acc_gate.astype(jnp.bfloat16), "dp", scatter_dimension=1, tiled=True
        ).astype(jnp.float32),
        lax.psum_scatter(acc_up.astype(jnp.bfloat16), "dp", scatter_dimension=1, tiled=True).astype(
            jnp.float32
        ),
        lax.psum_scatter(
            acc_down.astype(jnp.bfloat16), "dp", scatter_dimension=1, tiled=True
        ).astype(jnp.float32),
    )
    return (
        grad_tokens,
        grad_gate.astype(jnp.bfloat16),
        grad_up.astype(jnp.bfloat16),
        grad_down.astype(jnp.bfloat16),
    )


def solution(mesh):
    return jax.shard_map(
        per_device,
        mesh=mesh,
        in_specs=(
            P(("dp", "seq", "expert"), None),
            P(("dp", "seq", "expert"), None),
            P(("dp", "seq", "expert"), None),
            P(("dp", "seq", "expert"), None),
            P(("dp", "seq", "expert"), None),
            P(("seq", "expert"), None, None),
            P(("seq", "expert"), None, None),
            P(("seq", "expert"), None, None),
        ),
        out_specs=(
            P(("dp", "seq", "expert"), None),
            P(("seq", "expert"), "dp", None),
            P(("seq", "expert"), "dp", None),
            P(("seq", "expert"), "dp", None),
        ),
        check_vma=False,
    )
```

profile of v0, /device:TPU:1, one launch (start us, length us, event | category | flops | bytes accessed | tf_op | source)
XLA Modules:
  0.0 308.8 jit_solution(5543751386247432382)
XLA Ops:
  7.2 0.0 copy-start
  7.2 0.9 copy.30
  8.1 0.1 reshape.118
  8.2 1.3 compare_select_fusion
  9.5 0.1 copy.29
  9.7 0.1 reshape.116
  9.8 3.8 %scatter_custom_fusion = bf16[512]{0:T(512)(128)(2,1)S(1)} fusion(s32[512]{0:T(512)S(1)} %reshape.116, bf16[512]{0:T(512)(128)(2,1)S(1)} %reshape.118, bf16[]{:T(256)} %constant.6.clone.1), kind=kCustom, calls=%fused_computation.60 | custom fusion | bytes 1026 | tf_op jit(solution)/shard_map/scatter | solution.py:24
  13.6 0.7 reshape.142
  14.3 10.9 %all-to-all-start = ((bf16[64,1,8]{2,1,0:T(2,128)(2,1)}), bf16[64,1,8]{2,1,0:T(2,128)(2,1)S(1)}, u32[]{:S(2)}, u32[]{:S(2)}) async-start(bf16[64,1,8]{2,1,0:T(2,128)(2,1)} %reshape.142), calls=%async_computation | async-start | bytes 65536 | tf_op jit(solution)/shard_map/all_to_all | solution.py:31
  25.3 0.1 reshape.126
  25.4 2.4 scatter_custom_fusion.1
  27.9 0.0 copy-done
  27.9 3.3 %gather_fusion.1 = bf16[512,2048]{1,0:T(8,128)(2,1)} fusion(bf16[256,2048]{1,0:T(8,128)(2,1)S(1)} %copy-done, s32[1024]{0:T(1024)S(1)} %pad_clamp_fusion.2), kind=kCustom, calls=%fused_computation.1 | custom fusion | bytes 4196352 | tf_op jit(solution)/shard_map/gather | solution.py:25
  31.2 1.8 all-to-all-done
  32.9 7.4 %all-to-all-start.2 = ((bf16[64,1,8,2048]{3,2,1,0:T(8,128)(2,1)}), bf16[64,1,8,2048]{3,2,1,0:T(8,128)(2,1)}, u32[]{:S(2)}, u32[]{:S(2)}) async-start(bf16[64,1,8,2048]{3,2,1,0:T(8,128)(2,1)} %bitcast.146), calls=%async_computation.2 | async-start | bytes 4194304 | tf_op jit(solution)/shard_map/all_to_all | solution.py:29
  40.3 0.0 copy-done.1
  40.3 3.3 %gather_fusion = bf16[512,2048]{1,0:T(8,128)(2,1)} fusion(bf16[256,2048]{1,0:T(8,128)(2,1)S(1)} %copy-done.1, s32[1024]{0:T(1024)S(1)} %pad_clamp_fusion.2), kind=kCustom, calls=%fused_computation | custom fusion | bytes 4196352 | tf_op jit(solution)/shard_map/gather | solution.py:26
  43.6 25.1 %all-to-all-done.2 = bf16[64,1,8,2048]{3,2,1,0:T(8,128)(2,1)} async-done(((bf16[64,1,8,2048]{3,2,1,0:T(8,128)(2,1)}), bf16[64,1,8,2048]{3,2,1,0:T(8,128)(2,1)}, u32[]{:S(2)}, u32[]{:S(2)}) %all-to-all-start.2) | async-done | bytes 2097184 | tf_op jit(solution)/shard_map/all_to_all | solution.py:29
  68.7 5.0 %all-to-all-start.1 = ((bf16[64,1,8,2048]{3,2,1,0:T(8,128)(2,1)}), bf16[64,1,8,2048]{3,2,1,0:T(8,128)(2,1)S(1)}, u32[]{:S(2)}, u32[]{:S(2)}) async-start(bf16[64,1,8,2048]{3,2,1,0:T(8,128)(2,1)} %bitcast.145), calls=%async_computation.1 | async-start | bytes 4194304 | tf_op jit(solution)/shard_map/all_to_all | solution.py:30
  73.7 0.2 reduce-scatter.8.cloned.1.call-start
  74.0 0.0 copy-start.3
  74.0 6.6 %fusion.2 = f32[64,8,1024]{2,1,0:T(8,128)} fusion(bf16[1,2048,1024]{2,1,0:T(8,128)(2,1)} %param.13, bf16[64,1,8,2048]{3,2,1,0:T(8,128)(2,1)} %all-to-all-done.2), kind=kOutput, calls=%fused_computation.11 | convolution fusion | flops 2147483648 | bytes 8388608 | tf_op jit(solution)/shard_map/gesd,edf->gesf/dot_general | solution.py:33
  80.6 0.0 copy-done.3
  80.6 5.3 %fusion.6 = f32[64,8,1024]{2,1,0:T(8,128)} fusion(bf16[1,2048,1024]{2,1,0:T(8,128)(2,1)S(1)} %copy-done.3, bf16[64,1,8,2048]{3,2,1,0:T(8,128)(2,1)} %all-to-all-done.2), kind=kOutput, calls=%fused_computation.15 | convolution fusion | flops 2147483648 | bytes 8388608 | tf_op jit(solution)/shard_map/gesd,edf->gesf/dot_general | solution.py:34
  85.9 16.2 %all-to-all-done.1 = bf16[64,1,8,2048]{3,2,1,0:T(8,128)(2,1)S(1)} async-done(((bf16[64,1,8,2048]{3,2,1,0:T(8,128)(2,1)}), bf16[64,1,8,2048]{3,2,1,0:T(8,128)(2,1)S(1)}, u32[]{:S(2)}, u32[]{:S(2)}) %all-to-all-start.1) | async-done | bytes 2097184 | tf_op jit(solution)/shard_map/all_to_all | solution.py:30
  102.2 6.7 %fusion.12 = bf16[1,2048,1024]{2,1,0:T(8,128)(2,1)} fusion(bf16[64,1,8,2048]{3,2,1,0:T(8,128)(2,1)S(1)} %all-to-all-done.1, f32[64,8]{1,0:T(8,128)S(1)} %bitcast.147, f32[64,8,1024]{2,1,0:T(8,128)} %fusion.6, f32[64,8,1024]{2,1,0:T(8,128)} %fusion.2), kind=kOutput, calls=%fused_computation.23 | convolution fusion | flops 2155872256 | bytes 10487808 | tf_op jit(solution)/shard_map/gesd,gesf->edf/dot_general | solution.py:48
  108.9 0.0 reduce-scatter.8.cloned.1.call-update
  108.9 0.0 reduce-scatter.6.cloned.1.call-start
  109.0 7.3 %fusion.34 = (bf16[64,8,1024]{2,1,0:T(8,128)(2,1)S(1)}, bf16[64,1,8,1024]{3,2,0,1:T(8,128)(2,1)}) fusion(f32[64,8,1024]{2,1,0:T(8,128)} %fusion.2, f32[64,8,1024]{2,1,0:T(8,128)} %fusion.6, bf16[1,2048,1024]{2,1,0:T(8,128)(2,1)} %param.15, bf16[64,1,8,2048]{3,2,1,0:T(8,128)(2,1)S(1)} %all-to-all-done.1, f32[64,8]{1,0:T(8,128)S(1)} %bitcast.148), kind=kOutput, calls=%fused_computation.46 | convolution fusion | flops 2157445120 | bytes 12584960 | tf_op jit(solution)/shard_map/gesd,edf->gesf/dot_general | solution.py:41
  116.3 1.0 copy-done.5
  117.3 6.0 %fusion.11 = bf16[1,2048,1024]{2,1,0:T(8,128)(2,1)} fusion(bf16[64,8,1024]{2,1,0:T(8,128)(2,1)S(1)} %get-tuple-element.6, bf16[64,1,8,2048]{3,2,1,0:T(8,128)(2,1)} %all-to-all-done.2), kind=kOutput, calls=%fused_computation.22 | convolution fusion | flops 2149580800 | bytes 7340032 | tf_op jit(solution)/shard_map/gesd,gesf->edf/dot_general | solution.py:47
  123.2 0.0 reduce-scatter.6.cloned.1.call-update
  123.3 0.3 reduce-scatter.4.cloned.1.call-start
  123.5 0.9 copy-done.7
  124.5 6.1 %fusion.10 = bf16[1,2048,1024]{2,1,0:T(8,128)(2,1)} fusion(bf16[64,1,8,2048]{3,2,1,0:T(8,128)(2,1)} %all-to-all-done.2, bf16[64,1,8,1024]{3,2,0,1:T(8,128)(2,1)S(1)} %copy-done.7), kind=kOutput, calls=%fused_computation.21 | convolution fusion | flops 2149580800 | bytes 7340032 | tf_op jit(solution)/shard_map/gesd,gesf->edf/dot_general | solution.py:46
  130.5 0.0 reduce-scatter.4.cloned.1.call-update
  130.6 0.0 copy-start.4
  130.6 0.0 copy-start.6
  130.6 4.8 %fusion = f32[64,8,2048]{2,1,0:T(8,128)S(1)} fusion(bf16[1,2048,1024]{2,1,0:T(8,128)(2,1)} %param.13, bf16[64,1,8,1024]{3,2,0,1:T(8,128)(2,1)S(1)} %copy-done.7), kind=kOutput, calls=%fused_computation.9 | convolution fusion | flops 2147483648 | bytes 9437184 | tf_op jit(solution)/shard_map/gesf,edf->gesd/dot_general | solution.py:49
  135.4 0.0 copy-done.4
  135.5 3.8 %fusion.15 = bf16[64,1,8,2048]{3,2,1,0:T(8,128)(2,1)} fusion(f32[64,8,2048]{2,1,0:T(8,128)S(1)} %fusion, bf16[64,8,1024]{2,1,0:T(8,128)(2,1)S(1)} %copy-done.6, bf16[1,2048,1024]{2,1,0:T(8,128)(2,1)S(1)} %copy-done.4), kind=kOutput, calls=%fused_computation.24 | convolution fusion | flops 2149580800 | bytes 11534336 | tf_op jit(solution)/shard_map/gesf,edf->gesd/dot_general | solution.py:51
  139.2 5.0 %all-to-all-start.3 = ((bf16[64,1,8,2048]{3,2,1,0:T(8,128)(2,1)}), bf16[64,1,8,2048]{3,2,1,0:T(8,128)(2,1)S(1)}, u32[]{:S(2)}, u32[]{:S(2)}) async-start(bf16[64,1,8,2048]{3,2,1,0:T(8,128)(2,1)} %fusion.15), calls=%async_computation.3 | async-start | bytes 4194304 | tf_op jit(solution)/shard_map/all_to_all | solution.py:53
  144.3 44.2 %all-to-all-done.3 = bf16[64,1,8,2048]{3,2,1,0:T(8,128)(2,1)S(1)} async-done(((bf16[64,1,8,2048]{3,2,1,0:T(8,128)(2,1)}), bf16[64,1,8,2048]{3,2,1,0:T(8,128)(2,1)S(1)}, u32[]{:S(2)}, u32[]{:S(2)}) %all-to-all-start.3) | async-done | bytes 2097184 | tf_op jit(solution)/shard_map/all_to_all | solution.py:53
  188.5 2.3 gather_fusion.3
  190.8 2.4 gather_fusion.2
  193.2 2.9 add_convert_fusion.1
  196.2 45.4 %reduce-scatter.6.cloned.1.call-done = bf16[1,1024,1024]{2,1,0:T(8,128)(2,1)} async-done(((bf16[1,2048,1024]{2,1,0:T(8,128)(2,1)}), bf16[1,1024,1024]{2,1,0:T(8,128)(2,1)}) %reduce-scatter.6.cloned.1.call-update) | async-done | bytes 2097168 | tf_op jit(solution)/shard_map/reduce_scatter | solution.py:62
  241.5 60.8 %reduce-scatter.4.cloned.1.call-done = bf16[1,1024,1024]{2,1,0:T(8,128)(2,1)} async-done(((bf16[1,2048,1024]{2,1,0:T(8,128)(2,1)}), bf16[1,1024,1024]{2,1,0:T(8,128)(2,1)}) %reduce-scatter.4.cloned.1.call-update) | async-done | bytes 2097168 | tf_op jit(solution)/shard_map/reduce_scatter | solution.py:59
  (14 shorter events, 0.1 us)
Async XLA Ops:
  7.2 20.7 %copy-start = (bf16[256,2048]{1,0:T(8,128)(2,1)S(1)}, bf16[256,2048]{1,0:T(8,128)(2,1)}, u32[]{:S(2)}) copy-start(bf16[256,2048]{1,0:T(8,128)(2,1)} %param.8) | copy-start | bytes 3145732
  14.3 18.6 %all-to-all-start = ((bf16[64,1,8]{2,1,0:T(2,128)(2,1)}), bf16[64,1,8]{2,1,0:T(2,128)(2,1)S(1)}, u32[]{:S(2)}, u32[]{:S(2)}) async-start(bf16[64,1,8]{2,1,0:T(2,128)(2,1)} %reshape.142), calls=%async_computation | async-start | bytes 65536 | tf_op jit(solution)/shard_map/all_to_all | solution.py:31
  32.9 7.4 %copy-start.1 = (bf16[256,2048]{1,0:T(8,128)(2,1)S(1)}, bf16[256,2048]{1,0:T(8,128)(2,1)}, u32[]{:S(2)}) copy-start(bf16[256,2048]{1,0:T(8,128)(2,1)} %param.9) | copy-start | bytes 3145732
  32.9 35.8 %all-to-all-start.2 = ((bf16[64,1,8,2048]{3,2,1,0:T(8,128)(2,1)}), bf16[64,1,8,2048]{3,2,1,0:T(8,128)(2,1)}, u32[]{:S(2)}, u32[]{:S(2)}) async-start(bf16[64,1,8,2048]{3,2,1,0:T(8,128)(2,1)} %bitcast.146), calls=%async_computation.2 | async-start | bytes 4194304 | tf_op jit(solution)/shard_map/all_to_all | solution.py:29
  68.7 33.5 %all-to-all-start.1 = ((bf16[64,1,8,2048]{3,2,1,0:T(8,128)(2,1)}), bf16[64,1,8,2048]{3,2,1,0:T(8,128)(2,1)S(1)}, u32[]{:S(2)}, u32[]{:S(2)}) async-start(bf16[64,1,8,2048]{3,2,1,0:T(8,128)(2,1)} %bitcast.145), calls=%async_computation.1 | async-start | bytes 4194304 | tf_op jit(solution)/shard_map/all_to_all | solution.py:30
  73.7 122.5 %reduce-scatter.8.cloned.1.call-start = ((), (), s32[]{:S(2)}) async-start(), calls=%async_computation.9 | async-start | bytes 6291456 | tf_op jit(solution)/shard_map/reduce_scatter | solution.py:65
  74.0 6.6 %copy-start.3 = (bf16[1,2048,1024]{2,1,0:T(8,128)(2,1)S(1)}, bf16[1,2048,1024]{2,1,0:T(8,128)(2,1)}, u32[]{:S(2)}) copy-start(bf16[1,2048,1024]{2,1,0:T(8,128)(2,1)} %param.14) | copy-start | bytes 12582916
  108.9 132.6 %reduce-scatter.6.cloned.1.call-start = ((), (), s32[]{:S(2)}) async-start(), calls=%async_computation.8 | async-start | bytes 6291456 | tf_op jit(solution)/shard_map/reduce_scatter | solution.py:62
  116.3 1.0 copy-start.5
  123.2 1.2 copy-start.7
  123.3 179.0 %reduce-scatter.4.cloned.1.call-start = ((), (), s32[]{:S(2)}) async-start(), calls=%async_computation.7 | async-start | bytes 6291456 | tf_op jit(solution)/shard_map/reduce_scatter | solution.py:59
  130.6 4.9 %copy-start.4 = (bf16[1,2048,1024]{2,1,0:T(8,128)(2,1)S(1)}, bf16[1,2048,1024]{2,1,0:T(8,128)(2,1)}, u32[]{:S(2)}) copy-start(bf16[1,2048,1024]{2,1,0:T(8,128)(2,1)} %param.14) | copy-start | bytes 12582916
  130.6 4.9 %copy-start.6 = (bf16[64,8,1024]{2,1,0:T(8,128)(2,1)S(1)}, bf16[64,8,1024]{2,1,0:T(8,128)(2,1)}, u32[]{:S(2)}) copy-start(bf16[64,8,1024]{2,1,0:T(8,128)(2,1)} %copy-done.5) | copy-start | bytes 3145732
  139.2 5.0 %copy-start.2 = (s32[256,2]{0,1:T(2,128)S(1)}, s32[256,2]{0,1:T(2,128)}, u32[]{:S(2)}) copy-start(s32[256,2]{0,1:T(2,128)} %get-tuple-element.5) | copy-start | bytes 6148
  139.2 49.3 %all-to-all-start.3 = ((bf16[64,1,8,2048]{3,2,1,0:T(8,128)(2,1)}), bf16[64,1,8,2048]{3,2,1,0:T(8,128)(2,1)S(1)}, u32[]{:S(2)}, u32[]{:S(2)}) async-start(bf16[64,1,8,2048]{3,2,1,0:T(8,128)(2,1)} %fusion.15), calls=%async_computation.3 | async-start | bytes 4194304 | tf_op jit(solution)/shard_map/all_to_all | solution.py:53
Sparse Core Ops, SparseCore 0:
  109.0 71.2 reduce-scatter.7
  183.4 58.0 reduce-scatter.5
  244.5 57.7 reduce-scatter.3
where the time goes:
time: 310 us; the launch traced here: 309 us
  waiting for transfers between devices  193 us (62%)
  matrix products  46.6 us (15%)
  starting transfers between devices  28.8 us (9%)
  local copies, waits for them, and re-layouts  21.7 us (7%)
  between operations  14 us (5%)
  other arithmetic  4.26 us (1%)
    reduce_scatter x1, waiting for transfers between devices, per_device(): lax.psum_scatter(acc_gate.astype(jnp.bfloat16), 'dp', scatter_dimension=1...  60.8 us
    reduce_scatter x1, waiting for transfers between devices, per_device(): lax.psum_scatter(acc_up.astype(jnp.bfloat16), 'dp', scatter_dimension=1,...  45.4 us
    all_to_all x1, waiting for transfers between devices, per_device(): lax.all_to_all(back, ('seq', 'expert'), split_axis=0, concat_axis=0, tile...  44.2 us
    all_to_all x1, waiting for transfers between devices, per_device(): lax.all_to_all(send_x, ('seq', 'expert'), split_axis=0, concat_axis=0, ti...  25.1 us
    all_to_all x1, waiting for transfers between devices, per_device(): lax.all_to_all(send_g, ('seq', 'expert'), split_axis=0, concat_axis=0, ti...  16.2 us
    all_to_all x1, starting transfers between devices, per_device(): lax.all_to_all(send_c, ('seq', 'expert'), split_axis=0, concat_axis=0, ti...  10.9 us
    all_to_all x1, starting transfers between devices, per_device(): lax.all_to_all(send_x, ('seq', 'expert'), split_axis=0, concat_axis=0, ti...  7.37 us
    dot_general x1, matrix products, per_device(): jnp.einsum('gesd,edf->gesf', route_grad, w_down, preferred_element_type=j...  7.31 us
  transfers between devices with their start and end apart: 7, of which 6 were waited for; matrix products, arithmetic and copies ran while one was open for 18% of the time, Pallas kernels for 0%

commit v1 on v0

v1 whole, which is shorter than its diff:
```python
import jax
import jax.numpy as jnp
from jax import lax
from jax.sharding import PartitionSpec as P

E = 64


def forward_rows(x, g, c, w_gate, w_up, w_down):
    gate_pre = jnp.dot(x, w_gate, preferred_element_type=jnp.float32)
    up_pre = jnp.dot(x, w_up, preferred_element_type=jnp.float32)
    gate_sig = jax.nn.sigmoid(gate_pre)
    silu_g = gate_pre * gate_sig
    act = (silu_g * up_pre).astype(jnp.bfloat16)
    route_grad = (c.astype(jnp.float32)[:, None] * g.astype(jnp.float32)).astype(jnp.bfloat16)
    act_grad = jnp.dot(route_grad, w_down, preferred_element_type=jnp.float32)
    gate_grad = (act_grad * up_pre * gate_sig * (1.0 + gate_pre * (1.0 - gate_sig))).astype(
        jnp.bfloat16
    )
    up_grad = (act_grad * silu_g).astype(jnp.bfloat16)
    return act, route_grad, gate_grad, up_grad


def per_device(tokens, grad_out, route_weights, expert_ids, route_slots, w_gate, w_up, w_down):
    dp_count = lax.axis_size("dp")
    seq_count = lax.axis_size("seq")
    exp_count = lax.axis_size("expert")
    group = seq_count * exp_count
    exp_local = w_gate.shape[0]
    cell_count = tokens.shape[0]
    width = tokens.shape[1]
    slot_count = 2 * cell_count // E
    half = width // dp_count
    me = lax.axis_index("dp")
    position = expert_ids * slot_count + route_slots
    cells = jnp.arange(cell_count, dtype=jnp.int32)
    table = (
        jnp.zeros((E * slot_count,), jnp.int32)
        .at[position]
        .set(jnp.broadcast_to(cells[:, None], (cell_count, 2)))
    )
    weight_table = jnp.zeros((E * slot_count,), jnp.bfloat16).at[position].set(route_weights)
    send_x = jnp.broadcast_to(
        tokens[table].reshape(1, group, slot_count, width), (dp_count, group, slot_count, width)
    ).reshape(dp_count * group, slot_count, width)
    send_g = jnp.broadcast_to(
        grad_out[table].reshape(1, group, slot_count, width), (dp_count, group, slot_count, width)
    ).reshape(dp_count * group, slot_count, width)
    send_c = jnp.broadcast_to(
        weight_table.reshape(1, group, slot_count), (dp_count, group, slot_count)
    ).reshape(dp_count * group, slot_count)
    axes = ("dp", "seq", "expert")
    recv_x = lax.all_to_all(send_x, axes, split_axis=0, concat_axis=0, tiled=True)
    recv_g = lax.all_to_all(send_g, axes, split_axis=0, concat_axis=0, tiled=True)
    recv_c = lax.all_to_all(send_c, axes, split_axis=0, concat_axis=0, tiled=True)
    rows = group * slot_count
    recv_x = recv_x.reshape(dp_count, rows, width)
    recv_g = recv_g.reshape(dp_count, rows, width)
    recv_c = recv_c.reshape(dp_count, rows)
    wg, wu, wd = w_gate[0], w_up[0], w_down[0]

    own = [lax.dynamic_index_in_dim(a, me, 0, keepdims=False) for a in (recv_x, recv_g, recv_c)]
    act_o, rg_o, gg_o, ug_o = forward_rows(*own, wg, wu, wd)
    back = jnp.dot(gg_o, wg.T, preferred_element_type=jnp.float32)
    back = (back + jnp.dot(ug_o, wu.T, preferred_element_type=jnp.float32)).astype(jnp.bfloat16)
    returned = lax.all_to_all(
        back.reshape(group, slot_count, width), ("seq", "expert"), split_axis=0, concat_axis=0,
        tiled=True,
    )
    other = [lax.dynamic_index_in_dim(a, 1 - me, 0, keepdims=False) for a in (recv_x, recv_g, recv_c)]
    act_p, rg_p, gg_p, ug_p = forward_rows(*other, wg, wu, wd)

    def wgrad(left_o, left_p, right_o, right_p):
        total = jnp.zeros((half, right_o.shape[1]), jnp.float32)
        for left, right in ((left_o, right_o), (left_p, right_p)):
            left_half = lax.dynamic_slice_in_dim(left, me * half, half, axis=1)
            part = jnp.dot(left_half.T, right, preferred_element_type=jnp.float32)
            total = total + part.astype(jnp.bfloat16).astype(jnp.float32)
        return total.astype(jnp.bfloat16)[None]

    grad_gate = wgrad(own[0], other[0], gg_o, gg_p)
    grad_up = wgrad(own[0], other[0], ug_o, ug_p)
    grad_down = wgrad(rg_o, rg_p, act_o, act_p)

    returned = returned.reshape(E * slot_count, width)
    grad_tokens = (
        returned[position[:, 0]].astype(jnp.float32) + returned[position[:, 1]].astype(jnp.float32)
    ).astype(jnp.bfloat16)
    return grad_tokens, grad_gate, grad_up, grad_down


def solution(mesh):
    return jax.shard_map(
        per_device,
        mesh=mesh,
        in_specs=(
            P(("dp", "seq", "expert"), None),
            P(("dp", "seq", "expert"), None),
            P(("dp", "seq", "expert"), None),
            P(("dp", "seq", "expert"), None),
            P(("dp", "seq", "expert"), None),
            P(("seq", "expert"), None, None),
            P(("seq", "expert"), None, None),
            P(("seq", "expert"), None, None),
        ),
        out_specs=(
            P(("dp", "seq", "expert"), None),
            P(("seq", "expert"), "dp", None),
            P(("seq", "expert"), "dp", None),
            P(("seq", "expert"), "dp", None),
        ),
        check_vma=False,
    )
```

time: 310 us -> 234 us (0.75)
  waiting for transfers between devices: 193 us -> 99.6 us
  matrix products: 46.6 us -> 67 us
  between operations: 14 us -> 1.19 us
  other arithmetic: 4.26 us -> 9.04 us
    reduce_scatter x3 -> x0, waiting for transfers between devices: 106 us -> none  [the longest x1 60.8 us: per_device(): lax.psum_scatter(acc_gate.astype(jnp.bfloat16), 'dp', scatter_dimension=1...]
    dot_general x8 -> x14, matrix products: 46.6 us -> 67 us  [the longest x6 20.6 us: wgrad(): part = jnp.dot(left_half.T, right, preferred_element_type=jnp.float32)]
    all_to_all x4, waiting for transfers between devices: 87.3 us -> 99.6 us  [the longest x1 48.7 us: per_device(): lax.all_to_all(send_x, axes, split_axis=0, concat_axis=0, tiled=True)]
    broadcast_in_dim x0 -> x5, local copies, waits for them, and re-layouts: none -> 5.2 us  [the longest x1 2.52 us: per_device(): jnp.broadcast_to(tokens[table].reshape(1, group, slot_count, width), (dp_...]
    convert_element_type x0 -> x2, other arithmetic: none -> 5.13 us  [the longest x1 5.12 us: forward_rows(): g.astype(jnp.float32)]
  transfers between devices with their start and end apart: 7 -> 4, of which waited for: 6 -> 4; matrix products, arithmetic and copies ran while one was open for 18% -> 17% of each run, Pallas kernels for 0% -> 0%
where the time goes in v1:
time: 234 us; the launch traced here: 232 us
  waiting for transfers between devices  99.6 us (43%)
  matrix products  67 us (29%)
  starting transfers between devices  31.2 us (13%)
  local copies, waits for them, and re-layouts  23.5 us (10%)
  other arithmetic  9.04 us (4%)
    all_to_all x1, waiting for transfers between devices, per_device(): lax.all_to_all(send_x, axes, split_axis=0, concat_axis=0, tiled=True)  48.7 us
    all_to_all x1, waiting for transfers between devices, per_device(): lax.all_to_all(send_g, axes, split_axis=0, concat_axis=0, tiled=True)  40 us
    dot_general x6, matrix products, wgrad(): part = jnp.dot(left_half.T, right, preferred_element_type=jnp.float32)  20.6 us
    dot_general x1, matrix products, per_device(): back = jnp.dot(gg_o, wg.T, preferred_element_type=jnp.float32)  13.5 us
    all_to_all x1, starting transfers between devices, per_device(): lax.all_to_all(send_c, axes, split_axis=0, concat_axis=0, tiled=True)  11.5 us
    dot_general x2, matrix products, forward_rows(): gate_pre = jnp.dot(x, w_gate, preferred_element_type=jnp.float32)  10.6 us
    dot_general x2, matrix products, forward_rows(): act_grad = jnp.dot(route_grad, w_down, preferred_element_type=jnp.float32)  10.5 us
    dot_general x2, matrix products, forward_rows(): up_pre = jnp.dot(x, w_up, preferred_element_type=jnp.float32)  8.06 us
  transfers between devices with their start and end apart: 4, of which 4 were waited for; matrix products, arithmetic and copies ran while one was open for 17% of the time, Pallas kernels for 0%

profile of v1, /device:TPU:1, one launch (start us, length us, event | category | flops | bytes accessed | tf_op | source)
XLA Modules:
  0.0 231.6 jit_solution(1165477110473982165)
XLA Ops:
  0.6 0.0 copy-start
  0.6 0.8 compare_select_fusion
  1.4 0.1 copy.16
  1.6 0.1 reshape.121
  1.7 0.8 copy.17
  2.6 0.1 reshape.123
  2.7 3.8 %scatter_custom_fusion = bf16[512]{0:T(512)(128)(2,1)S(1)} fusion(s32[512]{0:T(512)S(1)} %reshape.121, bf16[512]{0:T(512)(128)(2,1)S(1)} %reshape.123, bf16[]{:T(256)} %constant.66.clone.1), kind=kCustom, calls=%fused_computation.104 | custom fusion | bytes 1026 | tf_op jit(solution)/shard_map/scatter | solution.py:42
  6.5 0.1 broadcast_in_dim.53
  6.6 0.1 copy.18
  6.7 0.1 all_to_all.15
  6.7 0.8 copy.19
  7.5 11.5 %all-to-all-start = ((bf16[128,1,8]{2,1,0:T(2,128)(2,1)}), bf16[128,1,8]{2,1,0:T(2,128)(2,1)S(1)}, u32[]{:S(2)}, u32[]{:S(2)}) async-start(bf16[128,1,8]{2,1,0:T(2,128)(2,1)} %copy.19), calls=%async_computation | async-start | bytes 131072 | tf_op jit(solution)/shard_map/all_to_all | solution.py:55
  19.0 0.1 reshape.131
  19.2 2.4 %scatter_custom_fusion.1 = s32[512]{0:T(512)S(1)} fusion(s32[512]{0:T(512)S(1)} %reshape.121, s32[512]{0:T(512)S(1)} %reshape.131, s32[]{:T(128)} %constant.68.clone.1), kind=kCustom, calls=%fused_computation.102 | custom fusion | bytes 2052 | tf_op jit(solution)/shard_map/scatter | solution.py:40
  21.7 2.5 %gather_fusion.1 = bf16[512,2048]{1,0:T(8,128)(2,1)S(1)} fusion(bf16[256,2048]{1,0:T(8,128)(2,1)S(1)} %copy-done, s32[1024]{0:T(1024)S(1)} %pad_clamp_fusion.2), kind=kCustom, calls=%fused_computation.1 | custom fusion | bytes 4196352 | tf_op jit(solution)/shard_map/gather | solution.py:44
  24.1 4.4 %all-to-all-done = bf16[128,1,8]{2,1,0:T(2,128)(2,1)S(1)} async-done(((bf16[128,1,8]{2,1,0:T(2,128)(2,1)}), bf16[128,1,8]{2,1,0:T(2,128)(2,1)S(1)}, u32[]{:S(2)}, u32[]{:S(2)}) %all-to-all-start) | async-done | bytes 2080 | tf_op jit(solution)/shard_map/all_to_all | solution.py:55
  28.6 2.5 %broadcast_in_dim.60 = bf16[2,64,8,2048]{3,2,1,0:T(8,128)(2,1)} broadcast(bf16[64,8,2048]{2,1,0:T(8,128)(2,1)S(1)} %bitcast.87), dimensions={1,2,3} | broadcast | bytes 6291456 | tf_op jit(solution)/shard_map/broadcast_in_dim | solution.py:43
  31.1 5.8 %all-to-all-start.2 = ((bf16[128,8,2048]{2,1,0:T(8,128)(2,1)}), bf16[128,8,2048]{2,1,0:T(8,128)(2,1)}, u32[]{:S(2)}, u32[]{:S(2)}) async-start(bf16[128,8,2048]{2,1,0:T(8,128)(2,1)} %bitcast.85), calls=%async_computation.2 | async-start | bytes 8388608 | tf_op jit(solution)/shard_map/all_to_all | solution.py:53
  36.9 2.5 %gather_fusion = bf16[512,2048]{1,0:T(8,128)(2,1)S(1)} fusion(bf16[256,2048]{1,0:T(8,128)(2,1)S(1)} %copy-done.2, s32[1024]{0:T(1024)S(1)} %pad_clamp_fusion.2), kind=kCustom, calls=%fused_computation | custom fusion | bytes 4196352 | tf_op jit(solution)/shard_map/gather | solution.py:47
  39.4 48.7 %all-to-all-done.2 = bf16[128,8,2048]{2,1,0:T(8,128)(2,1)} async-done(((bf16[128,8,2048]{2,1,0:T(8,128)(2,1)}), bf16[128,8,2048]{2,1,0:T(8,128)(2,1)}, u32[]{:S(2)}, u32[]{:S(2)}) %all-to-all-start.2) | async-done | bytes 4194336 | tf_op jit(solution)/shard_map/all_to_all | solution.py:53
  88.1 2.5 %broadcast_in_dim.58 = bf16[2,64,8,2048]{3,2,1,0:T(8,128)(2,1)} broadcast(bf16[64,8,2048]{2,1,0:T(8,128)(2,1)S(1)} %bitcast.86), dimensions={1,2,3} | broadcast | bytes 6291456 | tf_op jit(solution)/shard_map/broadcast_in_dim | solution.py:46
  90.6 7.5 %all-to-all-start.1 = ((bf16[128,8,2048]{2,1,0:T(8,128)(2,1)}), bf16[128,8,2048]{2,1,0:T(8,128)(2,1)}, u32[]{:S(2)}, u32[]{:S(2)}) async-start(bf16[128,8,2048]{2,1,0:T(8,128)(2,1)} %bitcast.84), calls=%async_computation.1 | async-start | bytes 8388608 | tf_op jit(solution)/shard_map/all_to_all | solution.py:54
  98.2 0.2 reduce
  98.4 0.1 reshape.76
  98.5 0.0 copy-start.5
  98.5 5.3 %fusion.6 = f32[512,1024]{1,0:T(8,128)S(1)} fusion(bf16[1,2048,1024]{2,1,0:T(8,128)(2,1)} %param.13, bf16[2,512,2048]{2,1,0:T(8,128)(2,1)} %bitcast.8, s32[]{:T(128)S(6)} %select_n.43), kind=kOutput, calls=%fused_computation.16 | convolution fusion | flops 2147483648 | bytes 8388612 | tf_op jit(solution)/shard_map/dot_general | solution.py:10
  103.9 5.3 %fusion.2 = f32[512,1024]{1,0:T(8,128)} fusion(bf16[1,2048,1024]{2,1,0:T(8,128)(2,1)S(1)} %copy-done.5, bf16[2,512,2048]{2,1,0:T(8,128)(2,1)} %bitcast.8, s32[]{:T(128)S(6)} %select_n.50), kind=kOutput, calls=%fused_computation.12 | convolution fusion | flops 2147483648 | bytes 8388612 | tf_op jit(solution)/shard_map/dot_general | solution.py:10
  109.1 40.0 %all-to-all-done.1 = bf16[128,8,2048]{2,1,0:T(8,128)(2,1)} async-done(((bf16[128,8,2048]{2,1,0:T(8,128)(2,1)}), bf16[128,8,2048]{2,1,0:T(8,128)(2,1)}, u32[]{:S(2)}, u32[]{:S(2)}) %all-to-all-start.1) | async-done | bytes 4194336 | tf_op jit(solution)/shard_map/all_to_all | solution.py:54
  149.1 5.1 %convert_bitcast_fusion = (f32[512,2048]{1,0:T(8,128)}, f32[512,2048]{1,0:T(8,128)S(1)}) fusion(bf16[2,512,2048]{2,1,0:T(8,128)(2,1)} %bitcast.3, s32[]{:T(128)S(6)} %select_n.50, s32[]{:T(128)S(6)} %select_n.43), kind=kLoop, calls=%fused_computation.6 | loop fusion | flops 2097152 | bytes 12582920 | tf_op jit(solution)/shard_map/convert_element_type | solution.py:15
  154.2 4.0 %fusion.12 = f32[512,1024]{1,0:T(8,128)S(1)} fusion(bf16[1,2048,1024]{2,1,0:T(8,128)(2,1)S(1)} %copy-done.7, bf16[2,512,2048]{2,1,0:T(8,128)(2,1)} %bitcast.8, s32[]{:T(128)S(6)} %select_n.43), kind=kOutput, calls=%fused_computation.22 | convolution fusion | flops 2147483648 | bytes 8388612 | tf_op jit(solution)/shard_map/dot_general | solution.py:11
  158.2 0.0 copy-start.4
  158.2 2.8 %fusion.46 = bf16[1024,1024]{1,0:T(8,128)(2,1)} fusion(f32[512,1024]{1,0:T(8,128)S(1)} %fusion.12, f32[512,2048]{1,0:T(8,128)S(1)} %get-tuple-element.7, s32[]{:T(128)S(6)} %select_n.48, f32[512]{0:T(512)S(1)} %bitcast.92, f32[512,1024]{1,0:T(8,128)S(1)} %fusion.6), kind=kOutput, calls=%fused_computation.65 | convolution fusion | flops 1077936128 | bytes 8390660 | tf_op jit(solution)/shard_map/dot_general | solution.py:77
  161.0 4.5 %multiply_convert_fusion.4 = (bf16[512,1024]{1,0:T(8,128)(2,1)S(1)}, bf16[512,1024]{1,0:T(8,128)(2,1)S(1)}) fusion(f32[512,1024]{1,0:T(8,128)S(1)} %fusion.6, f32[512,1024]{1,0:T(8,128)S(1)} %fusion.12, bf16[1,2048,1024]{2,1,0:T(8,128)(2,1)S(1)} %copy-done.4, f32[512]{0:T(512)S(1)} %bitcast.93, bf16[2,512,2048]{2,1,0:T(8,128)(2,1)} %bitcast.3, s32[]{:T(128)S(6)} %select_n.43), kind=kOutput, calls=%fused_computation.54 | convolution fusion | flops 2157445120 | bytes 12584964 | tf_op jit(solution)/shard_map/dot_general | solution.py:16
  165.6 0.0 copy-start.6
  165.6 6.1 %fusion.14 = f32[512,1024]{1,0:T(8,128)} fusion(bf16[1,2048,1024]{2,1,0:T(8,128)(2,1)S(1)} %copy-done.4, f32[512]{0:T(512)S(1)} %bitcast.90, bf16[2,512,2048]{2,1,0:T(8,128)(2,1)} %bitcast.3, s32[]{:T(128)S(6)} %select_n.50), kind=kOutput, calls=%fused_computation.24 | convolution fusion | flops 2150629376 | bytes 8390660 | tf_op jit(solution)/shard_map/dot_general | solution.py:16
  171.6 13.5 %fusion.4 = f32[512,2048]{1,0:T(8,128)S(1)} fusion(bf16[512,1024]{1,0:T(8,128)(2,1)S(1)} %get-tuple-element.9, bf16[1,2048,1024]{2,1,0:T(8,128)(2,1)S(1)} %copy-done.6), kind=kOutput, calls=%fused_computation.14 | convolution fusion | flops 2147483648 | bytes 9437184 | tf_op jit(solution)/shard_map/dot_general | solution.py:64
  185.1 3.8 %fusion.20 = bf16[64,8,2048]{2,1,0:T(8,128)(2,1)} fusion(f32[512,2048]{1,0:T(8,128)S(1)} %fusion.4, bf16[512,1024]{1,0:T(8,128)(2,1)S(1)} %get-tuple-element.8, bf16[1,2048,1024]{2,1,0:T(8,128)(2,1)S(1)} %copy-done.7), kind=kOutput, calls=%fused_computation.32 | convolution fusion | flops 2149580800 | bytes 11534336 | tf_op jit(solution)/shard_map/dot_general | solution.py:65
  188.9 6.4 %all-to-all-start.3 = ((bf16[64,8,2048]{2,1,0:T(8,128)(2,1)}), bf16[64,8,2048]{2,1,0:T(8,128)(2,1)S(1)}, u32[]{:S(2)}, u32[]{:S(2)}) async-start(bf16[64,8,2048]{2,1,0:T(8,128)(2,1)} %fusion.20), calls=%async_computation.3 | async-start | bytes 4194304 | tf_op jit(solution)/shard_map/all_to_all | solution.py:66
  195.3 3.3 %fusion.53 = bf16[1024,1024]{1,0:T(8,128)(2,1)S(1)} fusion(bf16[512,1024]{1,0:T(8,128)(2,1)} %copy-done.11, bf16[2,512,2048]{2,1,0:T(8,128)(2,1)} %bitcast.8, s32[]{:T(128)S(6)} %select_n.47, s32[]{:T(128)S(6)} %select_n.49), kind=kOutput, calls=%fused_computation.70 | convolution fusion | flops 1073741824 | bytes 4194312 | tf_op jit(solution)/shard_map/dot_general | solution.py:77
  198.7 4.3 %fusion.24 = bf16[1,1024,1024]{2,1,0:T(8,128)(2,1)} fusion(bf16[1024,1024]{1,0:T(8,128)(2,1)S(1)} %fusion.53, f32[512,1024]{1,0:T(8,128)S(1)} %copy-done.14, bf16[2,512,2048]{2,1,0:T(8,128)(2,1)} %bitcast.8, s32[]{:T(128)S(6)} %select_n.51, s32[]{:T(128)S(6)} %select_n.49, f32[512,1024]{1,0:T(8,128)S(1)} %copy-done.13), kind=kOutput, calls=%fused_computation.34 | convolution fusion | flops 1082130432 | bytes 9437192 | tf_op jit(solution)/shard_map/dot_general | solution.py:77
  203.0 3.0 %fusion.55 = bf16[1024,1024]{1,0:T(8,128)(2,1)S(1)} fusion(bf16[512,1024]{1,0:T(8,128)(2,1)S(1)} %copy-done.10, bf16[2,512,2048]{2,1,0:T(8,128)(2,1)} %bitcast.8, s32[]{:T(128)S(6)} %select_n.47, s32[]{:T(128)S(6)} %select_n.49), kind=kOutput, calls=%fused_computation.72 | convolution fusion | flops 1073741824 | bytes 4194312 | tf_op jit(solution)/shard_map/dot_general | solution.py:77
  206.0 4.1 %fusion.8 = f32[512,1024]{1,0:T(8,128)S(1)} fusion(bf16[1,2048,1024]{2,1,0:T(8,128)(2,1)S(1)} %copy-done.8, bf16[2,512,2048]{2,1,0:T(8,128)(2,1)} %bitcast.8, s32[]{:T(128)S(6)} %select_n.50), kind=kOutput, calls=%fused_computation.18 | convolution fusion | flops 2147483648 | bytes 8388612 | tf_op jit(solution)/shard_map/dot_general | solution.py:11
  210.2 2.8 %fusion.25 = bf16[1,1024,1024]{2,1,0:T(8,128)(2,1)} fusion(bf16[1024,1024]{1,0:T(8,128)(2,1)S(1)} %copy-done.12, f32[512,1024]{1,0:T(8,128)S(1)} %fusion.8, f32[512,2048]{1,0:T(8,128)S(1)} %copy-done.3, s32[]{:T(128)S(6)} %select_n.48, f32[512]{0:T(512)S(1)} %bitcast.91, f32[512,1024]{1,0:T(8,128)S(1)} %copy-done.13), kind=kOutput, calls=%fused_computation.35 | convolution fusion | flops 1083179008 | bytes 10487812 | tf_op jit(solution)/shard_map/dot_general | solution.py:77
  213.0 4.3 %fusion.23 = bf16[1,1024,1024]{2,1,0:T(8,128)(2,1)} fusion(bf16[1024,1024]{1,0:T(8,128)(2,1)S(1)} %fusion.55, f32[512,1024]{1,0:T(8,128)S(1)} %copy-done.13, f32[512,1024]{1,0:T(8,128)S(1)} %copy-done.14, f32[512,1024]{1,0:T(8,128)S(1)} %fusion.8, bf16[2,512,2048]{2,1,0:T(8,128)(2,1)} %bitcast.8, s32[]{:T(128)S(6)} %select_n.51, s32[]{:T(128)S(6)} %select_n.49), kind=kOutput, calls=%fused_computation.33 | convolution fusion | flops 1084227584 | bytes 11534344 | tf_op jit(solution)/shard_map/dot_general | solution.py:77
  217.3 6.5 %all-to-all-done.3 = bf16[64,8,2048]{2,1,0:T(8,128)(2,1)S(1)} async-done(((bf16[64,8,2048]{2,1,0:T(8,128)(2,1)}), bf16[64,8,2048]{2,1,0:T(8,128)(2,1)S(1)}, u32[]{:S(2)}, u32[]{:S(2)}) %all-to-all-start.3) | async-done | bytes 2097184 | tf_op jit(solution)/shard_map/all_to_all | solution.py:66
  223.8 2.3 %gather_fusion.2 = bf16[256,2048]{1,0:T(8,128)(2,1)} fusion(bf16[512,2048]{1,0:T(8,128)(2,1)S(1)} %bitcast.82, s32[1024]{0:T(1024)S(1)} %pad_clamp_fusion.1), kind=kCustom, calls=%fused_computation.2 | custom fusion | bytes 2098176 | tf_op jit(solution)/shard_map/gather | solution.py:87
  226.1 2.3 %gather_fusion.3 = bf16[256,2048]{1,0:T(8,128)(2,1)} fusion(bf16[512,2048]{1,0:T(8,128)(2,1)S(1)} %bitcast.83, s32[1024]{0:T(1024)S(1)} %pad_clamp_fusion), kind=kCustom, calls=%fused_computation.3 | custom fusion | bytes 2098176 | tf_op jit(solution)/shard_map/gather | solution.py:87
  228.5 2.9 %add_convert_fusion.4 = bf16[256,2048]{1,0:T(8,128)(2,1)} fusion(bf16[256,2048]{1,0:T(8,128)(2,1)} %gather_fusion.3, bf16[256,2048]{1,0:T(8,128)(2,1)} %gather_fusion.2), kind=kLoop, calls=%fused_computation.53 | loop fusion | flops 2097152 | bytes 3145728 | tf_op jit(solution)/shard_map/convert_element_type | solution.py:88
  (34 shorter events, 0.1 us)
Async XLA Ops:
  0.6 21.0 %copy-start = (bf16[256,2048]{1,0:T(8,128)(2,1)S(1)}, bf16[256,2048]{1,0:T(8,128)(2,1)}, u32[]{:S(2)}) copy-start(bf16[256,2048]{1,0:T(8,128)(2,1)} %param.8) | copy-start | bytes 3145732
  7.5 21.0 %all-to-all-start = ((bf16[128,1,8]{2,1,0:T(2,128)(2,1)}), bf16[128,1,8]{2,1,0:T(2,128)(2,1)S(1)}, u32[]{:S(2)}, u32[]{:S(2)}) async-start(bf16[128,1,8]{2,1,0:T(2,128)(2,1)} %copy.19), calls=%async_computation | async-start | bytes 131072 | tf_op jit(solution)/shard_map/all_to_all | solution.py:55
  31.1 5.8 %copy-start.2 = (bf16[256,2048]{1,0:T(8,128)(2,1)S(1)}, bf16[256,2048]{1,0:T(8,128)(2,1)}, u32[]{:S(2)}) copy-start(bf16[256,2048]{1,0:T(8,128)(2,1)} %param.9) | copy-start | bytes 3145732
  31.1 57.0 %all-to-all-start.2 = ((bf16[128,8,2048]{2,1,0:T(8,128)(2,1)}), bf16[128,8,2048]{2,1,0:T(8,128)(2,1)}, u32[]{:S(2)}, u32[]{:S(2)}) async-start(bf16[128,8,2048]{2,1,0:T(8,128)(2,1)} %bitcast.85), calls=%async_computation.2 | async-start | bytes 8388608 | tf_op jit(solution)/shard_map/all_to_all | solution.py:53
  90.6 58.5 %all-to-all-start.1 = ((bf16[128,8,2048]{2,1,0:T(8,128)(2,1)}), bf16[128,8,2048]{2,1,0:T(8,128)(2,1)}, u32[]{:S(2)}, u32[]{:S(2)}) async-start(bf16[128,8,2048]{2,1,0:T(8,128)(2,1)} %bitcast.84), calls=%async_computation.1 | async-start | bytes 8388608 | tf_op jit(solution)/shard_map/all_to_all | solution.py:54
  98.5 5.3 %copy-start.5 = (bf16[1,2048,1024]{2,1,0:T(8,128)(2,1)S(1)}, bf16[1,2048,1024]{2,1,0:T(8,128)(2,1)}, u32[]{:S(2)}) copy-start(bf16[1,2048,1024]{2,1,0:T(8,128)(2,1)} %param.13) | copy-start | bytes 12582916
  149.1 5.1 %copy-start.7 = (bf16[1,2048,1024]{2,1,0:T(8,128)(2,1)S(1)}, bf16[1,2048,1024]{2,1,0:T(8,128)(2,1)}, u32[]{:S(2)}) copy-start(bf16[1,2048,1024]{2,1,0:T(8,128)(2,1)} %param.14) | copy-start | bytes 12582916
  158.2 2.8 %copy-start.4 = (bf16[1,2048,1024]{2,1,0:T(8,128)(2,1)S(1)}, bf16[1,2048,1024]{2,1,0:T(8,128)(2,1)}, u32[]{:S(2)}) copy-start(bf16[1,2048,1024]{2,1,0:T(8,128)(2,1)} %param.15) | copy-start | bytes 12582916
  165.5 6.1 %copy-start.9 = (bf16[512,1024]{1,0:T(8,128)(2,1)}, bf16[512,1024]{1,0:T(8,128)(2,1)S(1)}, u32[]{:S(2)}) copy-start(bf16[512,1024]{1,0:T(8,128)(2,1)S(1)} %get-tuple-element.9) | copy-start | bytes 3145732
  165.5 19.6 %copy-start.11 = (bf16[512,1024]{1,0:T(8,128)(2,1)}, bf16[512,1024]{1,0:T(8,128)(2,1)S(1)}, u32[]{:S(2)}) copy-start(bf16[512,1024]{1,0:T(8,128)(2,1)S(1)} %get-tuple-element.8) | copy-start | bytes 3145732
  165.6 6.1 %copy-start.6 = (bf16[1,2048,1024]{2,1,0:T(8,128)(2,1)S(1)}, bf16[1,2048,1024]{2,1,0:T(8,128)(2,1)}, u32[]{:S(2)}) copy-start(bf16[1,2048,1024]{2,1,0:T(8,128)(2,1)} %param.13) | copy-start | bytes 12582916
  188.9 34.9 %all-to-all-start.3 = ((bf16[64,8,2048]{2,1,0:T(8,128)(2,1)}), bf16[64,8,2048]{2,1,0:T(8,128)(2,1)S(1)}, u32[]{:S(2)}, u32[]{:S(2)}) async-start(bf16[64,8,2048]{2,1,0:T(8,128)(2,1)} %fusion.20), calls=%async_computation.3 | async-start | bytes 4194304 | tf_op jit(solution)/shard_map/all_to_all | solution.py:66
  195.3 3.3 %copy-start.13 = (f32[512,1024]{1,0:T(8,128)S(1)}, f32[512,1024]{1,0:T(8,128)}, u32[]{:S(2)}) copy-start(f32[512,1024]{1,0:T(8,128)} %fusion.2) | copy-start | bytes 6291460
  195.3 3.3 %copy-start.14 = (f32[512,1024]{1,0:T(8,128)S(1)}, f32[512,1024]{1,0:T(8,128)}, u32[]{:S(2)}) copy-start(f32[512,1024]{1,0:T(8,128)} %fusion.14) | copy-start | bytes 6291460
  198.7 4.3 %copy-start.10 = (bf16[512,1024]{1,0:T(8,128)(2,1)S(1)}, bf16[512,1024]{1,0:T(8,128)(2,1)}, u32[]{:S(2)}) copy-start(bf16[512,1024]{1,0:T(8,128)(2,1)} %copy-done.9) | copy-start | bytes 3145732
  203.0 3.0 %copy-start.8 = (bf16[1,2048,1024]{2,1,0:T(8,128)(2,1)S(1)}, bf16[1,2048,1024]{2,1,0:T(8,128)(2,1)}, u32[]{:S(2)}) copy-start(bf16[1,2048,1024]{2,1,0:T(8,128)(2,1)} %param.14) | copy-start | bytes 12582916
  206.0 4.1 %copy-start.3 = (f32[512,2048]{1,0:T(8,128)S(1)}, f32[512,2048]{1,0:T(8,128)}, u32[]{:S(2)}) copy-start(f32[512,2048]{1,0:T(8,128)} %get-tuple-element.6) | copy-start | bytes 12582916
  206.0 4.1 %copy-start.12 = (bf16[1024,1024]{1,0:T(8,128)(2,1)S(1)}, bf16[1024,1024]{1,0:T(8,128)(2,1)}, u32[]{:S(2)}) copy-start(bf16[1024,1024]{1,0:T(8,128)(2,1)} %fusion.46) | copy-start | bytes 6291460
  226.1 5.2 %copy-start.1 = (bf16[256,2048]{1,0:T(8,128)(2,1)S(1)}, bf16[256,2048]{1,0:T(8,128)(2,1)}, u32[]{:S(2)}) copy-start(bf16[256,2048]{1,0:T(8,128)(2,1)} %param.8) | copy-start | bytes 3145732

commit v2 on v0

v2 whole, which is shorter than its diff:
```python
import jax
import jax.numpy as jnp
from jax import lax
from jax.sharding import PartitionSpec as P

E = 64


def per_device(tokens, grad_out, route_weights, expert_ids, route_slots, w_gate, w_up, w_down):
    dp_count = lax.axis_size("dp")
    seq_count = lax.axis_size("seq")
    exp_count = lax.axis_size("expert")
    group = seq_count * exp_count
    cell_count = tokens.shape[0]
    width = tokens.shape[1]
    slot_count = 2 * cell_count // E
    rows = E * slot_count
    half = width // dp_count
    me = lax.axis_index("dp")
    position = expert_ids * slot_count + route_slots

    slots = lax.broadcasted_iota(jnp.int32, (dp_count * rows, cell_count), 0) % rows
    hit0 = slots == position[None, :, 0]
    hit1 = slots == position[None, :, 1]
    pick = (hit0 | hit1).astype(jnp.bfloat16)
    weigh = jnp.where(hit0, route_weights[None, :, 0], jnp.where(hit1, route_weights[None, :, 1], 0))
    send_x = jnp.dot(pick, tokens, preferred_element_type=jnp.float32).astype(jnp.bfloat16)
    send_rg = jnp.dot(weigh.astype(jnp.bfloat16), grad_out, preferred_element_type=jnp.float32).astype(
        jnp.bfloat16
    )
    axes = ("dp", "seq", "expert")
    recv_x = lax.all_to_all(
        send_x.reshape(dp_count * group, slot_count, width), axes, 0, 0, tiled=True
    ).reshape(dp_count, group * slot_count, width)
    recv_rg = lax.all_to_all(
        send_rg.reshape(dp_count * group, slot_count, width), axes, 0, 0, tiled=True
    ).reshape(dp_count, group * slot_count, width)

    wg, wu, wd = w_gate[0], w_up[0], w_down[0]
    gate_pre = jnp.einsum("srd,df->srf", recv_x, wg, preferred_element_type=jnp.float32)
    up_pre = jnp.einsum("srd,df->srf", recv_x, wu, preferred_element_type=jnp.float32)
    gate_sig = jax.nn.sigmoid(gate_pre)
    silu_g = gate_pre * gate_sig
    act = (silu_g * up_pre).astype(jnp.bfloat16)
    act_grad = jnp.einsum("srd,df->srf", recv_rg, wd, preferred_element_type=jnp.float32)
    gate_grad = (act_grad * up_pre * gate_sig * (1.0 + gate_pre * (1.0 - gate_sig))).astype(
        jnp.bfloat16
    )
    up_grad = (act_grad * silu_g).astype(jnp.bfloat16)

    gg_own = lax.dynamic_index_in_dim(gate_grad, me, 0, keepdims=False)
    ug_own = lax.dynamic_index_in_dim(up_grad, me, 0, keepdims=False)
    back = jnp.dot(gg_own, wg.T, preferred_element_type=jnp.float32)
    back = (back + jnp.dot(ug_own, wu.T, preferred_element_type=jnp.float32)).astype(jnp.bfloat16)
    returned = lax.all_to_all(
        back.reshape(group, slot_count, width), ("seq", "expert"), 0, 0, tiled=True
    ).reshape(rows, width)

    x_half = lax.dynamic_slice_in_dim(recv_x, me * half, half, axis=2)
    rg_half = lax.dynamic_slice_in_dim(recv_rg, me * half, half, axis=2)

    def wgrad(left, right):
        per_seq = jnp.einsum("srd,srf->sdf", left, right, preferred_element_type=jnp.float32)
        per_seq = per_seq.astype(jnp.bfloat16).astype(jnp.float32)
        return per_seq.sum(axis=0).astype(jnp.bfloat16)[None]

    grad_gate = wgrad(x_half, gate_grad)
    grad_up = wgrad(x_half, up_grad)
    grad_down = wgrad(rg_half, act)

    grad_tokens = jnp.dot(
        pick[:rows].T, returned, preferred_element_type=jnp.float32
    ).astype(jnp.bfloat16)
    return grad_tokens, grad_gate, grad_up, grad_down


def solution(mesh):
    return jax.shard_map(
        per_device,
        mesh=mesh,
        in_specs=(
            P(("dp", "seq", "expert"), None),
            P(("dp", "seq", "expert"), None),
            P(("dp", "seq", "expert"), None),
            P(("dp", "seq", "expert"), None),
            P(("dp", "seq", "expert"), None),
            P(("seq", "expert"), None, None),
            P(("seq", "expert"), None, None),
            P(("seq", "expert"), None, None),
        ),
        out_specs=(
            P(("dp", "seq", "expert"), None),
            P(("seq", "expert"), "dp", None),
            P(("seq", "expert"), "dp", None),
            P(("seq", "expert"), "dp", None),
        ),
        check_vma=False,
    )
```

time: 310 us -> 183 us (0.59)
  waiting for transfers between devices: 193 us -> 89.8 us
  local copies, waits for them, and re-layouts: 21.7 us -> 1.79 us
  matrix products: 46.6 us -> 62.8 us
  between operations: 14 us -> 0.8 us
  starting transfers between devices: 28.8 us -> 25.6 us
    reduce_scatter x3 -> x0, waiting for transfers between devices: 106 us -> none  [the longest x1 60.8 us: per_device(): lax.psum_scatter(acc_gate.astype(jnp.bfloat16), 'dp', scatter_dimension=1...]
    dot_general x8 -> x11, matrix products: 46.6 us -> 62.8 us  [the longest x3 18.6 us: wgrad(): jnp.einsum('srd,srf->sdf', left, right, preferred_element_type=jnp.float32)]
    gather x4 -> x0, local copies, waits for them, and re-layouts: 11.3 us -> none  [the longest x1 3.31 us: per_device(): send_g = grad_out[table].reshape(group, exp_local, slot_count, width)]
    scatter x2 -> x0, local copies, waits for them, and re-layouts: 6.21 us -> none  [the longest x1 3.77 us: per_device(): jnp.zeros((E * slot_count,), jnp.bfloat16).at[position].set(route_weights)]
    all_to_all x4 -> x3, starting transfers between devices: 28.3 us -> 25.6 us  [the longest x1 12 us: per_device(): lax.all_to_all(send_x.reshape(dp_count * group, slot_count, width), axes,...]
    all_to_all x4 -> x3, waiting for transfers between devices: 87.3 us -> 89.8 us  [the longest x1 47.9 us: per_device(): lax.all_to_all(send_x.reshape(dp_count * group, slot_count, width), axes,...]
  transfers between devices with their start and end apart: 7 -> 3, of which waited for: 6 -> 3; matrix products, arithmetic and copies ran while one was open for 18% -> 22% of each run, Pallas kernels for 0% -> 0%
where the time goes in v2:
time: 183 us
  waiting for transfers between devices  89.8 us (49%)
  matrix products  62.8 us (34%)
  starting transfers between devices  25.6 us (14%)
    all_to_all x1, waiting for transfers between devices, per_device(): lax.all_to_all(send_x.reshape(dp_count * group, slot_count, width), axes,...  47.9 us
    all_to_all x1, waiting for transfers between devices, per_device(): lax.all_to_all(send_rg.reshape(dp_count * group, slot_count, width), axes...  32.9 us
    dot_general x3, matrix products, wgrad(): jnp.einsum('srd,srf->sdf', left, right, preferred_element_type=jnp.float32)  18.6 us
    all_to_all x1, starting transfers between devices, per_device(): lax.all_to_all(send_x.reshape(dp_count * group, slot_count, width), axes,...  12 us
    dot_general x1, matrix products, per_device(): jnp.einsum('srd,df->srf', recv_rg, wd, preferred_element_type=jnp.float32)  11.6 us
    dot_general x1, matrix products, per_device(): jnp.einsum('srd,df->srf', recv_x, wg, preferred_element_type=jnp.float32)  10.1 us
    all_to_all x1, waiting for transfers between devices, per_device(): lax.all_to_all(back.reshape(group, slot_count, width), ('seq', 'expert'),...  8.97 us
    dot_general x1, matrix products, per_device(): jnp.einsum('srd,df->srf', recv_x, wu, preferred_element_type=jnp.float32)  8.25 us
  transfers between devices with their start and end apart: 3, of which 3 were waited for; matrix products, arithmetic and copies ran while one was open for 22% of the time, Pallas kernels for 0%

profile of v2, /device:TPU:1, one launch (start us, length us, event | category | flops | bytes accessed | tf_op | source)
XLA Modules:
  0.0 182.5 jit_solution(14400502883097040960)
XLA Ops:
  0.6 0.0 copy-start
  0.7 0.8 multiply_add_fusion
  1.5 0.4 copy-done
  1.9 3.2 %convert_bitcast_fusion = bf16[128,8,2048]{2,1,0:T(8,128)(2,1)} fusion(bf16[256,2048]{1,0:T(8,128)(2,1)S(1)} %copy-done, s32[256]{0:T(256)S(1)} %bitcast.54, s32[256]{0:T(256)S(1)} %bitcast.51, s32[1024]{0:T(1024)S(1)} %get-tuple-element.10, s32[1024]{0:T(1024)S(1)} %get-tuple-element.11, pred[1024]{0:T(1024)(128)(4,1)S(1)} %fusion.41), kind=kOutput, calls=%fused_computation.19 | convolution fusion | flops 1076887552 | bytes 5254144 | tf_op jit(solution)/shard_map/dot_general | solution.py:27
  5.1 0.0 copy-start.1
  5.1 0.0 copy-start.5
  5.1 12.0 %all-to-all-start.1 = ((bf16[128,8,2048]{2,1,0:T(8,128)(2,1)}), bf16[128,8,2048]{2,1,0:T(8,128)(2,1)}, u32[]{:S(2)}, u32[]{:S(2)}) async-start(bf16[128,8,2048]{2,1,0:T(8,128)(2,1)} %convert_bitcast_fusion), calls=%async_computation.1 | async-start | bytes 8388608 | tf_op jit(solution)/shard_map/all_to_all | solution.py:32
  17.1 0.0 copy-done.1
  17.1 0.0 copy-done.5
  17.1 3.2 %convert_bitcast_fusion.1 = bf16[128,8,2048]{2,1,0:T(8,128)(2,1)} fusion(bf16[256,2048]{1,0:T(8,128)(2,1)S(1)} %copy-done.5, s32[256]{0:T(256)S(1)} %bitcast.55, s32[256]{0:T(256)S(1)} %bitcast.52, s32[1024]{0:T(1024)S(1)} %get-tuple-element.10, s32[1024]{0:T(1024)S(1)} %get-tuple-element.11, pred[1024]{0:T(1024)(128)(4,1)S(1)} %fusion.41, ...), kind=kOutput, calls=%fused_computation.20 | convolution fusion | flops 1077149696 | bytes 5255168 | tf_op jit(solution)/shard_map/dot_general | solution.py:28
  20.4 47.9 %all-to-all-done.1 = bf16[128,8,2048]{2,1,0:T(8,128)(2,1)} async-done(((bf16[128,8,2048]{2,1,0:T(8,128)(2,1)}), bf16[128,8,2048]{2,1,0:T(8,128)(2,1)}, u32[]{:S(2)}, u32[]{:S(2)}) %all-to-all-start.1) | async-done | bytes 4194336 | tf_op jit(solution)/shard_map/all_to_all | solution.py:32
  68.3 7.3 %all-to-all-start = ((bf16[128,8,2048]{2,1,0:T(8,128)(2,1)}), bf16[128,8,2048]{2,1,0:T(8,128)(2,1)}, u32[]{:S(2)}, u32[]{:S(2)}) async-start(bf16[128,8,2048]{2,1,0:T(8,128)(2,1)} %convert_bitcast_fusion.1), calls=%async_computation | async-start | bytes 8388608 | tf_op jit(solution)/shard_map/all_to_all | solution.py:35
  75.6 0.0 copy-start.3
  75.6 10.1 %fusion = f32[2,512,1024]{2,1,0:T(8,128)} fusion(bf16[2,512,2048]{2,1,0:T(8,128)(2,1)} %bitcast.7, bf16[1,2048,1024]{2,1,0:T(8,128)(2,1)} %param.13), kind=kOutput, calls=%fused_computation | convolution fusion | flops 4294967296 | bytes 12582912 | tf_op jit(solution)/shard_map/srd,df->srf/dot_general | solution.py:40
  85.7 0.0 copy-done.3
  85.7 8.2 %fusion.4 = f32[2,512,1024]{2,1,0:T(8,128)} fusion(bf16[2,512,2048]{2,1,0:T(8,128)(2,1)} %bitcast.7, bf16[1,2048,1024]{2,1,0:T(8,128)(2,1)S(1)} %copy-done.3), kind=kOutput, calls=%fused_computation.4 | convolution fusion | flops 4294967296 | bytes 12582912 | tf_op jit(solution)/shard_map/srd,df->srf/dot_general | solution.py:41
  93.9 32.9 %all-to-all-done = bf16[128,8,2048]{2,1,0:T(8,128)(2,1)} async-done(((bf16[128,8,2048]{2,1,0:T(8,128)(2,1)}), bf16[128,8,2048]{2,1,0:T(8,128)(2,1)}, u32[]{:S(2)}, u32[]{:S(2)}) %all-to-all-start) | async-done | bytes 4194336 | tf_op jit(solution)/shard_map/all_to_all | solution.py:35
  126.8 0.0 copy-start.2
  126.8 11.6 %multiply_convert_fusion.1 = (bf16[2,512,1024]{2,1,0:T(8,128)(2,1)S(1)}, bf16[2,512,1024]{2,1,0:T(8,128)(2,1)S(1)}) fusion(f32[2,512,1024]{2,1,0:T(8,128)} %fusion, f32[2,512,1024]{2,1,0:T(8,128)} %fusion.4, bf16[2,512,2048]{2,1,0:T(8,128)(2,1)} %bitcast.3, bf16[1,2048,1024]{2,1,0:T(8,128)(2,1)} %param.15), kind=kOutput, calls=%fused_computation.15 | convolution fusion | flops 4308598784 | bytes 20971520 | tf_op jit(solution)/shard_map/srd,df->srf/dot_general | solution.py:45
  138.4 0.0 copy-start.6
  138.4 0.0 copy-start.8
  138.5 0.0 copy-done.2
  138.5 0.0 copy-start.4
  138.5 2.4 %fusion.2 = f32[512,2048]{1,0:T(8,128)S(1)} fusion(bf16[1,2048,1024]{2,1,0:T(8,128)(2,1)S(1)} %copy-done.2, bf16[2,512,1024]{2,1,0:T(8,128)(2,1)S(1)} %get-tuple-element.7, s32[]{:T(128)S(6)} %select_n.29), kind=kOutput, calls=%fused_computation.2 | convolution fusion | flops 2147483648 | bytes 9437188 | tf_op jit(solution)/shard_map/dot_general | solution.py:53
  140.9 0.0 copy-done.6
  140.9 0.0 copy-done.8
  140.9 1.3 copy-done.4
  142.2 3.7 %fusion.13 = bf16[64,8,2048]{2,1,0:T(8,128)(2,1)} fusion(f32[512,2048]{1,0:T(8,128)S(1)} %fusion.2, bf16[1,2048,1024]{2,1,0:T(8,128)(2,1)S(1)} %copy-done.4, bf16[2,512,1024]{2,1,0:T(8,128)(2,1)S(1)} %get-tuple-element.6, s32[]{:T(128)S(6)} %select_n.29), kind=kOutput, calls=%fused_computation.21 | convolution fusion | flops 2149580800 | bytes 11534340 | tf_op jit(solution)/shard_map/dot_general | solution.py:54
  145.9 6.4 %all-to-all-start.2 = ((bf16[64,8,2048]{2,1,0:T(8,128)(2,1)}), bf16[64,8,2048]{2,1,0:T(8,128)(2,1)S(1)}, u32[]{:S(2)}, u32[]{:S(2)}) async-start(bf16[64,8,2048]{2,1,0:T(8,128)(2,1)} %fusion.13), calls=%async_computation.2 | async-start | bytes 4194304 | tf_op jit(solution)/shard_map/all_to_all | solution.py:55
  152.3 0.9 fusion.21
  153.2 0.0 copy-start.7
  153.2 6.5 %convert_reduce_fusion.1 = bf16[1024,1024]{1,0:T(8,128)(2,1)} fusion(bf16[2,512,1024]{2,1,0:T(8,128)(2,1)} %copy-done.8, bf16[2,512,2048]{2,1,0:T(8,128)(2,1)} %bitcast.7, s32[]{:T(128)S(6)} %select_n.30), kind=kOutput, calls=%fused_computation.12 | convolution fusion | flops 2150629376 | bytes 6291460 | tf_op jit(solution)/shard_map/srd,srf->sdf/dot_general | solution.py:63
  159.8 0.0 copy-done.7
  159.8 0.0 copy-start.9
  159.8 0.0 copy-start.10
  159.8 6.0 %convert_reduce_fusion.2 = bf16[1024,1024]{1,0:T(8,128)(2,1)} fusion(bf16[2,512,1024]{2,1,0:T(8,128)(2,1)S(1)} %copy-done.7, bf16[2,512,2048]{2,1,0:T(8,128)(2,1)} %bitcast.7, s32[]{:T(128)S(6)} %select_n.30), kind=kOutput, calls=%fused_computation.13 | convolution fusion | flops 2150629376 | bytes 6291460 | tf_op jit(solution)/shard_map/srd,srf->sdf/dot_general | solution.py:63
  165.7 0.0 copy-done.9
  165.7 0.0 copy-done.10
  165.7 6.1 %convert_reduce_fusion = bf16[1024,1024]{1,0:T(8,128)(2,1)} fusion(f32[2,512,1024]{2,1,0:T(8,128)S(1)} %copy-done.10, bf16[2,512,2048]{2,1,0:T(8,128)(2,1)} %bitcast.3, s32[]{:T(128)S(6)} %select_n.30, f32[2,512,1024]{2,1,0:T(8,128)S(1)} %copy-done.9), kind=kOutput, calls=%fused_computation.10 | convolution fusion | flops 2156920832 | bytes 12582916 | tf_op jit(solution)/shard_map/srd,srf->sdf/dot_general | solution.py:63
  171.8 9.0 %all-to-all-done.2 = bf16[64,8,2048]{2,1,0:T(8,128)(2,1)S(1)} async-done(((bf16[64,8,2048]{2,1,0:T(8,128)(2,1)}), bf16[64,8,2048]{2,1,0:T(8,128)(2,1)S(1)}, u32[]{:S(2)}, u32[]{:S(2)}) %all-to-all-start.2) | async-done | bytes 2097184 | tf_op jit(solution)/shard_map/all_to_all | solution.py:55
  180.8 1.7 convolution_convert_fusion
  (4 shorter events, 0.0 us)
Async XLA Ops:
  0.6 1.3 copy-start
  5.1 12.0 %copy-start.1 = (bf16[256,2]{0,1:T(2,128)(2,1)S(1)}, bf16[256,2]{0,1:T(2,128)(2,1)}, u32[]{:S(2)}) copy-start(bf16[256,2]{0,1:T(2,128)(2,1)} %param.10) | copy-start | bytes 3076
  5.1 12.0 %copy-start.5 = (bf16[256,2048]{1,0:T(8,128)(2,1)S(1)}, bf16[256,2048]{1,0:T(8,128)(2,1)}, u32[]{:S(2)}) copy-start(bf16[256,2048]{1,0:T(8,128)(2,1)} %param.9) | copy-start | bytes 3145732
  5.1 63.2 %all-to-all-start.1 = ((bf16[128,8,2048]{2,1,0:T(8,128)(2,1)}), bf16[128,8,2048]{2,1,0:T(8,128)(2,1)}, u32[]{:S(2)}, u32[]{:S(2)}) async-start(bf16[128,8,2048]{2,1,0:T(8,128)(2,1)} %convert_bitcast_fusion), calls=%async_computation.1 | async-start | bytes 8388608 | tf_op jit(solution)/shard_map/all_to_all | solution.py:32
  68.3 58.5 %all-to-all-start = ((bf16[128,8,2048]{2,1,0:T(8,128)(2,1)}), bf16[128,8,2048]{2,1,0:T(8,128)(2,1)}, u32[]{:S(2)}, u32[]{:S(2)}) async-start(bf16[128,8,2048]{2,1,0:T(8,128)(2,1)} %convert_bitcast_fusion.1), calls=%async_computation | async-start | bytes 8388608 | tf_op jit(solution)/shard_map/all_to_all | solution.py:35
  75.6 10.1 %copy-start.3 = (bf16[1,2048,1024]{2,1,0:T(8,128)(2,1)S(1)}, bf16[1,2048,1024]{2,1,0:T(8,128)(2,1)}, u32[]{:S(2)}) copy-start(bf16[1,2048,1024]{2,1,0:T(8,128)(2,1)} %param.14) | copy-start | bytes 12582916
  126.8 11.6 %copy-start.2 = (bf16[1,2048,1024]{2,1,0:T(8,128)(2,1)S(1)}, bf16[1,2048,1024]{2,1,0:T(8,128)(2,1)}, u32[]{:S(2)}) copy-start(bf16[1,2048,1024]{2,1,0:T(8,128)(2,1)} %param.13) | copy-start | bytes 12582916
  138.4 2.4 %copy-start.6 = (bf16[2,512,1024]{2,1,0:T(8,128)(2,1)}, bf16[2,512,1024]{2,1,0:T(8,128)(2,1)S(1)}, u32[]{:S(2)}) copy-start(bf16[2,512,1024]{2,1,0:T(8,128)(2,1)S(1)} %get-tuple-element.7) | copy-start | bytes 6291460
  138.4 2.4 %copy-start.8 = (bf16[2,512,1024]{2,1,0:T(8,128)(2,1)}, bf16[2,512,1024]{2,1,0:T(8,128)(2,1)S(1)}, u32[]{:S(2)}) copy-start(bf16[2,512,1024]{2,1,0:T(8,128)(2,1)S(1)} %get-tuple-element.6) | copy-start | bytes 6291460
  138.5 3.7 %copy-start.4 = (bf16[1,2048,1024]{2,1,0:T(8,128)(2,1)S(1)}, bf16[1,2048,1024]{2,1,0:T(8,128)(2,1)}, u32[]{:S(2)}) copy-start(bf16[1,2048,1024]{2,1,0:T(8,128)(2,1)} %param.14) | copy-start | bytes 12582916
  145.9 34.9 %all-to-all-start.2 = ((bf16[64,8,2048]{2,1,0:T(8,128)(2,1)}), bf16[64,8,2048]{2,1,0:T(8,128)(2,1)S(1)}, u32[]{:S(2)}, u32[]{:S(2)}) async-start(bf16[64,8,2048]{2,1,0:T(8,128)(2,1)} %fusion.13), calls=%async_computation.2 | async-start | bytes 4194304 | tf_op jit(solution)/shard_map/all_to_all | solution.py:55
  153.2 6.6 %copy-start.7 = (bf16[2,512,1024]{2,1,0:T(8,128)(2,1)S(1)}, bf16[2,512,1024]{2,1,0:T(8,128)(2,1)}, u32[]{:S(2)}) copy-start(bf16[2,512,1024]{2,1,0:T(8,128)(2,1)} %copy-done.6) | copy-start | bytes 6291460
  159.8 6.0 %copy-start.9 = (f32[2,512,1024]{2,1,0:T(8,128)S(1)}, f32[2,512,1024]{2,1,0:T(8,128)}, u32[]{:S(2)}) copy-start(f32[2,512,1024]{2,1,0:T(8,128)} %fusion) | copy-start | bytes 12582916
  159.8 6.0 %copy-start.10 = (f32[2,512,1024]{2,1,0:T(8,128)S(1)}, f32[2,512,1024]{2,1,0:T(8,128)}, u32[]{:S(2)}) copy-start(f32[2,512,1024]{2,1,0:T(8,128)} %fusion.4) | copy-start | bytes 12582916

commit v3 on v2

--- a/solution.py
+++ b/solution.py
@@ -37,8 +37,10 @@
     ).reshape(dp_count, group * slot_count, width)
 
     wg, wu, wd = w_gate[0], w_up[0], w_down[0]
-    gate_pre = jnp.einsum("srd,df->srf", recv_x, wg, preferred_element_type=jnp.float32)
-    up_pre = jnp.einsum("srd,df->srf", recv_x, wu, preferred_element_type=jnp.float32)
+    ff = wg.shape[1]
+    wgu = jnp.concatenate([wg, wu], axis=1)
+    pre = jnp.einsum("srd,df->srf", recv_x, wgu, preferred_element_type=jnp.float32)
+    gate_pre, up_pre = pre[..., :ff], pre[..., ff:]
     gate_sig = jax.nn.sigmoid(gate_pre)
     silu_g = gate_pre * gate_sig
     act = (silu_g * up_pre).astype(jnp.bfloat16)
@@ -47,11 +49,10 @@
         jnp.bfloat16
     )
     up_grad = (act_grad * silu_g).astype(jnp.bfloat16)
+    gu_grad = jnp.concatenate([gate_grad, up_grad], axis=-1)
 
-    gg_own = lax.dynamic_index_in_dim(gate_grad, me, 0, keepdims=False)
-    ug_own = lax.dynamic_index_in_dim(up_grad, me, 0, keepdims=False)
-    back = jnp.dot(gg_own, wg.T, preferred_element_type=jnp.float32)
-    back = (back + jnp.dot(ug_own, wu.T, preferred_element_type=jnp.float32)).astype(jnp.bfloat16)
+    gu_own = lax.dynamic_index_in_dim(gu_grad, me, 0, keepdims=False)
+    back = jnp.dot(gu_own, wgu.T, preferred_element_type=jnp.float32).astype(jnp.bfloat16)
     returned = lax.all_to_all(
         back.reshape(group, slot_count, width), ("seq", "expert"), 0, 0, tiled=True
     ).reshape(rows, width)
@@ -61,11 +62,11 @@
 
     def wgrad(left, right):
         per_seq = jnp.einsum("srd,srf->sdf", left, right, preferred_element_type=jnp.float32)
-        per_seq = per_seq.astype(jnp.bfloat16).astype(jnp.float32)
+        per_seq = lax.reduce_precision(per_seq, exponent_bits=8, mantissa_bits=7)
         return per_seq.sum(axis=0).astype(jnp.bfloat16)[None]
 
-    grad_gate = wgrad(x_half, gate_grad)
-    grad_up = wgrad(x_half, up_grad)
+    grad_gu = wgrad(x_half, gu_grad)
+    grad_gate, grad_up = grad_gu[..., :ff], grad_gu[..., ff:]
     grad_down = wgrad(rg_half, act)
 
     grad_tokens = jnp.dot(

time: 183 us -> 183 us (level)
  local copies, waits for them, and re-layouts: 1.79 us -> 7.15 us
  matrix products: 62.8 us -> 60.1 us
  waiting for transfers between devices: 89.8 us -> 87.6 us
    slice x0 -> x1, local copies, waits for them, and re-layouts: none -> 4.67 us  [per_device(): grad_gate, grad_up = (grad_gu[..., :ff], grad_gu[..., ff:])]
    all_to_all x1, waiting for transfers between devices: 8.97 us -> 4.39 us  [per_device(): lax.all_to_all(back.reshape(group, slot_count, width), ('seq', 'expert'),...]
    dot_general x4 -> x2, matrix products: 24.4 us -> 20.9 us  [the longest x1 15 us: per_device(): jnp.einsum('srd,df->srf', recv_x, wgu, preferred_element_type=jnp.float32)]
    all_to_all x1, waiting for transfers between devices: 32.9 us -> 35.3 us  [per_device(): lax.all_to_all(send_rg.reshape(dp_count * group, slot_count, width), axes...]
    dot_general x3 -> x2, matrix products: 18.6 us -> 19.4 us  [wgrad(): jnp.einsum('srd,srf->sdf', left, right, preferred_element_type=jnp.float32)]
  transfers between devices with their start and end apart: 3 -> 3, of which waited for: 3 -> 3; matrix products, arithmetic and copies ran while one was open for 22% -> 24% of each run, Pallas kernels for 0% -> 0%
where the time goes in v3:
time: 183 us
  waiting for transfers between devices  87.6 us (48%)
  matrix products  60.1 us (33%)
  starting transfers between devices  25.6 us (14%)
  local copies, waits for them, and re-layouts  7.15 us (4%)
    all_to_all x1, waiting for transfers between devices, per_device(): lax.all_to_all(send_x.reshape(dp_count * group, slot_count, width), axes,...  47.9 us
    all_to_all x1, waiting for transfers between devices, per_device(): lax.all_to_all(send_rg.reshape(dp_count * group, slot_count, width), axes...  35.3 us
    dot_general x2, matrix products, wgrad(): jnp.einsum('srd,srf->sdf', left, right, preferred_element_type=jnp.float32)  19.4 us
    dot_general x1, matrix products, per_device(): jnp.einsum('srd,df->srf', recv_x, wgu, preferred_element_type=jnp.float32)  15 us
    all_to_all x1, starting transfers between devices, per_device(): lax.all_to_all(send_x.reshape(dp_count * group, slot_count, width), axes,...  12 us
    dot_general x1, matrix products, per_device(): jnp.einsum('srd,df->srf', recv_rg, wd, preferred_element_type=jnp.float32)  11.6 us
    all_to_all x1, starting transfers between devices, per_device(): lax.all_to_all(send_rg.reshape(dp_count * group, slot_count, width), axes...  7.29 us
    all_to_all x1, starting transfers between devices, per_device(): lax.all_to_all(back.reshape(group, slot_count, width), ('seq', 'expert'),...  6.4 us
  transfers between devices with their start and end apart: 3, of which 3 were waited for; matrix products, arithmetic and copies ran while one was open for 24% of the time, Pallas kernels for 0%

profile of v3, /device:TPU:1, one launch (start us, length us, event | category | flops | bytes accessed | tf_op | source)
XLA Modules:
  0.0 182.9 jit_solution(14774717962915092354)
XLA Ops:
  0.6 0.0 copy-start
  0.7 0.8 multiply_add_fusion
  1.5 0.4 copy-done
  1.9 3.2 %convert_bitcast_fusion.1 = bf16[128,8,2048]{2,1,0:T(8,128)(2,1)} fusion(bf16[256,2048]{1,0:T(8,128)(2,1)S(1)} %copy-done, s32[256]{0:T(256)S(1)} %bitcast.41, s32[256]{0:T(256)S(1)} %bitcast.38, s32[1024]{0:T(1024)S(1)} %get-tuple-element.12, s32[1024]{0:T(1024)S(1)} %get-tuple-element.13, pred[1024]{0:T(1024)(128)(4,1)S(1)} %fusion.31), kind=kOutput, calls=%fused_computation.17 | convolution fusion | flops 1076887552 | bytes 5254144 | tf_op jit(solution)/shard_map/dot_general | solution.py:27
  5.1 0.0 copy-start.1
  5.1 0.0 copy-start.4
  5.1 12.0 %all-to-all-start.1 = ((bf16[128,8,2048]{2,1,0:T(8,128)(2,1)}), bf16[128,8,2048]{2,1,0:T(8,128)(2,1)}, u32[]{:S(2)}, u32[]{:S(2)}) async-start(bf16[128,8,2048]{2,1,0:T(8,128)(2,1)} %convert_bitcast_fusion.1), calls=%async_computation.1 | async-start | bytes 8388608 | tf_op jit(solution)/shard_map/all_to_all | solution.py:32
  17.1 0.0 copy-done.1
  17.1 0.0 copy-done.4
  17.1 3.2 %convert_bitcast_fusion.2 = bf16[128,8,2048]{2,1,0:T(8,128)(2,1)} fusion(bf16[256,2048]{1,0:T(8,128)(2,1)S(1)} %copy-done.4, s32[256]{0:T(256)S(1)} %bitcast.42, s32[256]{0:T(256)S(1)} %bitcast.39, s32[1024]{0:T(1024)S(1)} %get-tuple-element.12, s32[1024]{0:T(1024)S(1)} %get-tuple-element.13, pred[1024]{0:T(1024)(128)(4,1)S(1)} %fusion.31, ...), kind=kOutput, calls=%fused_computation.18 | convolution fusion | flops 1077149696 | bytes 5255168 | tf_op jit(solution)/shard_map/dot_general | solution.py:28
  20.4 47.9 %all-to-all-done.1 = bf16[128,8,2048]{2,1,0:T(8,128)(2,1)} async-done(((bf16[128,8,2048]{2,1,0:T(8,128)(2,1)}), bf16[128,8,2048]{2,1,0:T(8,128)(2,1)}, u32[]{:S(2)}, u32[]{:S(2)}) %all-to-all-start.1) | async-done | bytes 4194336 | tf_op jit(solution)/shard_map/all_to_all | solution.py:32
  68.3 7.3 %all-to-all-start = ((bf16[128,8,2048]{2,1,0:T(8,128)(2,1)}), bf16[128,8,2048]{2,1,0:T(8,128)(2,1)}, u32[]{:S(2)}, u32[]{:S(2)}) async-start(bf16[128,8,2048]{2,1,0:T(8,128)(2,1)} %convert_bitcast_fusion.2), calls=%async_computation | async-start | bytes 8388608 | tf_op jit(solution)/shard_map/all_to_all | solution.py:35
  75.6 0.9 fusion.15
  76.5 15.0 %fusion = f32[2,512,2048]{2,1,0:T(8,128)} fusion(bf16[2,512,2048]{2,1,0:T(8,128)(2,1)} %bitcast.7, bf16[2048,1024]{1,0:T(8,128)(2,1)} %bitcast.44, bf16[2048,1024]{1,0:T(8,128)(2,1)} %bitcast.46), kind=kOutput, calls=%fused_computation.2 | convolution fusion | flops 8606711808 | bytes 20971520 | tf_op jit(solution)/shard_map/srd,df->srf/dot_general | solution.py:42
  91.6 35.3 %all-to-all-done = bf16[128,8,2048]{2,1,0:T(8,128)(2,1)} async-done(((bf16[128,8,2048]{2,1,0:T(8,128)(2,1)}), bf16[128,8,2048]{2,1,0:T(8,128)(2,1)}, u32[]{:S(2)}, u32[]{:S(2)}) %all-to-all-start) | async-done | bytes 4194336 | tf_op jit(solution)/shard_map/all_to_all | solution.py:35
  126.8 0.0 copy-start.2
  126.8 0.0 copy-start.3
  126.8 11.6 %multiply_convert_fusion.1 = (bf16[2,512,1024]{2,1,0:T(8,128)(2,1)S(1)}, bf16[2,512,1024]{2,1,0:T(8,128)(2,1)S(1)}) fusion(f32[2,512,2048]{2,1,0:T(8,128)} %fusion, bf16[2,512,2048]{2,1,0:T(8,128)(2,1)} %bitcast.3, bf16[1,2048,1024]{2,1,0:T(8,128)(2,1)} %param.15), kind=kOutput, calls=%fused_computation.13 | convolution fusion | flops 4308598784 | bytes 20971520 | tf_op jit(solution)/shard_map/srd,df->srf/dot_general | solution.py:47
  138.4 0.0 copy-start.5
  138.4 0.0 copy-start.6
  138.5 1.3 copy-done.5
  139.8 0.7 copy-done.6
  140.4 0.0 copy-done.2
  140.4 0.0 copy-done.3
  140.5 5.9 %fusion.7 = bf16[64,8,2048]{2,1,0:T(8,128)(2,1)} fusion(bf16[2048,1024]{1,0:T(8,128)(2,1)S(1)} %bitcast.45, bf16[2048,1024]{1,0:T(8,128)(2,1)S(1)} %bitcast.47, s32[]{:T(128)S(6)} %select_n.28, bf16[2,512,1024]{2,1,0:T(8,128)(2,1)S(1)} %get-tuple-element.7, bf16[2,512,1024]{2,1,0:T(8,128)(2,1)S(1)} %get-tuple-element.6), kind=kOutput, calls=%fused_computation.20 | convolution fusion | flops 4316987392 | bytes 14680068 | tf_op jit(solution)/shard_map/dot_general | solution.py:55
  146.3 6.4 %all-to-all-start.2 = ((bf16[64,8,2048]{2,1,0:T(8,128)(2,1)}), bf16[64,8,2048]{2,1,0:T(8,128)(2,1)S(1)}, u32[]{:S(2)}, u32[]{:S(2)}) async-start(bf16[64,8,2048]{2,1,0:T(8,128)(2,1)} %fusion.7), calls=%async_computation.2 | async-start | bytes 4194304 | tf_op jit(solution)/shard_map/all_to_all | solution.py:56
  152.7 10.8 %reduce-precision_reduce_fusion = bf16[1024,2048]{1,0:T(8,128)(2,1)} fusion(bf16[2,512,1024]{2,1,0:T(8,128)(2,1)} %copy-done.5, bf16[2,512,1024]{2,1,0:T(8,128)(2,1)} %copy-done.6, bf16[2,512,2048]{2,1,0:T(8,128)(2,1)} %bitcast.7, s32[]{:T(128)S(6)} %select_n.29), kind=kOutput, calls=%fused_computation | convolution fusion | flops 4309647360 | bytes 10485764 | tf_op jit(solution)/shard_map/srd,srf->sdf/dot_general | solution.py:64
  163.6 4.7 %fusion.41 = (bf16[1,1024,1024]{2,1,0:T(8,128)(2,1)}, bf16[1,1024,1024]{2,1,0:T(8,128)(2,1)}) fusion(bf16[1,1024,2048]{2,1,0:T(8,128)(2,1)} %bitcast.37), kind=kLoop, calls=%fused_computation.58 | loop fusion | bytes 8388608 | tf_op jit(solution)/shard_map/slice | solution.py:69
  168.2 8.6 %reduce-precision_reduce_fusion.1 = bf16[1024,1024]{1,0:T(8,128)(2,1)} fusion(f32[2,512,2048]{2,1,0:T(8,128)} %fusion, bf16[2,512,2048]{2,1,0:T(8,128)(2,1)} %bitcast.3, s32[]{:T(128)S(6)} %select_n.29), kind=kOutput, calls=%fused_computation.4 | convolution fusion | flops 2156920832 | bytes 12582916 | tf_op jit(solution)/shard_map/srd,srf->sdf/dot_general | solution.py:64
  176.8 4.4 %all-to-all-done.2 = bf16[64,8,2048]{2,1,0:T(8,128)(2,1)S(1)} async-done(((bf16[64,8,2048]{2,1,0:T(8,128)(2,1)}), bf16[64,8,2048]{2,1,0:T(8,128)(2,1)S(1)}, u32[]{:S(2)}, u32[]{:S(2)}) %all-to-all-start.2) | async-done | bytes 2097184 | tf_op jit(solution)/shard_map/all_to_all | solution.py:56
  181.2 1.7 convolution_convert_fusion
  (4 shorter events, 0.0 us)
Async XLA Ops:
  0.6 1.3 copy-start
  5.1 12.0 %copy-start.1 = (bf16[256,2]{0,1:T(2,128)(2,1)S(1)}, bf16[256,2]{0,1:T(2,128)(2,1)}, u32[]{:S(2)}) copy-start(bf16[256,2]{0,1:T(2,128)(2,1)} %param.10) | copy-start | bytes 3076
  5.1 12.0 %copy-start.4 = (bf16[256,2048]{1,0:T(8,128)(2,1)S(1)}, bf16[256,2048]{1,0:T(8,128)(2,1)}, u32[]{:S(2)}) copy-start(bf16[256,2048]{1,0:T(8,128)(2,1)} %param.9) | copy-start | bytes 3145732
  5.1 63.2 %all-to-all-start.1 = ((bf16[128,8,2048]{2,1,0:T(8,128)(2,1)}), bf16[128,8,2048]{2,1,0:T(8,128)(2,1)}, u32[]{:S(2)}, u32[]{:S(2)}) async-start(bf16[128,8,2048]{2,1,0:T(8,128)(2,1)} %convert_bitcast_fusion.1), calls=%async_computation.1 | async-start | bytes 8388608 | tf_op jit(solution)/shard_map/all_to_all | solution.py:32
  68.3 58.5 %all-to-all-start = ((bf16[128,8,2048]{2,1,0:T(8,128)(2,1)}), bf16[128,8,2048]{2,1,0:T(8,128)(2,1)}, u32[]{:S(2)}, u32[]{:S(2)}) async-start(bf16[128,8,2048]{2,1,0:T(8,128)(2,1)} %convert_bitcast_fusion.2), calls=%async_computation | async-start | bytes 8388608 | tf_op jit(solution)/shard_map/all_to_all | solution.py:35
  126.8 13.6 %copy-start.2 = (bf16[1,2048,1024]{2,1,0:T(8,128)(2,1)S(1)}, bf16[1,2048,1024]{2,1,0:T(8,128)(2,1)}, u32[]{:S(2)}) copy-start(bf16[1,2048,1024]{2,1,0:T(8,128)(2,1)} %param.14) | copy-start | bytes 12582916
  126.8 13.6 %copy-start.3 = (bf16[1,2048,1024]{2,1,0:T(8,128)(2,1)S(1)}, bf16[1,2048,1024]{2,1,0:T(8,128)(2,1)}, u32[]{:S(2)}) copy-start(bf16[1,2048,1024]{2,1,0:T(8,128)(2,1)} %param.13) | copy-start | bytes 12582916
  138.4 1.3 copy-start.5
  138.4 2.0 %copy-start.6 = (bf16[2,512,1024]{2,1,0:T(8,128)(2,1)}, bf16[2,512,1024]{2,1,0:T(8,128)(2,1)S(1)}, u32[]{:S(2)}) copy-start(bf16[2,512,1024]{2,1,0:T(8,128)(2,1)S(1)} %get-tuple-element.7) | copy-start | bytes 6291460
  146.3 34.9 %all-to-all-start.2 = ((bf16[64,8,2048]{2,1,0:T(8,128)(2,1)}), bf16[64,8,2048]{2,1,0:T(8,128)(2,1)S(1)}, u32[]{:S(2)}, u32[]{:S(2)}) async-start(bf16[64,8,2048]{2,1,0:T(8,128)(2,1)} %fusion.7), calls=%async_computation.2 | async-start | bytes 4194304 | tf_op jit(solution)/shard_map/all_to_all | solution.py:56

commit v4 on v3

--- a/solution.py
+++ b/solution.py
@@ -19,32 +19,59 @@
     me = lax.axis_index("dp")
     position = expert_ids * slot_count + route_slots
 
-    slots = lax.broadcasted_iota(jnp.int32, (dp_count * rows, cell_count), 0) % rows
+    slots = lax.broadcasted_iota(jnp.int32, (rows, cell_count), 0)
     hit0 = slots == position[None, :, 0]
     hit1 = slots == position[None, :, 1]
     pick = (hit0 | hit1).astype(jnp.bfloat16)
     weigh = jnp.where(hit0, route_weights[None, :, 0], jnp.where(hit1, route_weights[None, :, 1], 0))
-    send_x = jnp.dot(pick, tokens, preferred_element_type=jnp.float32).astype(jnp.bfloat16)
-    send_rg = jnp.dot(weigh.astype(jnp.bfloat16), grad_out, preferred_element_type=jnp.float32).astype(
-        jnp.bfloat16
-    )
+    rows_x = jnp.dot(pick, tokens, preferred_element_type=jnp.float32).astype(jnp.bfloat16)
+    rows_rg = jnp.dot(
+        weigh.astype(jnp.bfloat16), grad_out, preferred_element_type=jnp.float32
+    ).astype(jnp.bfloat16)
     axes = ("dp", "seq", "expert")
-    recv_x = lax.all_to_all(
-        send_x.reshape(dp_count * group, slot_count, width), axes, 0, 0, tiled=True
-    ).reshape(dp_count, group * slot_count, width)
-    recv_rg = lax.all_to_all(
-        send_rg.reshape(dp_count * group, slot_count, width), axes, 0, 0, tiled=True
-    ).reshape(dp_count, group * slot_count, width)
+
+    def exchange(rows_all, first):
+        halves = [rows_all[:, d * half:(d + 1) * half] for d in range(dp_count)]
+        if not first:
+            halves = halves[1:] + halves[:1]
+        send = jnp.stack(halves, axis=0).reshape(dp_count * group, slot_count, half)
+        recv = lax.all_to_all(send, axes, 0, 0, tiled=True)
+        return recv.reshape(dp_count, group * slot_count, half)
+
+    x_mine = exchange(rows_x, True)
+    x_rest = exchange(rows_x, False)
+    rg_mine = exchange(rows_rg, True)
+    rg_rest = exchange(rows_rg, False)
 
     wg, wu, wd = w_gate[0], w_up[0], w_down[0]
     ff = wg.shape[1]
     wgu = jnp.concatenate([wg, wu], axis=1)
-    pre = jnp.einsum("srd,df->srf", recv_x, wgu, preferred_element_type=jnp.float32)
+    wgu_mine = lax.dynamic_slice_in_dim(wgu, me * half, half, axis=0)
+    wgu_rest = lax.dynamic_slice_in_dim(wgu, (1 - me) * half, half, axis=0)
+    wd_mine = lax.dynamic_slice_in_dim(wd, me * half, half, axis=0)
+    wd_rest = lax.dynamic_slice_in_dim(wd, (1 - me) * half, half, axis=0)
+    def wgrad(left, right):
+        per_seq = jnp.einsum("srd,srf->sdf", left, right, preferred_element_type=jnp.float32)
+        per_seq = lax.reduce_precision(per_seq, exponent_bits=8, mantissa_bits=7)
+        return per_seq.sum(axis=0).astype(jnp.bfloat16)[None]
+
+    pre = jnp.einsum("srd,df->srf", x_mine, wgu_mine, preferred_element_type=jnp.float32)
+    x_rest, pre = lax.optimization_barrier((x_rest, pre))
+    pre = pre + jnp.einsum("srd,df->srf", x_rest, wgu_rest, preferred_element_type=jnp.float32)
     gate_pre, up_pre = pre[..., :ff], pre[..., ff:]
     gate_sig = jax.nn.sigmoid(gate_pre)
     silu_g = gate_pre * gate_sig
     act = (silu_g * up_pre).astype(jnp.bfloat16)
-    act_grad = jnp.einsum("srd,df->srf", recv_rg, wd, preferred_element_type=jnp.float32)
+    rg_mine, pre, act = lax.optimization_barrier((rg_mine, pre, act))
+    gate_pre, up_pre = pre[..., :ff], pre[..., ff:]
+    gate_sig = jax.nn.sigmoid(gate_pre)
+    silu_g = gate_pre * gate_sig
+    act_grad = jnp.einsum("srd,df->srf", rg_mine, wd_mine, preferred_element_type=jnp.float32)
+    grad_down = wgrad(rg_mine, act)
+    rg_rest, act_grad, grad_down = lax.optimization_barrier((rg_rest, act_grad, grad_down))
+    act_grad = act_grad + jnp.einsum(
+        "srd,df->srf", rg_rest, wd_rest, preferred_element_type=jnp.float32
+    )
     gate_grad = (act_grad * up_pre * gate_sig * (1.0 + gate_pre * (1.0 - gate_sig))).astype(
         jnp.bfloat16
     )
@@ -57,20 +84,11 @@
         back.reshape(group, slot_count, width), ("seq", "expert"), 0, 0, tiled=True
     ).reshape(rows, width)
 
-    x_half = lax.dynamic_slice_in_dim(recv_x, me * half, half, axis=2)
-    rg_half = lax.dynamic_slice_in_dim(recv_rg, me * half, half, axis=2)
-
-    def wgrad(left, right):
-        per_seq = jnp.einsum("srd,srf->sdf", left, right, preferred_element_type=jnp.float32)
-        per_seq = lax.reduce_precision(per_seq, exponent_bits=8, mantissa_bits=7)
-        return per_seq.sum(axis=0).astype(jnp.bfloat16)[None]
-
-    grad_gu = wgrad(x_half, gu_grad)
+    grad_gu = wgrad(x_mine, gu_grad)
     grad_gate, grad_up = grad_gu[..., :ff], grad_gu[..., ff:]
-    grad_down = wgrad(rg_half, act)
 
     grad_tokens = jnp.dot(
-        pick[:rows].T, returned, preferred_element_type=jnp.float32
+        pick.T, returned, preferred_element_type=jnp.float32
     ).astype(jnp.bfloat16)
     return grad_tokens, grad_gate, grad_up, grad_down
 

time: 183 us -> 204 us (1.11)
  blocking collectives: 0 us -> 40.9 us
  waiting for transfers between devices: 87.6 us -> 62.2 us
  other arithmetic: 1.68 us -> 6.35 us
  local copies, waits for them, and re-layouts: 7.15 us -> 11.4 us
  matrix products: 60.1 us -> 58 us
    all_to_all x0 -> x1, blocking collectives: none -> 40.9 us  [exchange(): recv = lax.all_to_all(send, axes, 0, 0, tiled=True)]
    all_to_all x2 -> x3, waiting for transfers between devices: 83.2 us -> 49.4 us  [exchange(): recv = lax.all_to_all(send, axes, 0, 0, tiled=True)]
    all_to_all x1, waiting for transfers between devices: 4.39 us -> 12.9 us  [per_device(): lax.all_to_all(back.reshape(group, slot_count, width), ('seq', 'expert'),...]
    dot_general x3 -> x5, matrix products: 28.4 us -> 33.8 us  [the longest x1 9.76 us: per_device(): jnp.einsum('srd,df->srf', x_rest, wgu_rest, preferred_element_type=jnp.fl...]
    another operation x0 -> x2, other arithmetic: none -> 4.13 us  [exchange(): send = jnp.stack(halves, axis=0).reshape(dp_count * group, slot_count, half)]
    unnamed x14 -> x22, local copies, waits for them, and re-layouts: 2.45 us -> 6.25 us
    dot_general x2, matrix products: 19.4 us -> 16.8 us  [wgrad(): jnp.einsum('srd,srf->sdf', left, right, preferred_element_type=jnp.float32)]
    dot_general x1, matrix products: 3.24 us -> 0.72 us  [per_device(): jnp.dot(weigh.astype(jnp.bfloat16), grad_out, preferred_element_type=jnp....]
  transfers between devices with their start and end apart: 3 -> 4, of which waited for: 3 -> 4; matrix products, arithmetic and copies ran while one was open for 24% -> 25% of each run, Pallas kernels for 0% -> 0%
where the time goes in v4:
time: 204 us
  waiting for transfers between devices  62.2 us (30%)
  matrix products  58 us (28%)
  blocking collectives  40.9 us (20%)
  starting transfers between devices  23.9 us (12%)
  local copies, waits for them, and re-layouts  11.4 us (6%)
  other arithmetic  6.35 us (3%)
    all_to_all x3, waiting for transfers between devices, exchange(): recv = lax.all_to_all(send, axes, 0, 0, tiled=True)  49.4 us
    all_to_all x1, blocking collectives, exchange(): recv = lax.all_to_all(send, axes, 0, 0, tiled=True)  40.9 us
    all_to_all x3, starting transfers between devices, exchange(): recv = lax.all_to_all(send, axes, 0, 0, tiled=True)  17.4 us
    dot_general x2, matrix products, wgrad(): jnp.einsum('srd,srf->sdf', left, right, preferred_element_type=jnp.float32)  16.8 us
    all_to_all x1, waiting for transfers between devices, per_device(): lax.all_to_all(back.reshape(group, slot_count, width), ('seq', 'expert'),...  12.9 us
    dot_general x1, matrix products, per_device(): jnp.einsum('srd,df->srf', x_rest, wgu_rest, preferred_element_type=jnp.fl...  9.76 us
    dot_general x1, matrix products, per_device(): jnp.einsum('srd,df->srf', x_mine, wgu_mine, preferred_element_type=jnp.fl...  8.91 us
    dot_general x1, matrix products, per_device(): jnp.einsum('srd,df->srf', rg_rest, wd_rest, preferred_element_type=jnp.fl...  7.53 us
  transfers between devices with their start and end apart: 4, of which 4 were waited for; matrix products, arithmetic and copies ran while one was open for 25% of the time, Pallas kernels for 0%

profile of v4, /device:TPU:1, one launch (start us, length us, event | category | flops | bytes accessed | tf_op | source)
XLA Modules:
  0.0 203.6 jit_solution(3241545878512220417)
XLA Ops:
  0.6 0.0 copy-start
  0.6 0.8 multiply_add_fusion
  1.4 0.5 copy-done
  1.9 0.7 convolution_convert_fusion
  2.6 0.2 slice_bitcast_fusion.1
  2.8 1.7 pad_maximum_fusion.11
  4.5 0.0 copy-start.5
  4.5 0.0 copy-start.4
  4.5 40.9 %all_to_all.25 = bf16[128,8,1024]{2,1,0:T(8,128)(2,1)S(1)} all-to-all(bf16[128,8,1024]{2,1,0:T(8,128)(2,1)S(1)} %bitcast.63), channel_id=1, replica_groups=mesh['dp'=2,'seq'=8,'expert'=8] {'dp','seq','expert'}, dimensions={0} | all-to-all | bytes 4194304 | tf_op jit(solution)/shard_map/all_to_all | solution.py:38
  45.4 0.0 copy-start.3
  45.4 6.2 %all-to-all-start.2 = ((bf16[128,8,1024]{2,1,0:T(8,128)(2,1)}), bf16[128,8,1024]{2,1,0:T(8,128)(2,1)}, u32[]{:S(2)}, u32[]{:S(2)}) async-start(bf16[128,8,1024]{2,1,0:T(8,128)(2,1)} %bitcast.10), calls=%async_computation.2 | async-start | bytes 4194304 | tf_op jit(solution)/shard_map/all_to_all | solution.py:38
  51.6 0.0 copy-done.5
  51.6 0.0 copy-done.4
  51.7 0.7 convolution_convert_fusion.1
  52.4 0.2 slice_bitcast_fusion.3
  52.6 2.4 %pad_maximum_fusion.9 = (bf16[2,512,1024]{2,1,0:T(8,128)(2,1)}, bf16[2,512,1024]{2,1,0:T(8,128)(2,1)}) fusion(bf16[1,512,1024]{2,1,0:T(8,128)(2,1)S(1)} %get-tuple-element.32, bf16[1,512,1024]{2,1,0:T(8,128)(2,1)S(1)} %get-tuple-element.33), kind=kLoop, calls=%fused_computation.32 | loop fusion | flops 2097152 | bytes 6291456 | tf_op jit(solution)/shard_map/stack | solution.py:37
  55.0 26.0 %all-to-all-done.2 = bf16[128,8,1024]{2,1,0:T(8,128)(2,1)} async-done(((bf16[128,8,1024]{2,1,0:T(8,128)(2,1)}), bf16[128,8,1024]{2,1,0:T(8,128)(2,1)}, u32[]{:S(2)}, u32[]{:S(2)}) %all-to-all-start.2) | async-done | bytes 2097184 | tf_op jit(solution)/shard_map/all_to_all | solution.py:38
  81.0 6.1 %all-to-all-start.1 = ((bf16[128,8,1024]{2,1,0:T(8,128)(2,1)}), bf16[128,8,1024]{2,1,0:T(8,128)(2,1)}, u32[]{:S(2)}, u32[]{:S(2)}) async-start(bf16[128,8,1024]{2,1,0:T(8,128)(2,1)} %bitcast.6), calls=%async_computation.1 | async-start | bytes 4194304 | tf_op jit(solution)/shard_map/all_to_all | solution.py:38
  87.2 0.0 copy-done.3
  87.2 8.9 %fusion.3 = f32[2,512,2048]{2,1,0:T(8,128)} fusion(bf16[2,512,1024]{2,1,0:T(8,128)(2,1)S(1)} %bitcast.65, s32[]{:T(128)S(6)} %select_n.22, bf16[2048,1024]{1,0:T(8,128)(2,1)} %bitcast.77, bf16[2048,1024]{1,0:T(8,128)(2,1)} %bitcast.74), kind=kOutput, calls=%fused_computation.13 | convolution fusion | flops 4303355904 | bytes 18874372 | tf_op jit(solution)/shard_map/srd,df->srf/dot_general | solution.py:58
  96.1 20.5 %all-to-all-done.1 = bf16[128,8,1024]{2,1,0:T(8,128)(2,1)} async-done(((bf16[128,8,1024]{2,1,0:T(8,128)(2,1)}), bf16[128,8,1024]{2,1,0:T(8,128)(2,1)}, u32[]{:S(2)}, u32[]{:S(2)}) %all-to-all-start.1) | async-done | bytes 2097184 | tf_op jit(solution)/shard_map/all_to_all | solution.py:38
  116.5 5.1 %all-to-all-start = ((bf16[128,8,1024]{2,1,0:T(8,128)(2,1)}), bf16[128,8,1024]{2,1,0:T(8,128)(2,1)S(1)}, u32[]{:S(2)}, u32[]{:S(2)}) async-start(bf16[128,8,1024]{2,1,0:T(8,128)(2,1)} %bitcast.4), calls=%async_computation | async-start | bytes 4194304 | tf_op jit(solution)/shard_map/all_to_all | solution.py:38
  121.6 9.8 %fusion.9 = f32[2,512,2048]{2,1,0:T(8,128)S(1)} fusion(f32[2,512,2048]{2,1,0:T(8,128)} %fusion.3, bf16[2,512,1024]{2,1,0:T(8,128)(2,1)} %bitcast.11, s32[]{:T(128)S(6)} %select_n.23, bf16[2048,1024]{1,0:T(8,128)(2,1)} %bitcast.78, bf16[2048,1024]{1,0:T(8,128)(2,1)} %bitcast.75), kind=kOutput, calls=%fused_computation.17 | convolution fusion | flops 4305453056 | bytes 27262980 | tf_op jit(solution)/shard_map/srd,df->srf/dot_general | solution.py:60
  131.4 0.0 copy-start.2
  131.4 0.0 copy-start.6
  131.4 1.4 fusion.12
  132.9 2.8 %copy-done.2 = f32[2,512,2048]{2,1,0:T(8,128)} copy-done((f32[2,512,2048]{2,1,0:T(8,128)}, f32[2,512,2048]{2,1,0:T(8,128)S(1)}, u32[]{:S(2)}) %copy-start.2) | copy-done | bytes 8388632
  135.7 1.0 copy-done.6
  136.6 5.9 %fusion.21 = f32[2,512,1024]{2,1,0:T(8,128)} fusion(bf16[2,512,1024]{2,1,0:T(8,128)(2,1)} %bitcast.7, bf16[1,2048,1024]{2,1,0:T(8,128)(2,1)S(1)} %copy-done.6, s32[]{:T(128)S(6)} %select_n.22), kind=kOutput, calls=%fused_computation.38 | convolution fusion | flops 2147483648 | bytes 8388612 | tf_op jit(solution)/shard_map/srd,df->srf/dot_general | solution.py:69
  142.5 6.0 %reduce-precision_reduce_fusion.1 = bf16[1024,1024]{1,0:T(8,128)(2,1)} fusion(bf16[2,512,1024]{2,1,0:T(8,128)(2,1)} %bitcast.7, bf16[2,512,1024]{2,1,0:T(8,128)(2,1)S(1)} %fusion.12), kind=kOutput, calls=%fused_computation.7 | convolution fusion | flops 2150629376 | bytes 6291456 | tf_op jit(solution)/shard_map/srd,srf->sdf/dot_general | solution.py:54
  148.5 2.9 %all-to-all-done = bf16[128,8,1024]{2,1,0:T(8,128)(2,1)S(1)} async-done(((bf16[128,8,1024]{2,1,0:T(8,128)(2,1)}), bf16[128,8,1024]{2,1,0:T(8,128)(2,1)S(1)}, u32[]{:S(2)}, u32[]{:S(2)}) %all-to-all-start) | async-done | bytes 2097184 | tf_op jit(solution)/shard_map/all_to_all | solution.py:38
  151.4 0.0 copy-start.7
  151.4 0.0 copy-start.8
  151.4 7.5 %multiply_convert_fusion = (bf16[2,512,1024]{2,1,0:T(8,128)(2,1)S(1)}, bf16[2,512,1024]{2,1,0:T(8,128)(2,1)S(1)}) fusion(f32[2,512,2048]{2,1,0:T(8,128)} %copy-done.2, f32[2,512,1024]{2,1,0:T(8,128)} %fusion.21, bf16[2,512,1024]{2,1,0:T(8,128)(2,1)S(1)} %bitcast.67, bf16[1,2048,1024]{2,1,0:T(8,128)(2,1)} %param.15, s32[]{:T(128)S(6)} %select_n.23), kind=kOutput, calls=%fused_computation.21 | convolution fusion | flops 2162163712 | bytes 20971524 | tf_op jit(solution)/shard_map/srd,df->srf/dot_general | solution.py:72
  158.9 0.0 copy-start.9
  158.9 0.0 copy-start.10
  158.9 1.3 copy-done.9
  160.2 0.7 copy-done.10
  160.9 0.0 copy-done.7
  160.9 0.0 copy-done.8
  160.9 5.9 %fusion.14 = bf16[64,8,2048]{2,1,0:T(8,128)(2,1)} fusion(bf16[2048,1024]{1,0:T(8,128)(2,1)S(1)} %bitcast.76, bf16[2048,1024]{1,0:T(8,128)(2,1)S(1)} %bitcast.79, s32[]{:T(128)S(6)} %select_n.24, bf16[2,512,1024]{2,1,0:T(8,128)(2,1)S(1)} %get-tuple-element.23, bf16[2,512,1024]{2,1,0:T(8,128)(2,1)S(1)} %get-tuple-element.22), kind=kOutput, calls=%fused_computation.27 | convolution fusion | flops 4316987392 | bytes 14680068 | tf_op jit(solution)/shard_map/dot_general | solution.py:82
  166.8 6.5 %all-to-all-start.4 = ((bf16[64,8,2048]{2,1,0:T(8,128)(2,1)}), bf16[64,8,2048]{2,1,0:T(8,128)(2,1)S(1)}, u32[]{:S(2)}, u32[]{:S(2)}) async-start(bf16[64,8,2048]{2,1,0:T(8,128)(2,1)} %fusion.14), calls=%async_computation.4 | async-start | bytes 4194304 | tf_op jit(solution)/shard_map/all_to_all | solution.py:83
  173.3 10.9 %reduce-precision_reduce_fusion = bf16[1024,2048]{1,0:T(8,128)(2,1)} fusion(bf16[2,512,1024]{2,1,0:T(8,128)(2,1)} %bitcast.66, bf16[2,512,1024]{2,1,0:T(8,128)(2,1)} %copy-done.9, bf16[2,512,1024]{2,1,0:T(8,128)(2,1)} %copy-done.10), kind=kOutput, calls=%fused_computation | convolution fusion | flops 4309647360 | bytes 10485760 | tf_op jit(solution)/shard_map/srd,srf->sdf/dot_general | solution.py:54
  184.2 0.0 copy-start.1
  184.2 4.8 %fusion.54 = (bf16[1,1024,1024]{2,1,0:T(8,128)(2,1)}, bf16[1,1024,1024]{2,1,0:T(8,128)(2,1)}) fusion(bf16[1,1024,2048]{2,1,0:T(8,128)(2,1)} %bitcast.64), kind=kLoop, calls=%fused_computation.75 | loop fusion | bytes 8388608 | tf_op jit(solution)/shard_map/slice | solution.py:88
  189.0 12.9 %all-to-all-done.4 = bf16[64,8,2048]{2,1,0:T(8,128)(2,1)S(1)} async-done(((bf16[64,8,2048]{2,1,0:T(8,128)(2,1)}), bf16[64,8,2048]{2,1,0:T(8,128)(2,1)S(1)}, u32[]{:S(2)}, u32[]{:S(2)}) %all-to-all-start.4) | async-done | bytes 2097184 | tf_op jit(solution)/shard_map/all_to_all | solution.py:83
  201.8 1.7 convolution_convert_fusion.2
  203.6 0.0 copy-done.1
  (2 shorter events, 0.0 us)
Async XLA Ops:
  0.6 1.3 copy-start
  4.5 47.1 %copy-start.5 = (bf16[256,2]{0,1:T(2,128)(2,1)S(1)}, bf16[256,2]{0,1:T(2,128)(2,1)}, u32[]{:S(2)}) copy-start(bf16[256,2]{0,1:T(2,128)(2,1)} %param.10) | copy-start | bytes 3076
  4.5 47.1 %copy-start.4 = (bf16[256,2048]{1,0:T(8,128)(2,1)S(1)}, bf16[256,2048]{1,0:T(8,128)(2,1)}, u32[]{:S(2)}) copy-start(bf16[256,2048]{1,0:T(8,128)(2,1)} %param.9) | copy-start | bytes 3145732
  45.4 41.7 %copy-start.3 = (bf16[128,8,1024]{2,1,0:T(8,128)(2,1)}, bf16[128,8,1024]{2,1,0:T(8,128)(2,1)S(1)}, u32[]{:S(2)}) copy-start(bf16[128,8,1024]{2,1,0:T(8,128)(2,1)S(1)} %all_to_all.25) | copy-start | bytes 6291460
  45.4 35.6 %all-to-all-start.2 = ((bf16[128,8,1024]{2,1,0:T(8,128)(2,1)}), bf16[128,8,1024]{2,1,0:T(8,128)(2,1)}, u32[]{:S(2)}, u32[]{:S(2)}) async-start(bf16[128,8,1024]{2,1,0:T(8,128)(2,1)} %bitcast.10), calls=%async_computation.2 | async-start | bytes 4194304 | tf_op jit(solution)/shard_map/all_to_all | solution.py:38
  81.0 35.5 %all-to-all-start.1 = ((bf16[128,8,1024]{2,1,0:T(8,128)(2,1)}), bf16[128,8,1024]{2,1,0:T(8,128)(2,1)}, u32[]{:S(2)}, u32[]{:S(2)}) async-start(bf16[128,8,1024]{2,1,0:T(8,128)(2,1)} %bitcast.6), calls=%async_computation.1 | async-start | bytes 4194304 | tf_op jit(solution)/shard_map/all_to_all | solution.py:38
  116.5 34.8 %all-to-all-start = ((bf16[128,8,1024]{2,1,0:T(8,128)(2,1)}), bf16[128,8,1024]{2,1,0:T(8,128)(2,1)S(1)}, u32[]{:S(2)}, u32[]{:S(2)}) async-start(bf16[128,8,1024]{2,1,0:T(8,128)(2,1)} %bitcast.4), calls=%async_computation | async-start | bytes 4194304 | tf_op jit(solution)/shard_map/all_to_all | solution.py:38
  131.4 4.3 %copy-start.2 = (f32[2,512,2048]{2,1,0:T(8,128)}, f32[2,512,2048]{2,1,0:T(8,128)S(1)}, u32[]{:S(2)}) copy-start(f32[2,512,2048]{2,1,0:T(8,128)S(1)} %fusion.9) | copy-start | bytes 25165828
  131.4 5.2 %copy-start.6 = (bf16[1,2048,1024]{2,1,0:T(8,128)(2,1)S(1)}, bf16[1,2048,1024]{2,1,0:T(8,128)(2,1)}, u32[]{:S(2)}) copy-start(bf16[1,2048,1024]{2,1,0:T(8,128)(2,1)} %param.15) | copy-start | bytes 12582916
  151.4 9.6 %copy-start.7 = (bf16[1,2048,1024]{2,1,0:T(8,128)(2,1)S(1)}, bf16[1,2048,1024]{2,1,0:T(8,128)(2,1)}, u32[]{:S(2)}) copy-start(bf16[1,2048,1024]{2,1,0:T(8,128)(2,1)} %param.14) | copy-start | bytes 12582916
  151.4 9.6 %copy-start.8 = (bf16[1,2048,1024]{2,1,0:T(8,128)(2,1)S(1)}, bf16[1,2048,1024]{2,1,0:T(8,128)(2,1)}, u32[]{:S(2)}) copy-start(bf16[1,2048,1024]{2,1,0:T(8,128)(2,1)} %param.13) | copy-start | bytes 12582916
  158.9 1.3 copy-start.9
  158.9 2.0 copy-start.10
  166.8 35.0 %all-to-all-start.4 = ((bf16[64,8,2048]{2,1,0:T(8,128)(2,1)}), bf16[64,8,2048]{2,1,0:T(8,128)(2,1)S(1)}, u32[]{:S(2)}, u32[]{:S(2)}) async-start(bf16[64,8,2048]{2,1,0:T(8,128)(2,1)} %fusion.14), calls=%async_computation.4 | async-start | bytes 4194304 | tf_op jit(solution)/shard_map/all_to_all | solution.py:83
  184.2 19.3 %copy-start.1 = (bf16[256,2048]{1,0:T(8,128)(2,1)S(1)}, bf16[256,2048]{1,0:T(8,128)(2,1)}, u32[]{:S(2)}) copy-start(bf16[256,2048]{1,0:T(8,128)(2,1)} %param.8) | copy-start | bytes 3145732

commit v5 on v2

--- a/solution.py
+++ b/solution.py
@@ -37,11 +37,16 @@
     ).reshape(dp_count, group * slot_count, width)
 
     wg, wu, wd = w_gate[0], w_up[0], w_down[0]
-    gate_pre = jnp.einsum("srd,df->srf", recv_x, wg, preferred_element_type=jnp.float32)
-    up_pre = jnp.einsum("srd,df->srf", recv_x, wu, preferred_element_type=jnp.float32)
+    ff = wg.shape[1]
+    wgu = jnp.concatenate([wg, wu], axis=1)
+    pre = jnp.einsum("srd,df->srf", recv_x, wgu, preferred_element_type=jnp.float32)
+    gate_pre, up_pre = pre[..., :ff], pre[..., ff:]
+    act = (gate_pre * jax.nn.sigmoid(gate_pre) * up_pre).astype(jnp.bfloat16)
+    x_half = lax.dynamic_slice_in_dim(recv_x, me * half, half, axis=2)
+    recv_rg, pre, act, x_half = lax.optimization_barrier((recv_rg, pre, act, x_half))
+    gate_pre, up_pre = pre[..., :ff], pre[..., ff:]
     gate_sig = jax.nn.sigmoid(gate_pre)
     silu_g = gate_pre * gate_sig
-    act = (silu_g * up_pre).astype(jnp.bfloat16)
     act_grad = jnp.einsum("srd,df->srf", recv_rg, wd, preferred_element_type=jnp.float32)
     gate_grad = (act_grad * up_pre * gate_sig * (1.0 + gate_pre * (1.0 - gate_sig))).astype(
         jnp.bfloat16
@@ -56,12 +61,11 @@
         back.reshape(group, slot_count, width), ("seq", "expert"), 0, 0, tiled=True
     ).reshape(rows, width)
 
-    x_half = lax.dynamic_slice_in_dim(recv_x, me * half, half, axis=2)
     rg_half = lax.dynamic_slice_in_dim(recv_rg, me * half, half, axis=2)
 
     def wgrad(left, right):
         per_seq = jnp.einsum("srd,srf->sdf", left, right, preferred_element_type=jnp.float32)
-        per_seq = per_seq.astype(jnp.bfloat16).astype(jnp.float32)
+        per_seq = lax.reduce_precision(per_seq, exponent_bits=8, mantissa_bits=7)
         return per_seq.sum(axis=0).astype(jnp.bfloat16)[None]
 
     grad_gate = wgrad(x_half, gate_grad)

time: 183 us -> 183 us (level)
  local copies, waits for them, and re-layouts: 1.79 us -> 14.5 us
  matrix products: 62.8 us -> 52.2 us
  waiting for transfers between devices: 89.8 us -> 85 us
  other arithmetic: 1.68 us -> 4.45 us
    dot_general x2 -> x1, matrix products: 18.3 us -> 11.6 us  [per_device(): jnp.einsum('srd,df->srf', recv_x, wgu, preferred_element_type=jnp.float32)]
    optimization_barrier x0 -> x1, local copies, waits for them, and re-layouts: none -> 6.22 us  [per_device(): lax.optimization_barrier((recv_rg, pre, act, x_half))]
    dot_general x3, matrix products: 18.6 us -> 14.6 us  [wgrad(): jnp.einsum('srd,srf->sdf', left, right, preferred_element_type=jnp.float32)]
    dynamic_slice x0 -> x1, local copies, waits for them, and re-layouts: none -> 3.25 us  [per_device(): x_half = lax.dynamic_slice_in_dim(recv_x, me * half, half, axis=2)]
    unnamed x22 -> x26, local copies, waits for them, and re-layouts: 1.77 us -> 5 us
    convert_element_type x0 -> x1, other arithmetic: none -> 2.77 us  [per_device(): act = (gate_pre * jax.nn.sigmoid(gate_pre) * up_pre).astype(jnp.bfloat16)]
    all_to_all x1, waiting for transfers between devices: 32.9 us -> 30.3 us  [per_device(): lax.all_to_all(send_rg.reshape(dp_count * group, slot_count, width), axes...]
    all_to_all x1, waiting for transfers between devices: 8.97 us -> 6.72 us  [per_device(): lax.all_to_all(back.reshape(group, slot_count, width), ('seq', 'expert'),...]
  transfers between devices with their start and end apart: 3 -> 3, of which waited for: 3 -> 3; matrix products, arithmetic and copies ran while one was open for 22% -> 23% of each run, Pallas kernels for 0% -> 0%
where the time goes in v5:
time: 183 us
  waiting for transfers between devices  85 us (46%)
  matrix products  52.2 us (29%)
  starting transfers between devices  25.6 us (14%)
  local copies, waits for them, and re-layouts  14.5 us (8%)
  other arithmetic  4.45 us (2%)
    all_to_all x1, waiting for transfers between devices, per_device(): lax.all_to_all(send_x.reshape(dp_count * group, slot_count, width), axes,...  47.9 us
    all_to_all x1, waiting for transfers between devices, per_device(): lax.all_to_all(send_rg.reshape(dp_count * group, slot_count, width), axes...  30.3 us
    dot_general x3, matrix products, wgrad(): jnp.einsum('srd,srf->sdf', left, right, preferred_element_type=jnp.float32)  14.6 us
    all_to_all x1, starting transfers between devices, per_device(): lax.all_to_all(send_x.reshape(dp_count * group, slot_count, width), axes,...  12 us
    dot_general x1, matrix products, per_device(): jnp.einsum('srd,df->srf', recv_x, wgu, preferred_element_type=jnp.float32)  11.6 us
    dot_general x1, matrix products, per_device(): jnp.einsum('srd,df->srf', recv_rg, wd, preferred_element_type=jnp.float32)  11.6 us
    all_to_all x1, starting transfers between devices, per_device(): lax.all_to_all(send_rg.reshape(dp_count * group, slot_count, width), axes...  7.27 us
    all_to_all x1, waiting for transfers between devices, per_device(): lax.all_to_all(back.reshape(group, slot_count, width), ('seq', 'expert'),...  6.72 us
  transfers between devices with their start and end apart: 3, of which 3 were waited for; matrix products, arithmetic and copies ran while one was open for 23% of the time, Pallas kernels for 0%

profile of v5, /device:TPU:1, one launch (start us, length us, event | category | flops | bytes accessed | tf_op | source)
XLA Modules:
  0.0 182.5 jit_solution(11814964828667782956)
XLA Ops:
  0.6 0.0 copy-start
  0.7 0.8 multiply_add_fusion
  1.5 0.4 copy-done
  1.9 3.3 %convert_bitcast_fusion = bf16[128,8,2048]{2,1,0:T(8,128)(2,1)} fusion(bf16[256,2048]{1,0:T(8,128)(2,1)S(1)} %copy-done, s32[256]{0:T(256)S(1)} %bitcast.55, s32[256]{0:T(256)S(1)} %bitcast.52, s32[1024]{0:T(1024)S(1)} %get-tuple-element.18, s32[1024]{0:T(1024)S(1)} %get-tuple-element.19, pred[1024]{0:T(1024)(128)(4,1)S(1)} %fusion.30), kind=kOutput, calls=%fused_computation.15 | convolution fusion | flops 1076887552 | bytes 5254144 | tf_op jit(solution)/shard_map/dot_general | solution.py:27
  5.2 0.0 copy-start.4
  5.2 0.0 copy-start.8
  5.2 12.0 %all-to-all-start.1 = ((bf16[128,8,2048]{2,1,0:T(8,128)(2,1)}), bf16[128,8,2048]{2,1,0:T(8,128)(2,1)}, u32[]{:S(2)}, u32[]{:S(2)}) async-start(bf16[128,8,2048]{2,1,0:T(8,128)(2,1)} %convert_bitcast_fusion), calls=%async_computation.1 | async-start | bytes 8388608 | tf_op jit(solution)/shard_map/all_to_all | solution.py:32
  17.1 0.0 copy-done.4
  17.2 0.0 copy-done.8
  17.2 3.2 %convert_bitcast_fusion.1 = bf16[128,8,2048]{2,1,0:T(8,128)(2,1)} fusion(bf16[256,2048]{1,0:T(8,128)(2,1)S(1)} %copy-done.8, s32[256]{0:T(256)S(1)} %bitcast.56, s32[256]{0:T(256)S(1)} %bitcast.53, s32[1024]{0:T(1024)S(1)} %get-tuple-element.18, s32[1024]{0:T(1024)S(1)} %get-tuple-element.19, pred[1024]{0:T(1024)(128)(4,1)S(1)} %fusion.30, ...), kind=kOutput, calls=%fused_computation.16 | convolution fusion | flops 1077149696 | bytes 5255168 | tf_op jit(solution)/shard_map/dot_general | solution.py:28
  20.4 47.9 %all-to-all-done.1 = bf16[128,8,2048]{2,1,0:T(8,128)(2,1)} async-done(((bf16[128,8,2048]{2,1,0:T(8,128)(2,1)}), bf16[128,8,2048]{2,1,0:T(8,128)(2,1)}, u32[]{:S(2)}, u32[]{:S(2)}) %all-to-all-start.1) | async-done | bytes 4194336 | tf_op jit(solution)/shard_map/all_to_all | solution.py:32
  68.4 7.3 %all-to-all-start = ((bf16[128,8,2048]{2,1,0:T(8,128)(2,1)}), bf16[128,8,2048]{2,1,0:T(8,128)(2,1)}, u32[]{:S(2)}, u32[]{:S(2)}) async-start(bf16[128,8,2048]{2,1,0:T(8,128)(2,1)} %convert_bitcast_fusion.1), calls=%async_computation | async-start | bytes 8388608 | tf_op jit(solution)/shard_map/all_to_all | solution.py:35
  75.6 0.0 copy-start.5
  75.7 3.2 %constant_dynamic-slice_fusion = bf16[2,512,1024]{2,1,0:T(8,128)(2,1)} fusion(bf16[2,512,2048]{2,1,0:T(8,128)(2,1)} %bitcast.5, s32[]{:T(128)S(6)} %select_n.29), kind=kLoop, calls=%fused_computation.54 | loop fusion | bytes 4194308 | tf_op jit(solution)/shard_map/dynamic_slice | solution.py:45
  78.9 0.0 copy-done.5
  78.9 11.6 %fusion = f32[2,512,2048]{2,1,0:T(8,128)S(1)} fusion(bf16[2,512,2048]{2,1,0:T(8,128)(2,1)} %bitcast.5, bf16[2048,1024]{1,0:T(8,128)(2,1)} %bitcast.59, bf16[2048,1024]{1,0:T(8,128)(2,1)S(1)} %bitcast.58), kind=kOutput, calls=%fused_computation.1 | convolution fusion | flops 8606711808 | bytes 20971520 | tf_op jit(solution)/shard_map/srd,df->srf/dot_general | solution.py:42
  90.5 0.0 copy-start.2
  90.5 3.2 %copy-done.2 = f32[2,512,2048]{2,1,0:T(8,128)} copy-done((f32[2,512,2048]{2,1,0:T(8,128)}, f32[2,512,2048]{2,1,0:T(8,128)S(1)}, u32[]{:S(2)}) %copy-start.2) | copy-done | bytes 8388632
  93.8 2.8 %fusion.3 = bf16[2,512,1024]{2,1,0:T(8,128)(2,1)} fusion(f32[2,512,2048]{2,1,0:T(8,128)S(1)} %fusion), kind=kLoop, calls=%fused_computation.8 | loop fusion | flops 6291456 | bytes 10485760 | tf_op jit(solution)/shard_map/convert_element_type | solution.py:44
  96.5 30.3 %all-to-all-done = bf16[128,8,2048]{2,1,0:T(8,128)(2,1)} async-done(((bf16[128,8,2048]{2,1,0:T(8,128)(2,1)}), bf16[128,8,2048]{2,1,0:T(8,128)(2,1)}, u32[]{:S(2)}, u32[]{:S(2)}) %all-to-all-start) | async-done | bytes 4194336 | tf_op jit(solution)/shard_map/all_to_all | solution.py:35
  126.9 0.0 copy-start.6
  126.9 11.6 %multiply_convert_fusion = (bf16[2,512,1024]{2,1,0:T(8,128)(2,1)S(1)}, bf16[2,512,1024]{2,1,0:T(8,128)(2,1)S(1)}) fusion(f32[2,512,2048]{2,1,0:T(8,128)} %copy-done.2, bf16[2,512,2048]{2,1,0:T(8,128)(2,1)} %bitcast.3, bf16[1,2048,1024]{2,1,0:T(8,128)(2,1)} %param.15), kind=kOutput, calls=%fused_computation.12 | convolution fusion | flops 4308598784 | bytes 20971520 | tf_op jit(solution)/shard_map/srd,df->srf/dot_general | solution.py:50
  138.5 0.0 copy-start.9
  138.5 0.0 copy-start.11
  138.5 0.0 copy-done.6
  138.5 0.0 copy-start.7
  138.5 2.4 %fusion.13 = f32[512,2048]{1,0:T(8,128)S(1)} fusion(bf16[2,512,1024]{2,1,0:T(8,128)(2,1)S(1)} %get-tuple-element.15, s32[]{:T(128)S(6)} %select_n.30, bf16[1,2048,1024]{2,1,0:T(8,128)(2,1)S(1)} %copy-done.6), kind=kOutput, calls=%fused_computation.30 | convolution fusion | flops 2147483648 | bytes 9437188 | tf_op jit(solution)/shard_map/dot_general | solution.py:58
  140.9 0.0 copy-done.9
  140.9 0.0 copy-done.11
  140.9 1.3 copy-done.7
  142.2 3.7 %fusion.6 = bf16[64,8,2048]{2,1,0:T(8,128)(2,1)} fusion(f32[512,2048]{1,0:T(8,128)S(1)} %fusion.13, bf16[2,512,1024]{2,1,0:T(8,128)(2,1)S(1)} %get-tuple-element.14, s32[]{:T(128)S(6)} %select_n.30, bf16[1,2048,1024]{2,1,0:T(8,128)(2,1)S(1)} %copy-done.7), kind=kOutput, calls=%fused_computation.17 | convolution fusion | flops 2149580800 | bytes 11534340 | tf_op jit(solution)/shard_map/dot_general | solution.py:59
  145.9 6.4 %all-to-all-start.2 = ((bf16[64,8,2048]{2,1,0:T(8,128)(2,1)}), bf16[64,8,2048]{2,1,0:T(8,128)(2,1)S(1)}, u32[]{:S(2)}, u32[]{:S(2)}) async-start(bf16[64,8,2048]{2,1,0:T(8,128)(2,1)} %fusion.6), calls=%async_computation.2 | async-start | bytes 4194304 | tf_op jit(solution)/shard_map/all_to_all | solution.py:60
  152.3 0.9 fusion.10
  153.2 6.2 %copy.17 = bf16[2,512,2048]{1,2,0:T(8,128)(2,1)} copy(bf16[2,512,2048]{2,1,0:T(8,128)(2,1)} %bitcast.3) | data formatting | bytes 8388608 | tf_op jit(solution)/shard_map/optimization_barrier | solution.py:46
  159.4 0.0 copy-start.3
  159.4 0.0 copy-start.10
  159.4 6.6 %reduce-precision_reduce_fusion = bf16[1024,1024]{1,0:T(8,128)(2,1)} fusion(bf16[2,512,1024]{2,1,0:T(8,128)(2,1)} %fusion.3, bf16[2,512,2048]{1,2,0:T(8,128)(2,1)} %copy.17, s32[]{:T(128)S(6)} %select_n.29), kind=kOutput, calls=%fused_computation.4 | convolution fusion | flops 2150629376 | bytes 6291460 | tf_op jit(solution)/shard_map/srd,srf->sdf/dot_general | solution.py:67
  166.0 0.0 copy-done.3
  166.0 0.0 copy-done.10
  166.0 0.0 copy-start.12
  166.0 4.0 %reduce-precision_reduce_fusion.2 = bf16[1024,1024]{1,0:T(8,128)(2,1)} fusion(bf16[2,512,1024]{2,1,0:T(8,128)(2,1)S(1)} %copy-done.3, bf16[2,512,1024]{2,1,0:T(8,128)(2,1)S(1)} %copy-done.10), kind=kOutput, calls=%fused_computation.6 | convolution fusion | flops 2150629376 | bytes 6291456 | tf_op jit(solution)/shard_map/srd,srf->sdf/dot_general | solution.py:67
  170.1 0.0 copy-done.12
  170.1 0.0 copy-start.1
  170.1 4.0 %reduce-precision_reduce_fusion.1 = bf16[1024,1024]{1,0:T(8,128)(2,1)} fusion(bf16[2,512,1024]{2,1,0:T(8,128)(2,1)S(1)} %copy-done.3, bf16[2,512,1024]{2,1,0:T(8,128)(2,1)S(1)} %copy-done.12), kind=kOutput, calls=%fused_computation.5 | convolution fusion | flops 2150629376 | bytes 6291456 | tf_op jit(solution)/shard_map/srd,srf->sdf/dot_general | solution.py:67
  174.1 6.7 %all-to-all-done.2 = bf16[64,8,2048]{2,1,0:T(8,128)(2,1)S(1)} async-done(((bf16[64,8,2048]{2,1,0:T(8,128)(2,1)}), bf16[64,8,2048]{2,1,0:T(8,128)(2,1)S(1)}, u32[]{:S(2)}, u32[]{:S(2)}) %all-to-all-start.2) | async-done | bytes 2097184 | tf_op jit(solution)/shard_map/all_to_all | solution.py:60
  180.8 1.7 convolution_convert_fusion
  182.5 0.0 copy-done.1
  (4 shorter events, 0.0 us)
Async XLA Ops:
  0.6 1.3 copy-start
  5.2 12.0 %copy-start.4 = (bf16[256,2]{0,1:T(2,128)(2,1)S(1)}, bf16[256,2]{0,1:T(2,128)(2,1)}, u32[]{:S(2)}) copy-start(bf16[256,2]{0,1:T(2,128)(2,1)} %param.10) | copy-start | bytes 3076
  5.2 12.0 %copy-start.8 = (bf16[256,2048]{1,0:T(8,128)(2,1)S(1)}, bf16[256,2048]{1,0:T(8,128)(2,1)}, u32[]{:S(2)}) copy-start(bf16[256,2048]{1,0:T(8,128)(2,1)} %param.9) | copy-start | bytes 3145732
  5.2 63.2 %all-to-all-start.1 = ((bf16[128,8,2048]{2,1,0:T(8,128)(2,1)}), bf16[128,8,2048]{2,1,0:T(8,128)(2,1)}, u32[]{:S(2)}, u32[]{:S(2)}) async-start(bf16[128,8,2048]{2,1,0:T(8,128)(2,1)} %convert_bitcast_fusion), calls=%async_computation.1 | async-start | bytes 8388608 | tf_op jit(solution)/shard_map/all_to_all | solution.py:32
  68.4 58.5 %all-to-all-start = ((bf16[128,8,2048]{2,1,0:T(8,128)(2,1)}), bf16[128,8,2048]{2,1,0:T(8,128)(2,1)}, u32[]{:S(2)}, u32[]{:S(2)}) async-start(bf16[128,8,2048]{2,1,0:T(8,128)(2,1)} %convert_bitcast_fusion.1), calls=%async_computation | async-start | bytes 8388608 | tf_op jit(solution)/shard_map/all_to_all | solution.py:35
  75.6 3.3 %copy-start.5 = (bf16[1,2048,1024]{2,1,0:T(8,128)(2,1)S(1)}, bf16[1,2048,1024]{2,1,0:T(8,128)(2,1)}, u32[]{:S(2)}) copy-start(bf16[1,2048,1024]{2,1,0:T(8,128)(2,1)} %param.13) | copy-start | bytes 12582916
  90.5 3.2 %copy-start.2 = (f32[2,512,2048]{2,1,0:T(8,128)}, f32[2,512,2048]{2,1,0:T(8,128)S(1)}, u32[]{:S(2)}) copy-start(f32[2,512,2048]{2,1,0:T(8,128)S(1)} %fusion) | copy-start | bytes 25165828
  126.9 11.6 %copy-start.6 = (bf16[1,2048,1024]{2,1,0:T(8,128)(2,1)S(1)}, bf16[1,2048,1024]{2,1,0:T(8,128)(2,1)}, u32[]{:S(2)}) copy-start(bf16[1,2048,1024]{2,1,0:T(8,128)(2,1)} %param.13) | copy-start | bytes 12582916
  138.5 2.4 %copy-start.9 = (bf16[2,512,1024]{2,1,0:T(8,128)(2,1)}, bf16[2,512,1024]{2,1,0:T(8,128)(2,1)S(1)}, u32[]{:S(2)}) copy-start(bf16[2,512,1024]{2,1,0:T(8,128)(2,1)S(1)} %get-tuple-element.15) | copy-start | bytes 6291460
  138.5 2.4 %copy-start.11 = (bf16[2,512,1024]{2,1,0:T(8,128)(2,1)}, bf16[2,512,1024]{2,1,0:T(8,128)(2,1)S(1)}, u32[]{:S(2)}) copy-start(bf16[2,512,1024]{2,1,0:T(8,128)(2,1)S(1)} %get-tuple-element.14) | copy-start | bytes 6291460
  138.5 3.7 %copy-start.7 = (bf16[1,2048,1024]{2,1,0:T(8,128)(2,1)S(1)}, bf16[1,2048,1024]{2,1,0:T(8,128)(2,1)}, u32[]{:S(2)}) copy-start(bf16[1,2048,1024]{2,1,0:T(8,128)(2,1)} %param.14) | copy-start | bytes 12582916
  145.9 34.9 %all-to-all-start.2 = ((bf16[64,8,2048]{2,1,0:T(8,128)(2,1)}), bf16[64,8,2048]{2,1,0:T(8,128)(2,1)S(1)}, u32[]{:S(2)}, u32[]{:S(2)}) async-start(bf16[64,8,2048]{2,1,0:T(8,128)(2,1)} %fusion.6), calls=%async_computation.2 | async-start | bytes 4194304 | tf_op jit(solution)/shard_map/all_to_all | solution.py:60
  159.4 6.6 %copy-start.3 = (bf16[2,512,1024]{2,1,0:T(8,128)(2,1)S(1)}, bf16[2,512,1024]{2,1,0:T(8,128)(2,1)}, u32[]{:S(2)}) copy-start(bf16[2,512,1024]{2,1,0:T(8,128)(2,1)} %constant_dynamic-slice_fusion) | copy-start | bytes 6291460
  159.4 6.6 %copy-start.10 = (bf16[2,512,1024]{2,1,0:T(8,128)(2,1)S(1)}, bf16[2,512,1024]{2,1,0:T(8,128)(2,1)}, u32[]{:S(2)}) copy-start(bf16[2,512,1024]{2,1,0:T(8,128)(2,1)} %copy-done.9) | copy-start | bytes 6291460
  166.0 4.0 %copy-start.12 = (bf16[2,512,1024]{2,1,0:T(8,128)(2,1)S(1)}, bf16[2,512,1024]{2,1,0:T(8,128)(2,1)}, u32[]{:S(2)}) copy-start(bf16[2,512,1024]{2,1,0:T(8,128)(2,1)} %copy-done.11) | copy-start | bytes 6291460
  170.1 12.5 %copy-start.1 = (bf16[256,2048]{1,0:T(8,128)(2,1)S(1)}, bf16[256,2048]{1,0:T(8,128)(2,1)}, u32[]{:S(2)}) copy-start(bf16[256,2048]{1,0:T(8,128)(2,1)} %param.8) | copy-start | bytes 3145732

commit v6 on v5

--- a/solution.py
+++ b/solution.py
@@ -44,33 +44,45 @@
     act = (gate_pre * jax.nn.sigmoid(gate_pre) * up_pre).astype(jnp.bfloat16)
     x_half = lax.dynamic_slice_in_dim(recv_x, me * half, half, axis=2)
     recv_rg, pre, act, x_half = lax.optimization_barrier((recv_rg, pre, act, x_half))
-    gate_pre, up_pre = pre[..., :ff], pre[..., ff:]
-    gate_sig = jax.nn.sigmoid(gate_pre)
-    silu_g = gate_pre * gate_sig
-    act_grad = jnp.einsum("srd,df->srf", recv_rg, wd, preferred_element_type=jnp.float32)
-    gate_grad = (act_grad * up_pre * gate_sig * (1.0 + gate_pre * (1.0 - gate_sig))).astype(
-        jnp.bfloat16
-    )
-    up_grad = (act_grad * silu_g).astype(jnp.bfloat16)
+    def gradients(pre_s, rg_s):
+        gate_pre, up_pre = pre_s[..., :ff], pre_s[..., ff:]
+        gate_sig = jax.nn.sigmoid(gate_pre)
+        silu_g = gate_pre * gate_sig
+        act_grad = jnp.dot(rg_s, wd, preferred_element_type=jnp.float32)
+        gate_grad = (act_grad * up_pre * gate_sig * (1.0 + gate_pre * (1.0 - gate_sig))).astype(
+            jnp.bfloat16
+        )
+        up_grad = (act_grad * silu_g).astype(jnp.bfloat16)
+        return gate_grad, up_grad
 
-    gg_own = lax.dynamic_index_in_dim(gate_grad, me, 0, keepdims=False)
-    ug_own = lax.dynamic_index_in_dim(up_grad, me, 0, keepdims=False)
+    pick_seq = lambda a, i: lax.dynamic_index_in_dim(a, i, 0, keepdims=False)
+    gg_own, ug_own = gradients(pick_seq(pre, me), pick_seq(recv_rg, me))
     back = jnp.dot(gg_own, wg.T, preferred_element_type=jnp.float32)
     back = (back + jnp.dot(ug_own, wu.T, preferred_element_type=jnp.float32)).astype(jnp.bfloat16)
     returned = lax.all_to_all(
         back.reshape(group, slot_count, width), ("seq", "expert"), 0, 0, tiled=True
     ).reshape(rows, width)
+    recv_rg, pre, act, x_half, gg_own, ug_own, _ = lax.optimization_barrier(
+        (recv_rg, pre, act, x_half, gg_own, ug_own, back)
+    )
+    gg_oth, ug_oth = gradients(pick_seq(pre, 1 - me), pick_seq(recv_rg, 1 - me))
 
     rg_half = lax.dynamic_slice_in_dim(recv_rg, me * half, half, axis=2)
+    x_own, x_oth = pick_seq(x_half, me), pick_seq(x_half, 1 - me)
+    rg_own, rg_oth = pick_seq(rg_half, me), pick_seq(rg_half, 1 - me)
+    act_own, act_oth = pick_seq(act, me), pick_seq(act, 1 - me)
 
-    def wgrad(left, right):
-        per_seq = jnp.einsum("srd,srf->sdf", left, right, preferred_element_type=jnp.float32)
-        per_seq = lax.reduce_precision(per_seq, exponent_bits=8, mantissa_bits=7)
-        return per_seq.sum(axis=0).astype(jnp.bfloat16)[None]
+    def wgrad(pairs):
+        total = None
+        for left, right in pairs:
+            part = jnp.dot(left.T, right, preferred_element_type=jnp.float32)
+            part = lax.reduce_precision(part, exponent_bits=8, mantissa_bits=7)
+            total = part if total is None else total + part
+        return total.astype(jnp.bfloat16)[None]
 
-    grad_gate = wgrad(x_half, gate_grad)
-    grad_up = wgrad(x_half, up_grad)
-    grad_down = wgrad(rg_half, act)
+    grad_gate = wgrad(((x_own, gg_own), (x_oth, gg_oth)))
+    grad_up = wgrad(((x_own, ug_own), (x_oth, ug_oth)))
+    grad_down = wgrad(((rg_own, act_own), (rg_oth, act_oth)))
 
     grad_tokens = jnp.dot(
         pick[:rows].T, returned, preferred_element_type=jnp.float32

time: 183 us -> 192 us (1.049)
  waiting for transfers between devices: 85 us -> 91.1 us
  matrix products: 52.2 us -> 56.9 us
    all_to_all x1, waiting for transfers between devices: 6.72 us -> 13.5 us  [per_device(): lax.all_to_all(back.reshape(group, slot_count, width), ('seq', 'expert'),...]
    optimization_barrier x1 -> x0, local copies, waits for them, and re-layouts: 6.22 us -> none  [per_device(): lax.optimization_barrier((recv_rg, pre, act, x_half))]
    squeeze x0 -> x2, local copies, waits for them, and re-layouts: none -> 5.09 us  [per_device(): pick_seq = lambda a, i: lax.dynamic_index_in_dim(a, i, 0, keepdims=False)]
    dot_general x4 -> x8, matrix products: 26.2 us -> 30.1 us  [the longest x6 20.1 us: wgrad(): part = jnp.dot(left.T, right, preferred_element_type=jnp.float32)]
    unnamed x26 -> x36, local copies, waits for them, and re-layouts: 5 us -> 5.64 us
  transfers between devices with their start and end apart: 3 -> 3, of which waited for: 3 -> 3; matrix products, arithmetic and copies ran while one was open for 23% -> 18% of each run, Pallas kernels for 0% -> 0%
where the time goes in v6:
time: 192 us
  waiting for transfers between devices  91.1 us (47%)
  matrix products  56.9 us (30%)
  starting transfers between devices  25.8 us (13%)
  local copies, waits for them, and re-layouts  12.9 us (7%)
  other arithmetic  4.43 us (2%)
    all_to_all x1, waiting for transfers between devices, per_device(): lax.all_to_all(send_x.reshape(dp_count * group, slot_count, width), axes,...  47.9 us
    all_to_all x1, waiting for transfers between devices, per_device(): lax.all_to_all(send_rg.reshape(dp_count * group, slot_count, width), axes...  29.8 us
    dot_general x6, matrix products, wgrad(): part = jnp.dot(left.T, right, preferred_element_type=jnp.float32)  20.1 us
    all_to_all x1, waiting for transfers between devices, per_device(): lax.all_to_all(back.reshape(group, slot_count, width), ('seq', 'expert'),...  13.5 us
    dot_general x1, matrix products, per_device(): jnp.einsum('srd,df->srf', recv_x, wgu, preferred_element_type=jnp.float32)  12.4 us
    all_to_all x1, starting transfers between devices, per_device(): lax.all_to_all(send_x.reshape(dp_count * group, slot_count, width), axes,...  12 us
    dot_general x2, matrix products, gradients(): act_grad = jnp.dot(rg_s, wd, preferred_element_type=jnp.float32)  9.95 us
    all_to_all x1, starting transfers between devices, per_device(): lax.all_to_all(send_rg.reshape(dp_count * group, slot_count, width), axes...  7.27 us
  transfers between devices with their start and end apart: 3, of which 3 were waited for; matrix products, arithmetic and copies ran while one was open for 18% of the time, Pallas kernels for 0%

profile of v6, /device:TPU:1, one launch (start us, length us, event | category | flops | bytes accessed | tf_op | source)
XLA Modules:
  0.0 192.1 jit_solution(4330211596584244139)
XLA Ops:
  0.6 0.0 copy-start
  0.7 0.8 multiply_add_fusion
  1.5 0.4 copy-done
  1.9 3.3 %convert_bitcast_fusion = bf16[128,8,2048]{2,1,0:T(8,128)(2,1)} fusion(bf16[256,2048]{1,0:T(8,128)(2,1)S(1)} %copy-done, s32[256]{0:T(256)S(1)} %bitcast.81, s32[256]{0:T(256)S(1)} %bitcast.78, s32[1024]{0:T(1024)S(1)} %get-tuple-element.30, s32[1024]{0:T(1024)S(1)} %get-tuple-element.31, pred[1024]{0:T(1024)(128)(4,1)S(1)} %fusion.60), kind=kOutput, calls=%fused_computation.16 | convolution fusion | flops 1076887552 | bytes 5254144 | tf_op jit(solution)/shard_map/dot_general | solution.py:27
  5.2 12.0 %all-to-all-start.1 = ((bf16[128,8,2048]{2,1,0:T(8,128)(2,1)}), bf16[128,8,2048]{2,1,0:T(8,128)(2,1)}, u32[]{:S(2)}, u32[]{:S(2)}) async-start(bf16[128,8,2048]{2,1,0:T(8,128)(2,1)} %convert_bitcast_fusion), calls=%async_computation.1 | async-start | bytes 8388608 | tf_op jit(solution)/shard_map/all_to_all | solution.py:32
  17.2 0.0 copy-done.7
  17.2 0.0 copy-done.12
  17.2 3.3 %convert_bitcast_fusion.1 = bf16[128,8,2048]{2,1,0:T(8,128)(2,1)} fusion(bf16[256,2048]{1,0:T(8,128)(2,1)S(1)} %copy-done.12, s32[256]{0:T(256)S(1)} %bitcast.82, s32[256]{0:T(256)S(1)} %bitcast.79, s32[1024]{0:T(1024)S(1)} %get-tuple-element.30, s32[1024]{0:T(1024)S(1)} %get-tuple-element.31, pred[1024]{0:T(1024)(128)(4,1)S(1)} %fusion.60, ...), kind=kOutput, calls=%fused_computation.17 | convolution fusion | flops 1077149696 | bytes 5255168 | tf_op jit(solution)/shard_map/dot_general | solution.py:28
  20.5 47.9 %all-to-all-done.1 = bf16[128,8,2048]{2,1,0:T(8,128)(2,1)} async-done(((bf16[128,8,2048]{2,1,0:T(8,128)(2,1)}), bf16[128,8,2048]{2,1,0:T(8,128)(2,1)}, u32[]{:S(2)}, u32[]{:S(2)}) %all-to-all-start.1) | async-done | bytes 4194336 | tf_op jit(solution)/shard_map/all_to_all | solution.py:32
  68.4 7.3 %all-to-all-start = ((bf16[128,8,2048]{2,1,0:T(8,128)(2,1)}), bf16[128,8,2048]{2,1,0:T(8,128)(2,1)}, u32[]{:S(2)}, u32[]{:S(2)}) async-start(bf16[128,8,2048]{2,1,0:T(8,128)(2,1)} %convert_bitcast_fusion.1), calls=%async_computation | async-start | bytes 8388608 | tf_op jit(solution)/shard_map/all_to_all | solution.py:35
  75.7 0.0 copy-start.8
  75.7 0.9 fusion.23
  76.6 2.1 %constant_dynamic-slice_fusion = bf16[2,512,1024]{2,1,0:T(8,128)(2,1)S(1)} fusion(bf16[2,512,2048]{2,1,0:T(8,128)(2,1)} %bitcast.5, s32[]{:T(128)S(6)} %select_n.47), kind=kLoop, calls=%fused_computation.87 | loop fusion | bytes 4194308 | tf_op jit(solution)/shard_map/dynamic_slice | solution.py:45
  78.7 0.0 copy-start.5
  78.7 0.0 copy-done.8
  78.7 12.4 %fusion = f32[2,512,2048]{2,1,0:T(8,128)S(1)} fusion(bf16[2,512,2048]{2,1,0:T(8,128)(2,1)} %bitcast.5, bf16[2048,1024]{1,0:T(8,128)(2,1)} %bitcast.85, bf16[2048,1024]{1,0:T(8,128)(2,1)S(1)} %bitcast.84), kind=kOutput, calls=%fused_computation.1 | convolution fusion | flops 8606711808 | bytes 20971520 | tf_op jit(solution)/shard_map/srd,df->srf/dot_general | solution.py:42
  91.1 0.0 copy-start.2
  91.1 3.2 %copy-done.2 = f32[2,512,2048]{2,1,0:T(8,128)} copy-done((f32[2,512,2048]{2,1,0:T(8,128)}, f32[2,512,2048]{2,1,0:T(8,128)S(1)}, u32[]{:S(2)}) %copy-start.2) | copy-done | bytes 8388632
  94.4 2.7 %fusion.3 = bf16[2,512,1024]{2,1,0:T(8,128)(2,1)} fusion(f32[2,512,2048]{2,1,0:T(8,128)S(1)} %fusion), kind=kLoop, calls=%fused_computation.5 | loop fusion | flops 6291456 | bytes 10485760 | tf_op jit(solution)/shard_map/convert_element_type | solution.py:44
  97.1 29.8 %all-to-all-done = bf16[128,8,2048]{2,1,0:T(8,128)(2,1)} async-done(((bf16[128,8,2048]{2,1,0:T(8,128)(2,1)}), bf16[128,8,2048]{2,1,0:T(8,128)(2,1)}, u32[]{:S(2)}, u32[]{:S(2)}) %all-to-all-start) | async-done | bytes 4194336 | tf_op jit(solution)/shard_map/all_to_all | solution.py:35
  126.9 2.8 %dynamic-slice_bitcast_fusion.1 = f32[512,2048]{1,0:T(8,128)S(1)} fusion(f32[2,512,2048]{2,1,0:T(8,128)} %copy-done.2, s32[]{:T(128)S(6)} %select_n.48), kind=kLoop, calls=%fused_computation.15 | loop fusion | bytes 8388612 | tf_op jit(solution)/shard_map/jit(dynamic_index_in_dim)/squeeze | solution.py:58
  129.7 0.6 copy-done.11
  130.3 4.7 %multiply_convert_fusion.1 = (bf16[512,1024]{1,0:T(8,128)(2,1)S(1)}, bf16[512,1024]{1,0:T(8,128)(2,1)S(1)}) fusion(f32[512,2048]{1,0:T(8,128)S(1)} %dynamic-slice_bitcast_fusion.1, bf16[1,2048,1024]{2,1,0:T(8,128)(2,1)S(1)} %copy-done.11, bf16[2,512,2048]{2,1,0:T(8,128)(2,1)} %bitcast.3, s32[]{:T(128)S(6)} %select_n.48), kind=kOutput, calls=%fused_computation.33 | convolution fusion | flops 2154299392 | bytes 12582916 | tf_op jit(solution)/shard_map/dot_general | solution.py:51
  135.0 0.0 copy-done.9
  135.0 0.0 copy-start.10
  135.0 0.0 slice-start
  135.0 2.4 %fusion.71 = f32[512,2048]{1,0:T(8,128)S(1)} fusion(bf16[512,1024]{1,0:T(8,128)(2,1)S(1)} %get-tuple-element.19, bf16[1,2048,1024]{2,1,0:T(8,128)(2,1)S(1)} %copy-done.9), kind=kOutput, calls=%fused_computation.93 | convolution fusion | flops 2147483648 | bytes 9437184 | tf_op jit(solution)/shard_map/dot_general | solution.py:60
  137.4 0.0 copy-done.10
  137.4 0.0 slice-start.1
  137.4 3.7 %add_convert_fusion.3 = bf16[512,2048]{1,0:T(8,128)(2,1)} fusion(f32[512,2048]{1,0:T(8,128)S(1)} %fusion.71, bf16[512,1024]{1,0:T(8,128)(2,1)S(1)} %get-tuple-element.22, bf16[1,2048,1024]{2,1,0:T(8,128)(2,1)S(1)} %copy-done.10), kind=kOutput, calls=%fused_computation.14 | convolution fusion | flops 2149580800 | bytes 11534336 | tf_op jit(solution)/shard_map/dot_general | solution.py:61
  141.2 2.3 %dynamic-slice_bitcast_fusion = f32[512,2048]{1,0:T(8,128)} fusion(f32[2,512,2048]{2,1,0:T(8,128)S(1)} %bitcast.76, s32[]{:T(128)S(6)} %select_n.49), kind=kLoop, calls=%fused_computation.13 | loop fusion | bytes 8388612 | tf_op jit(solution)/shard_map/jit(dynamic_index_in_dim)/squeeze | solution.py:58
  143.4 5.3 %fusion.4 = f32[512,1024]{1,0:T(8,128)} fusion(bf16[1,2048,1024]{2,1,0:T(8,128)(2,1)S(1)} %copy-done.11, bf16[2,512,2048]{2,1,0:T(8,128)(2,1)} %bitcast.3, s32[]{:T(128)S(6)} %select_n.49), kind=kOutput, calls=%fused_computation.6 | convolution fusion | flops 2147483648 | bytes 8388612 | tf_op jit(solution)/shard_map/dot_general | solution.py:51
  148.7 3.2 %fusion.33 = f32[1024,1024]{1,0:T(8,128)} fusion(bf16[512,1024]{1,0:T(8,128)(2,1)S(1)} %get-tuple-element.22, bf16[2,512,1024]{2,1,0:T(8,128)(2,1)S(1)} %constant_dynamic-slice_fusion, s32[]{:T(128)S(6)} %select_n.48), kind=kOutput, calls=%fused_computation.51 | convolution fusion | flops 1073741824 | bytes 6291460 | tf_op jit(solution)/shard_map/dot_general | solution.py:78
  152.0 3.2 %fusion.35 = f32[1024,1024]{1,0:T(8,128)} fusion(bf16[512,1024]{1,0:T(8,128)(2,1)S(1)} %get-tuple-element.19, bf16[2,512,1024]{2,1,0:T(8,128)(2,1)S(1)} %constant_dynamic-slice_fusion, s32[]{:T(128)S(6)} %select_n.48), kind=kOutput, calls=%fused_computation.53 | convolution fusion | flops 1073741824 | bytes 6291460 | tf_op jit(solution)/shard_map/dot_general | solution.py:78
  155.2 6.6 %all-to-all-start.2 = ((bf16[64,8,2048]{2,1,0:T(8,128)(2,1)}), bf16[64,8,2048]{2,1,0:T(8,128)(2,1)S(1)}, u32[]{:S(2)}, u32[]{:S(2)}) async-start(bf16[64,8,2048]{2,1,0:T(8,128)(2,1)} %bitcast.77), calls=%async_computation.2 | async-start | bytes 4194304 | tf_op jit(solution)/shard_map/all_to_all | solution.py:62
  161.8 0.0 copy-start.3
  161.9 3.3 %fusion.28 = f32[1024,1024]{1,0:T(8,128)S(1)} fusion(bf16[2,512,1024]{2,1,0:T(8,128)(2,1)} %fusion.3, s32[]{:T(128)S(6)} %select_n.48, bf16[2,512,2048]{2,1,0:T(8,128)(2,1)} %bitcast.3, s32[]{:T(128)S(6)} %select_n.50, s32[]{:T(128)S(6)} %select_n.51), kind=kOutput, calls=%fused_computation.46 | convolution fusion | flops 1073741824 | bytes 6291468 | tf_op jit(solution)/shard_map/dot_general | solution.py:78
  165.2 0.0 copy-start.6
  165.2 0.0 copy-start.14
  165.2 0.0 copy-start.15
  165.2 4.5 %fusion.21 = bf16[1,1024,1024]{2,1,0:T(8,128)(2,1)} fusion(f32[1024,1024]{1,0:T(8,128)S(1)} %fusion.28, bf16[2,512,1024]{2,1,0:T(8,128)(2,1)S(1)} %copy-done.3, s32[]{:T(128)S(6)} %select_n.49, bf16[2,512,2048]{2,1,0:T(8,128)(2,1)} %bitcast.3, s32[]{:T(128)S(6)} %select_n.52, s32[]{:T(128)S(6)} %select_n.51), kind=kOutput, calls=%fused_computation.38 | convolution fusion | flops 1077936128 | bytes 8388620 | tf_op jit(solution)/shard_map/dot_general | solution.py:78
  169.7 0.4 copy-done.14
  170.1 0.8 copy-done.15
  171.0 2.9 %fusion.20 = bf16[1,1024,1024]{2,1,0:T(8,128)(2,1)} fusion(f32[1024,1024]{1,0:T(8,128)S(1)} %copy-done.14, f32[512,1024]{1,0:T(8,128)S(1)} %copy-done.15, f32[512,2048]{1,0:T(8,128)S(1)} %copy-done.4, bf16[2,512,1024]{2,1,0:T(8,128)(2,1)S(1)} %copy-done.6, s32[]{:T(128)S(6)} %select_n.49), kind=kOutput, calls=%fused_computation.37 | convolution fusion | flops 1081081856 | bytes 11534340 | tf_op jit(solution)/shard_map/dot_general | solution.py:78
  173.8 3.0 %fusion.19 = bf16[1,1024,1024]{2,1,0:T(8,128)(2,1)} fusion(f32[1024,1024]{1,0:T(8,128)S(1)} %copy-done.13, f32[512,1024]{1,0:T(8,128)S(1)} %copy-done.15, f32[512,2048]{1,0:T(8,128)S(1)} %copy-done.4, bf16[2,512,1024]{2,1,0:T(8,128)(2,1)S(1)} %copy-done.6, s32[]{:T(128)S(6)} %select_n.49), kind=kOutput, calls=%fused_computation.36 | convolution fusion | flops 1083179008 | bytes 13631492 | tf_op jit(solution)/shard_map/dot_general | solution.py:78
  176.8 13.5 %all-to-all-done.2 = bf16[64,8,2048]{2,1,0:T(8,128)(2,1)S(1)} async-done(((bf16[64,8,2048]{2,1,0:T(8,128)(2,1)}), bf16[64,8,2048]{2,1,0:T(8,128)(2,1)S(1)}, u32[]{:S(2)}, u32[]{:S(2)}) %all-to-all-start.2) | async-done | bytes 2097184 | tf_op jit(solution)/shard_map/all_to_all | solution.py:62
  190.3 1.7 convolution_convert_fusion
  192.0 0.0 copy-done.1
  (19 shorter events, 0.1 us)
Async XLA Ops:
  0.6 1.3 copy-start
  5.2 12.0 %copy-start.7 = (bf16[256,2]{0,1:T(2,128)(2,1)S(1)}, bf16[256,2]{0,1:T(2,128)(2,1)}, u32[]{:S(2)}) copy-start(bf16[256,2]{0,1:T(2,128)(2,1)} %param.10) | copy-start | bytes 3076
  5.2 12.0 %copy-start.12 = (bf16[256,2048]{1,0:T(8,128)(2,1)S(1)}, bf16[256,2048]{1,0:T(8,128)(2,1)}, u32[]{:S(2)}) copy-start(bf16[256,2048]{1,0:T(8,128)(2,1)} %param.9) | copy-start | bytes 3145732
  5.2 63.2 %all-to-all-start.1 = ((bf16[128,8,2048]{2,1,0:T(8,128)(2,1)}), bf16[128,8,2048]{2,1,0:T(8,128)(2,1)}, u32[]{:S(2)}, u32[]{:S(2)}) async-start(bf16[128,8,2048]{2,1,0:T(8,128)(2,1)} %convert_bitcast_fusion), calls=%async_computation.1 | async-start | bytes 8388608 | tf_op jit(solution)/shard_map/all_to_all | solution.py:32
  68.4 58.5 %all-to-all-start = ((bf16[128,8,2048]{2,1,0:T(8,128)(2,1)}), bf16[128,8,2048]{2,1,0:T(8,128)(2,1)}, u32[]{:S(2)}, u32[]{:S(2)}) async-start(bf16[128,8,2048]{2,1,0:T(8,128)(2,1)} %convert_bitcast_fusion.1), calls=%async_computation | async-start | bytes 8388608 | tf_op jit(solution)/shard_map/all_to_all | solution.py:35
  75.7 3.0 %copy-start.8 = (bf16[1,2048,1024]{2,1,0:T(8,128)(2,1)S(1)}, bf16[1,2048,1024]{2,1,0:T(8,128)(2,1)}, u32[]{:S(2)}) copy-start(bf16[1,2048,1024]{2,1,0:T(8,128)(2,1)} %param.13) | copy-start | bytes 12582916
  78.7 73.3 %copy-start.5 = (bf16[2,512,1024]{2,1,0:T(8,128)(2,1)}, bf16[2,512,1024]{2,1,0:T(8,128)(2,1)S(1)}, u32[]{:S(2)}) copy-start(bf16[2,512,1024]{2,1,0:T(8,128)(2,1)S(1)} %constant_dynamic-slice_fusion) | copy-start | bytes 6291460
  91.1 3.2 %copy-start.2 = (f32[2,512,2048]{2,1,0:T(8,128)}, f32[2,512,2048]{2,1,0:T(8,128)S(1)}, u32[]{:S(2)}) copy-start(f32[2,512,2048]{2,1,0:T(8,128)S(1)} %fusion) | copy-start | bytes 25165828
  126.9 3.4 %copy-start.11 = (bf16[1,2048,1024]{2,1,0:T(8,128)(2,1)S(1)}, bf16[1,2048,1024]{2,1,0:T(8,128)(2,1)}, u32[]{:S(2)}) copy-start(bf16[1,2048,1024]{2,1,0:T(8,128)(2,1)} %param.15) | copy-start | bytes 12582916
  130.3 4.7 %copy-start.9 = (bf16[1,2048,1024]{2,1,0:T(8,128)(2,1)S(1)}, bf16[1,2048,1024]{2,1,0:T(8,128)(2,1)}, u32[]{:S(2)}) copy-start(bf16[1,2048,1024]{2,1,0:T(8,128)(2,1)} %param.13) | copy-start | bytes 12582916
  135.0 2.4 %copy-start.10 = (bf16[1,2048,1024]{2,1,0:T(8,128)(2,1)S(1)}, bf16[1,2048,1024]{2,1,0:T(8,128)(2,1)}, u32[]{:S(2)}) copy-start(bf16[1,2048,1024]{2,1,0:T(8,128)(2,1)} %param.14) | copy-start | bytes 12582916
  135.0 6.1 %slice-start = ((s8[8388608]{0:T(1024)(128)(4,1)}), s8[4194304]{0:T(1024)(128)(4,1)S(1)}, s32[]{:S(2)}) async-start(s8[8388608]{0:T(1024)(128)(4,1)} %bitcast.75), calls=%async_computation.3 | async-start | bytes 8388608
  137.4 3.7 %slice-start.1 = ((s8[8388608]{0:T(1024)(128)(4,1)}), s8[4194304]{0:T(1024)(128)(4,1)S(1)}, s32[]{:S(2)}) async-start(s8[8388608]{0:T(1024)(128)(4,1)} %bitcast.75), calls=%async_computation.4 | async-start | bytes 8388608
  155.2 35.1 %all-to-all-start.2 = ((bf16[64,8,2048]{2,1,0:T(8,128)(2,1)}), bf16[64,8,2048]{2,1,0:T(8,128)(2,1)S(1)}, u32[]{:S(2)}, u32[]{:S(2)}) async-start(bf16[64,8,2048]{2,1,0:T(8,128)(2,1)} %bitcast.77), calls=%async_computation.2 | async-start | bytes 4194304 | tf_op jit(solution)/shard_map/all_to_all | solution.py:62
  161.8 3.3 %copy-start.3 = (bf16[2,512,1024]{2,1,0:T(8,128)(2,1)S(1)}, bf16[2,512,1024]{2,1,0:T(8,128)(2,1)}, u32[]{:S(2)}) copy-start(bf16[2,512,1024]{2,1,0:T(8,128)(2,1)} %fusion.3) | copy-start | bytes 6291460
  165.2 4.5 %copy-start.4 = (f32[512,2048]{1,0:T(8,128)S(1)}, f32[512,2048]{1,0:T(8,128)}, u32[]{:S(2)}) copy-start(f32[512,2048]{1,0:T(8,128)} %dynamic-slice_bitcast_fusion) | copy-start | bytes 12582916
  165.2 4.5 %copy-start.6 = (bf16[2,512,1024]{2,1,0:T(8,128)(2,1)S(1)}, bf16[2,512,1024]{2,1,0:T(8,128)(2,1)}, u32[]{:S(2)}) copy-start(bf16[2,512,1024]{2,1,0:T(8,128)(2,1)} %copy-done.5) | copy-start | bytes 6291460
  165.2 4.9 %copy-start.14 = (f32[1024,1024]{1,0:T(8,128)S(1)}, f32[1024,1024]{1,0:T(8,128)}, u32[]{:S(2)}) copy-start(f32[1024,1024]{1,0:T(8,128)} %fusion.33) | copy-start | bytes 12582916
  165.2 5.8 %copy-start.15 = (f32[512,1024]{1,0:T(8,128)S(1)}, f32[512,1024]{1,0:T(8,128)}, u32[]{:S(2)}) copy-start(f32[512,1024]{1,0:T(8,128)} %fusion.4) | copy-start | bytes 6291460
  170.9 2.9 %copy-start.13 = (f32[1024,1024]{1,0:T(8,128)S(1)}, f32[1024,1024]{1,0:T(8,128)}, u32[]{:S(2)}) copy-start(f32[1024,1024]{1,0:T(8,128)} %fusion.35) | copy-start | bytes 12582916
  173.8 18.2 %copy-start.1 = (bf16[256,2048]{1,0:T(8,128)(2,1)S(1)}, bf16[256,2048]{1,0:T(8,128)(2,1)}, u32[]{:S(2)}) copy-start(bf16[256,2048]{1,0:T(8,128)(2,1)} %param.8) | copy-start | bytes 3145732

commit v7 on v5

--- a/solution.py
+++ b/solution.py
@@ -41,16 +41,16 @@
     wgu = jnp.concatenate([wg, wu], axis=1)
     pre = jnp.einsum("srd,df->srf", recv_x, wgu, preferred_element_type=jnp.float32)
     gate_pre, up_pre = pre[..., :ff], pre[..., ff:]
-    act = (gate_pre * jax.nn.sigmoid(gate_pre) * up_pre).astype(jnp.bfloat16)
-    x_half = lax.dynamic_slice_in_dim(recv_x, me * half, half, axis=2)
-    recv_rg, pre, act, x_half = lax.optimization_barrier((recv_rg, pre, act, x_half))
-    gate_pre, up_pre = pre[..., :ff], pre[..., ff:]
     gate_sig = jax.nn.sigmoid(gate_pre)
     silu_g = gate_pre * gate_sig
+    act = (silu_g * up_pre).astype(jnp.bfloat16)
+    gate_fac = up_pre * gate_sig * (1.0 + gate_pre * (1.0 - gate_sig))
+    x_half = lax.dynamic_slice_in_dim(recv_x, me * half, half, axis=2)
+    recv_rg, gate_fac, silu_g, act, x_half = lax.optimization_barrier(
+        (recv_rg, gate_fac, silu_g, act, x_half)
+    )
     act_grad = jnp.einsum("srd,df->srf", recv_rg, wd, preferred_element_type=jnp.float32)
-    gate_grad = (act_grad * up_pre * gate_sig * (1.0 + gate_pre * (1.0 - gate_sig))).astype(
-        jnp.bfloat16
-    )
+    gate_grad = (act_grad * gate_fac).astype(jnp.bfloat16)
     up_grad = (act_grad * silu_g).astype(jnp.bfloat16)
 
     gg_own = lax.dynamic_index_in_dim(gate_grad, me, 0, keepdims=False)

time: 183 us -> 182 us (level)
  local copies, waits for them, and re-layouts: 14.5 us -> 11.3 us
  other arithmetic: 4.45 us -> 6.66 us
    unnamed x26 -> x24, local copies, waits for them, and re-layouts: 5 us -> 1.77 us
    convert_element_type x1, other arithmetic: 2.77 us -> 4.98 us  [per_device(): act = (silu_g * up_pre).astype(jnp.bfloat16)]
  transfers between devices with their start and end apart: 3 -> 3, of which waited for: 3 -> 3; matrix products, arithmetic and copies ran while one was open for 23% -> 25% of each run, Pallas kernels for 0% -> 0%
where the time goes in v7:
time: 182 us; the launch traced here: 181 us
  waiting for transfers between devices  86.1 us (47%)
  matrix products  50.9 us (28%)
  starting transfers between devices  25.6 us (14%)
  local copies, waits for them, and re-layouts  11.3 us (6%)
  other arithmetic  6.66 us (4%)
    all_to_all x1, waiting for transfers between devices, per_device(): lax.all_to_all(send_x.reshape(dp_count * group, slot_count, width), axes,...  47.9 us
    all_to_all x1, waiting for transfers between devices, per_device(): lax.all_to_all(send_rg.reshape(dp_count * group, slot_count, width), axes...  31.5 us
    dot_general x3, matrix products, wgrad(): jnp.einsum('srd,srf->sdf', left, right, preferred_element_type=jnp.float32)  14.6 us
    all_to_all x1, starting transfers between devices, per_device(): lax.all_to_all(send_x.reshape(dp_count * group, slot_count, width), axes,...  12 us
    dot_general x1, matrix products, per_device(): jnp.einsum('srd,df->srf', recv_x, wgu, preferred_element_type=jnp.float32)  11.4 us
    dot_general x1, matrix products, per_device(): jnp.einsum('srd,df->srf', recv_rg, wd, preferred_element_type=jnp.float32)  10.5 us
    all_to_all x1, starting transfers between devices, per_device(): lax.all_to_all(send_rg.reshape(dp_count * group, slot_count, width), axes...  7.27 us
    all_to_all x1, waiting for transfers between devices, per_device(): lax.all_to_all(back.reshape(group, slot_count, width), ('seq', 'expert'),...  6.66 us
  transfers between devices with their start and end apart: 3, of which 3 were waited for; matrix products, arithmetic and copies ran while one was open for 25% of the time, Pallas kernels for 0%

profile of v7, /device:TPU:1, one launch (start us, length us, event | category | flops | bytes accessed | tf_op | source)
XLA Modules:
  0.0 181.3 jit_solution(8039606231276786379)
XLA Ops:
  0.6 0.0 copy-start
  0.7 0.8 multiply_add_fusion
  1.5 0.4 copy-done
  1.9 3.2 %convert_bitcast_fusion = bf16[128,8,2048]{2,1,0:T(8,128)(2,1)} fusion(bf16[256,2048]{1,0:T(8,128)(2,1)S(1)} %copy-done, s32[256]{0:T(256)S(1)} %bitcast.55, s32[256]{0:T(256)S(1)} %bitcast.52, s32[1024]{0:T(1024)S(1)} %get-tuple-element.23, s32[1024]{0:T(1024)S(1)} %get-tuple-element.24, pred[1024]{0:T(1024)(128)(4,1)S(1)} %fusion.30), kind=kOutput, calls=%fused_computation.16 | convolution fusion | flops 1076887552 | bytes 5254144 | tf_op jit(solution)/shard_map/dot_general | solution.py:27
  5.1 0.0 copy-start.3
  5.1 0.0 copy-start.7
  5.1 12.0 %all-to-all-start.1 = ((bf16[128,8,2048]{2,1,0:T(8,128)(2,1)}), bf16[128,8,2048]{2,1,0:T(8,128)(2,1)}, u32[]{:S(2)}, u32[]{:S(2)}) async-start(bf16[128,8,2048]{2,1,0:T(8,128)(2,1)} %convert_bitcast_fusion), calls=%async_computation.1 | async-start | bytes 8388608 | tf_op jit(solution)/shard_map/all_to_all | solution.py:32
  17.1 0.0 copy-done.3
  17.1 0.0 copy-done.7
  17.1 3.3 %convert_bitcast_fusion.1 = bf16[128,8,2048]{2,1,0:T(8,128)(2,1)} fusion(bf16[256,2048]{1,0:T(8,128)(2,1)S(1)} %copy-done.7, s32[256]{0:T(256)S(1)} %bitcast.56, s32[256]{0:T(256)S(1)} %bitcast.53, s32[1024]{0:T(1024)S(1)} %get-tuple-element.23, s32[1024]{0:T(1024)S(1)} %get-tuple-element.24, pred[1024]{0:T(1024)(128)(4,1)S(1)} %fusion.30, ...), kind=kOutput, calls=%fused_computation.17 | convolution fusion | flops 1077149696 | bytes 5255168 | tf_op jit(solution)/shard_map/dot_general | solution.py:28
  20.4 47.9 %all-to-all-done.1 = bf16[128,8,2048]{2,1,0:T(8,128)(2,1)} async-done(((bf16[128,8,2048]{2,1,0:T(8,128)(2,1)}), bf16[128,8,2048]{2,1,0:T(8,128)(2,1)}, u32[]{:S(2)}, u32[]{:S(2)}) %all-to-all-start.1) | async-done | bytes 4194336 | tf_op jit(solution)/shard_map/all_to_all | solution.py:32
  68.3 7.3 %all-to-all-start = ((bf16[128,8,2048]{2,1,0:T(8,128)(2,1)}), bf16[128,8,2048]{2,1,0:T(8,128)(2,1)}, u32[]{:S(2)}, u32[]{:S(2)}) async-start(bf16[128,8,2048]{2,1,0:T(8,128)(2,1)} %convert_bitcast_fusion.1), calls=%async_computation | async-start | bytes 8388608 | tf_op jit(solution)/shard_map/all_to_all | solution.py:35
  75.6 0.0 copy-start.4
  75.6 3.2 %constant_dynamic-slice_fusion = bf16[2,512,1024]{2,1,0:T(8,128)(2,1)} fusion(bf16[2,512,2048]{2,1,0:T(8,128)(2,1)} %bitcast.5, s32[]{:T(128)S(6)} %select_n.29), kind=kLoop, calls=%fused_computation.55 | loop fusion | bytes 4194308 | tf_op jit(solution)/shard_map/dynamic_slice | solution.py:48
  78.9 0.0 copy-done.4
  78.9 11.4 %fusion = f32[2,512,2048]{2,1,0:T(8,128)S(1)} fusion(bf16[2,512,2048]{2,1,0:T(8,128)(2,1)} %bitcast.5, bf16[2048,1024]{1,0:T(8,128)(2,1)} %bitcast.59, bf16[2048,1024]{1,0:T(8,128)(2,1)S(1)} %bitcast.58), kind=kOutput, calls=%fused_computation.1 | convolution fusion | flops 8606711808 | bytes 20971520 | tf_op jit(solution)/shard_map/srd,df->srf/dot_general | solution.py:42
  90.3 5.0 %multiply_convert_fusion.2 = (bf16[2,512,1024]{2,1,0:T(8,128)(2,1)}, f32[2,512,1024]{2,1,0:T(8,128)}, f32[2,512,1024]{2,1,0:T(8,128)}) fusion(f32[2,512,2048]{2,1,0:T(8,128)S(1)} %fusion), kind=kLoop, calls=%fused_computation.12 | loop fusion | flops 11534336 | bytes 18874368 | tf_op jit(solution)/shard_map/convert_element_type | solution.py:46
  95.3 31.5 %all-to-all-done = bf16[128,8,2048]{2,1,0:T(8,128)(2,1)} async-done(((bf16[128,8,2048]{2,1,0:T(8,128)(2,1)}), bf16[128,8,2048]{2,1,0:T(8,128)(2,1)}, u32[]{:S(2)}, u32[]{:S(2)}) %all-to-all-start) | async-done | bytes 4194336 | tf_op jit(solution)/shard_map/all_to_all | solution.py:35
  126.8 0.0 copy-start.5
  126.8 10.5 %multiply_convert_fusion = (bf16[2,512,1024]{2,1,0:T(8,128)(2,1)S(1)}, bf16[2,512,1024]{2,1,0:T(8,128)(2,1)S(1)}) fusion(f32[2,512,1024]{2,1,0:T(8,128)} %get-tuple-element.11, f32[2,512,1024]{2,1,0:T(8,128)} %get-tuple-element.10, bf16[2,512,2048]{2,1,0:T(8,128)(2,1)} %bitcast.3, bf16[1,2048,1024]{2,1,0:T(8,128)(2,1)} %param.15), kind=kOutput, calls=%fused_computation.10 | convolution fusion | flops 4299161600 | bytes 20971520 | tf_op jit(solution)/shard_map/srd,df->srf/dot_general | solution.py:52
  137.3 0.0 copy-start.8
  137.3 0.0 copy-start.10
  137.3 0.0 copy-done.5
  137.3 0.0 copy-start.6
  137.3 2.4 %fusion.13 = f32[512,2048]{1,0:T(8,128)S(1)} fusion(bf16[2,512,1024]{2,1,0:T(8,128)(2,1)S(1)} %get-tuple-element.20, s32[]{:T(128)S(6)} %select_n.30, bf16[1,2048,1024]{2,1,0:T(8,128)(2,1)S(1)} %copy-done.5), kind=kOutput, calls=%fused_computation.31 | convolution fusion | flops 2147483648 | bytes 9437188 | tf_op jit(solution)/shard_map/dot_general | solution.py:58
  139.7 0.0 copy-done.8
  139.7 0.0 copy-done.10
  139.7 1.3 copy-done.6
  141.0 3.7 %fusion.6 = bf16[64,8,2048]{2,1,0:T(8,128)(2,1)} fusion(f32[512,2048]{1,0:T(8,128)S(1)} %fusion.13, bf16[2,512,1024]{2,1,0:T(8,128)(2,1)S(1)} %get-tuple-element.19, s32[]{:T(128)S(6)} %select_n.30, bf16[1,2048,1024]{2,1,0:T(8,128)(2,1)S(1)} %copy-done.6), kind=kOutput, calls=%fused_computation.18 | convolution fusion | flops 2149580800 | bytes 11534340 | tf_op jit(solution)/shard_map/dot_general | solution.py:59
  144.7 6.4 %all-to-all-start.2 = ((bf16[64,8,2048]{2,1,0:T(8,128)(2,1)}), bf16[64,8,2048]{2,1,0:T(8,128)(2,1)S(1)}, u32[]{:S(2)}, u32[]{:S(2)}) async-start(bf16[64,8,2048]{2,1,0:T(8,128)(2,1)} %fusion.6), calls=%async_computation.2 | async-start | bytes 4194304 | tf_op jit(solution)/shard_map/all_to_all | solution.py:60
  151.1 0.9 fusion.10
  152.0 6.3 %copy.17 = bf16[2,512,2048]{1,2,0:T(8,128)(2,1)} copy(bf16[2,512,2048]{2,1,0:T(8,128)(2,1)} %bitcast.3) | data formatting | bytes 8388608 | tf_op jit(solution)/shard_map/optimization_barrier | solution.py:49
  158.3 0.0 copy-start.2
  158.3 0.0 copy-start.11
  158.3 6.6 %reduce-precision_reduce_fusion = bf16[1024,1024]{1,0:T(8,128)(2,1)} fusion(bf16[2,512,1024]{2,1,0:T(8,128)(2,1)} %get-tuple-element.13, bf16[2,512,2048]{1,2,0:T(8,128)(2,1)} %copy.17, s32[]{:T(128)S(6)} %select_n.29), kind=kOutput, calls=%fused_computation.4 | convolution fusion | flops 2150629376 | bytes 6291460 | tf_op jit(solution)/shard_map/srd,srf->sdf/dot_general | solution.py:67
  164.9 0.0 copy-done.2
  164.9 0.0 copy-done.11
  164.9 0.0 copy-start.9
  164.9 4.0 %reduce-precision_reduce_fusion.1 = bf16[1024,1024]{1,0:T(8,128)(2,1)} fusion(bf16[2,512,1024]{2,1,0:T(8,128)(2,1)S(1)} %copy-done.2, bf16[2,512,1024]{2,1,0:T(8,128)(2,1)S(1)} %copy-done.11), kind=kOutput, calls=%fused_computation.5 | convolution fusion | flops 2150629376 | bytes 6291456 | tf_op jit(solution)/shard_map/srd,srf->sdf/dot_general | solution.py:67
  168.9 0.0 copy-done.9
  168.9 0.0 copy-start.1
  168.9 4.0 %reduce-precision_reduce_fusion.2 = bf16[1024,1024]{1,0:T(8,128)(2,1)} fusion(bf16[2,512,1024]{2,1,0:T(8,128)(2,1)S(1)} %copy-done.2, bf16[2,512,1024]{2,1,0:T(8,128)(2,1)S(1)} %copy-done.9), kind=kOutput, calls=%fused_computation.6 | convolution fusion | flops 2150629376 | bytes 6291456 | tf_op jit(solution)/shard_map/srd,srf->sdf/dot_general | solution.py:67
  172.9 6.7 %all-to-all-done.2 = bf16[64,8,2048]{2,1,0:T(8,128)(2,1)S(1)} async-done(((bf16[64,8,2048]{2,1,0:T(8,128)(2,1)}), bf16[64,8,2048]{2,1,0:T(8,128)(2,1)S(1)}, u32[]{:S(2)}, u32[]{:S(2)}) %all-to-all-start.2) | async-done | bytes 2097184 | tf_op jit(solution)/shard_map/all_to_all | solution.py:60
  179.6 1.7 convolution_convert_fusion
  181.3 0.0 copy-done.1
  (4 shorter events, 0.0 us)
Async XLA Ops:
  0.6 1.3 copy-start
  5.1 12.0 %copy-start.3 = (bf16[256,2]{0,1:T(2,128)(2,1)S(1)}, bf16[256,2]{0,1:T(2,128)(2,1)}, u32[]{:S(2)}) copy-start(bf16[256,2]{0,1:T(2,128)(2,1)} %param.10) | copy-start | bytes 3076
  5.1 12.0 %copy-start.7 = (bf16[256,2048]{1,0:T(8,128)(2,1)S(1)}, bf16[256,2048]{1,0:T(8,128)(2,1)}, u32[]{:S(2)}) copy-start(bf16[256,2048]{1,0:T(8,128)(2,1)} %param.9) | copy-start | bytes 3145732
  5.1 63.2 %all-to-all-start.1 = ((bf16[128,8,2048]{2,1,0:T(8,128)(2,1)}), bf16[128,8,2048]{2,1,0:T(8,128)(2,1)}, u32[]{:S(2)}, u32[]{:S(2)}) async-start(bf16[128,8,2048]{2,1,0:T(8,128)(2,1)} %convert_bitcast_fusion), calls=%async_computation.1 | async-start | bytes 8388608 | tf_op jit(solution)/shard_map/all_to_all | solution.py:32
  68.3 58.5 %all-to-all-start = ((bf16[128,8,2048]{2,1,0:T(8,128)(2,1)}), bf16[128,8,2048]{2,1,0:T(8,128)(2,1)}, u32[]{:S(2)}, u32[]{:S(2)}) async-start(bf16[128,8,2048]{2,1,0:T(8,128)(2,1)} %convert_bitcast_fusion.1), calls=%async_computation | async-start | bytes 8388608 | tf_op jit(solution)/shard_map/all_to_all | solution.py:35
  75.6 3.3 %copy-start.4 = (bf16[1,2048,1024]{2,1,0:T(8,128)(2,1)S(1)}, bf16[1,2048,1024]{2,1,0:T(8,128)(2,1)}, u32[]{:S(2)}) copy-start(bf16[1,2048,1024]{2,1,0:T(8,128)(2,1)} %param.13) | copy-start | bytes 12582916
  126.8 10.5 %copy-start.5 = (bf16[1,2048,1024]{2,1,0:T(8,128)(2,1)S(1)}, bf16[1,2048,1024]{2,1,0:T(8,128)(2,1)}, u32[]{:S(2)}) copy-start(bf16[1,2048,1024]{2,1,0:T(8,128)(2,1)} %param.13) | copy-start | bytes 12582916
  137.3 2.4 %copy-start.8 = (bf16[2,512,1024]{2,1,0:T(8,128)(2,1)}, bf16[2,512,1024]{2,1,0:T(8,128)(2,1)S(1)}, u32[]{:S(2)}) copy-start(bf16[2,512,1024]{2,1,0:T(8,128)(2,1)S(1)} %get-tuple-element.20) | copy-start | bytes 6291460
  137.3 2.4 %copy-start.10 = (bf16[2,512,1024]{2,1,0:T(8,128)(2,1)}, bf16[2,512,1024]{2,1,0:T(8,128)(2,1)S(1)}, u32[]{:S(2)}) copy-start(bf16[2,512,1024]{2,1,0:T(8,128)(2,1)S(1)} %get-tuple-element.19) | copy-start | bytes 6291460
  137.3 3.7 %copy-start.6 = (bf16[1,2048,1024]{2,1,0:T(8,128)(2,1)S(1)}, bf16[1,2048,1024]{2,1,0:T(8,128)(2,1)}, u32[]{:S(2)}) copy-start(bf16[1,2048,1024]{2,1,0:T(8,128)(2,1)} %param.14) | copy-start | bytes 12582916
  144.7 34.9 %all-to-all-start.2 = ((bf16[64,8,2048]{2,1,0:T(8,128)(2,1)}), bf16[64,8,2048]{2,1,0:T(8,128)(2,1)S(1)}, u32[]{:S(2)}, u32[]{:S(2)}) async-start(bf16[64,8,2048]{2,1,0:T(8,128)(2,1)} %fusion.6), calls=%async_computation.2 | async-start | bytes 4194304 | tf_op jit(solution)/shard_map/all_to_all | solution.py:60
  158.3 6.6 %copy-start.2 = (bf16[2,512,1024]{2,1,0:T(8,128)(2,1)S(1)}, bf16[2,512,1024]{2,1,0:T(8,128)(2,1)}, u32[]{:S(2)}) copy-start(bf16[2,512,1024]{2,1,0:T(8,128)(2,1)} %constant_dynamic-slice_fusion) | copy-start | bytes 6291460
  158.3 6.6 %copy-start.11 = (bf16[2,512,1024]{2,1,0:T(8,128)(2,1)S(1)}, bf16[2,512,1024]{2,1,0:T(8,128)(2,1)}, u32[]{:S(2)}) copy-start(bf16[2,512,1024]{2,1,0:T(8,128)(2,1)} %copy-done.10) | copy-start | bytes 6291460
  164.9 4.0 %copy-start.9 = (bf16[2,512,1024]{2,1,0:T(8,128)(2,1)S(1)}, bf16[2,512,1024]{2,1,0:T(8,128)(2,1)}, u32[]{:S(2)}) copy-start(bf16[2,512,1024]{2,1,0:T(8,128)(2,1)} %copy-done.8) | copy-start | bytes 6291460
  168.9 12.4 %copy-start.1 = (bf16[256,2048]{1,0:T(8,128)(2,1)S(1)}, bf16[256,2048]{1,0:T(8,128)(2,1)}, u32[]{:S(2)}) copy-start(bf16[256,2048]{1,0:T(8,128)(2,1)} %param.8) | copy-start | bytes 3145732

commit v8 on v7

--- a/solution.py
+++ b/solution.py
@@ -29,12 +29,16 @@
         jnp.bfloat16
     )
     axes = ("dp", "seq", "expert")
-    recv_x = lax.all_to_all(
-        send_x.reshape(dp_count * group, slot_count, width), axes, 0, 0, tiled=True
-    ).reshape(dp_count, group * slot_count, width)
-    recv_rg = lax.all_to_all(
-        send_rg.reshape(dp_count * group, slot_count, width), axes, 0, 0, tiled=True
-    ).reshape(dp_count, group * slot_count, width)
+    send = jnp.stack(
+        [
+            send_x.reshape(dp_count * group, slot_count, width),
+            send_rg.reshape(dp_count * group, slot_count, width),
+        ],
+        axis=1,
+    )
+    recv = lax.all_to_all(send, axes, 0, 0, tiled=True)
+    recv_x = recv[:, 0].reshape(dp_count, group * slot_count, width)
+    recv_rg = recv[:, 1].reshape(dp_count, group * slot_count, width)
 
     wg, wu, wd = w_gate[0], w_up[0], w_down[0]
     ff = wg.shape[1]
@@ -46,9 +50,6 @@
     act = (silu_g * up_pre).astype(jnp.bfloat16)
     gate_fac = up_pre * gate_sig * (1.0 + gate_pre * (1.0 - gate_sig))
     x_half = lax.dynamic_slice_in_dim(recv_x, me * half, half, axis=2)
-    recv_rg, gate_fac, silu_g, act, x_half = lax.optimization_barrier(
-        (recv_rg, gate_fac, silu_g, act, x_half)
-    )
     act_grad = jnp.einsum("srd,df->srf", recv_rg, wd, preferred_element_type=jnp.float32)
     gate_grad = (act_grad * gate_fac).astype(jnp.bfloat16)
     up_grad = (act_grad * silu_g).astype(jnp.bfloat16)

time: 182 us -> 208 us (1.14)
  waiting for transfers between devices: 86.1 us -> 114 us
  local copies, waits for them, and re-layouts: 11.3 us -> 9.03 us
    all_to_all x2 -> x1, waiting for transfers between devices: 79.4 us -> 105 us  [per_device(): recv = lax.all_to_all(send, axes, 0, 0, tiled=True)]
    all_to_all x2 -> x1, starting transfers between devices: 19.2 us -> 12 us  [per_device(): recv = lax.all_to_all(send, axes, 0, 0, tiled=True)]
    another operation x0 -> x1, other arithmetic: none -> 6.3 us  [per_device(): jnp.stack([send_x.reshape(dp_count * group, slot_count, width), send_rg.r...]
    optimization_barrier x1 -> x0, local copies, waits for them, and re-layouts: 6.28 us -> none  [per_device(): lax.optimization_barrier((recv_rg, gate_fac, silu_g, act, x_half))]
    all_to_all x1, starting transfers between devices: 6.4 us -> 12.5 us  [per_device(): lax.all_to_all(back.reshape(group, slot_count, width), ('seq', 'expert'),...]
    convert_element_type x1 -> x0, other arithmetic: 4.98 us -> none  [per_device(): act = (silu_g * up_pre).astype(jnp.bfloat16)]
    dot_general x3, matrix products: 14.6 us -> 18.8 us  [wgrad(): jnp.einsum('srd,srf->sdf', left, right, preferred_element_type=jnp.float32)]
    slice x0 -> x1, local copies, waits for them, and re-layouts: none -> 3.95 us  [per_device(): recv_x = recv[:, 0].reshape(dp_count, group * slot_count, width)]
  transfers between devices with their start and end apart: 3 -> 2, of which waited for: 3 -> 2; matrix products, arithmetic and copies ran while one was open for 25% -> 9% of each run, Pallas kernels for 0% -> 0%
where the time goes in v8:
time: 208 us
  waiting for transfers between devices  114 us (55%)
  matrix products  51.7 us (25%)
  starting transfers between devices  24.5 us (12%)
  local copies, waits for them, and re-layouts  9.03 us (4%)
  other arithmetic  8.04 us (4%)
    all_to_all x1, waiting for transfers between devices, per_device(): recv = lax.all_to_all(send, axes, 0, 0, tiled=True)  105 us
    dot_general x3, matrix products, wgrad(): jnp.einsum('srd,srf->sdf', left, right, preferred_element_type=jnp.float32)  18.8 us
    all_to_all x1, starting transfers between devices, per_device(): lax.all_to_all(back.reshape(group, slot_count, width), ('seq', 'expert'),...  12.5 us
    all_to_all x1, starting transfers between devices, per_device(): recv = lax.all_to_all(send, axes, 0, 0, tiled=True)  12 us
    dot_general x1, matrix products, per_device(): jnp.einsum('srd,df->srf', recv_x, wgu, preferred_element_type=jnp.float32)  11.2 us
    all_to_all x1, waiting for transfers between devices, per_device(): lax.all_to_all(back.reshape(group, slot_count, width), ('seq', 'expert'),...  8.71 us
    dot_general x1, matrix products, per_device(): jnp.einsum('srd,df->srf', recv_rg, wd, preferred_element_type=jnp.float32)  8.52 us
    another operation x1, other arithmetic, per_device(): jnp.stack([send_x.reshape(dp_count * group, slot_count, width), send_rg.r...  6.3 us
  transfers between devices with their start and end apart: 2, of which 2 were waited for; matrix products, arithmetic and copies ran while one was open for 9% of the time, Pallas kernels for 0%

profile of v8, /device:TPU:1, one launch (start us, length us, event | category | flops | bytes accessed | tf_op | source)
XLA Modules:
  0.0 207.8 jit_solution(7761377058404903415)
XLA Ops:
  0.6 0.0 copy-start
  0.6 0.0 copy-start.9
  0.7 0.8 multiply_add_fusion
  1.5 0.8 slice_reduce_fusion.1
  2.3 0.0 copy-done
  2.3 2.0 convert_bitcast_fusion.1
  4.3 0.0 copy-done.9
  4.3 3.3 %convert_bitcast_fusion = bf16[128,1,8,2048]{3,2,1,0:T(8,128)(2,1)} fusion(bf16[256,2048]{1,0:T(8,128)(2,1)S(1)} %copy-done.9, s32[256]{0:T(256)S(1)} %bitcast.62, s32[256]{0:T(256)S(1)} %bitcast.59, s32[1024]{0:T(1024)S(1)} %get-tuple-element.12, s32[1024]{0:T(1024)S(1)} %get-tuple-element.13, pred[1024]{0:T(1024)(128)(4,1)S(1)} %fusion.33, ...), kind=kOutput, calls=%fused_computation.16 | convolution fusion | flops 1077149696 | bytes 5255168 | tf_op jit(solution)/shard_map/dot_general | solution.py:28
  7.6 6.3 %pad_maximum_fusion = bf16[128,2,8,2048]{3,2,1,0:T(8,128)(2,1)} fusion(bf16[128,1,8,2048]{3,2,1,0:T(8,128)(2,1)} %convert_bitcast_fusion, bf16[128,1,8,2048]{3,2,1,0:T(8,128)(2,1)S(1)} %convert_bitcast_fusion.1), kind=kLoop, calls=%fused_computation | loop fusion | flops 4194304 | bytes 16777216 | tf_op jit(solution)/shard_map/stack | solution.py:32
  13.9 12.0 %all-to-all-start = ((bf16[128,2,8,2048]{3,2,1,0:T(8,128)(2,1)}), bf16[128,2,8,2048]{3,2,1,0:T(8,128)(2,1)}, u32[]{:S(2)}, u32[]{:S(2)}) async-start(bf16[128,2,8,2048]{3,2,1,0:T(8,128)(2,1)} %pad_maximum_fusion), calls=%async_computation | async-start | bytes 16777216 | tf_op jit(solution)/shard_map/all_to_all | solution.py:39
  25.8 105.0 %all-to-all-done = bf16[128,2,8,2048]{3,2,1,0:T(8,128)(2,1)} async-done(((bf16[128,2,8,2048]{3,2,1,0:T(8,128)(2,1)}), bf16[128,2,8,2048]{3,2,1,0:T(8,128)(2,1)}, u32[]{:S(2)}, u32[]{:S(2)}) %all-to-all-start) | async-done | bytes 8388640 | tf_op jit(solution)/shard_map/all_to_all | solution.py:39
  130.9 0.0 copy-start.7
  130.9 0.0 copy-start.8
  130.9 3.9 %fusion.45 = (bf16[128,1,8,2048]{3,2,1,0:T(8,128)(2,1)S(1)}, bf16[128,1,8,2048]{3,2,1,0:T(8,128)(2,1)S(1)}) fusion(bf16[128,2,8,2048]{3,2,1,0:T(8,128)(2,1)} %all-to-all-done), kind=kLoop, calls=%fused_computation.64 | loop fusion | bytes 16777216 | tf_op jit(solution)/shard_map/slice | solution.py:40
  134.8 0.0 copy-start.4
  134.8 0.0 copy-start.2
  134.8 0.7 copy-done.7
  135.5 3.6 %copy-done.8 = bf16[1,2048,1024]{2,1,0:T(8,128)(2,1)S(1)} copy-done((bf16[1,2048,1024]{2,1,0:T(8,128)(2,1)S(1)}, bf16[1,2048,1024]{2,1,0:T(8,128)(2,1)}, u32[]{:S(2)}) %copy-start.8) | copy-done | bytes 4194328
  139.1 0.0 copy-start.6
  139.1 11.2 %fusion = f32[2,512,2048]{2,1,0:T(8,128)} fusion(bf16[2,512,2048]{2,1,0:T(8,128)(2,1)S(1)} %bitcast.55, bf16[2048,1024]{1,0:T(8,128)(2,1)S(1)} %bitcast.65, bf16[2048,1024]{1,0:T(8,128)(2,1)S(1)} %bitcast.64), kind=kOutput, calls=%fused_computation.2 | convolution fusion | flops 8606711808 | bytes 20971520 | tf_op jit(solution)/shard_map/srd,df->srf/dot_general | solution.py:46
  150.3 0.0 copy-done.4
  150.3 0.0 copy-done.2
  150.3 0.0 copy-done.6
  150.3 8.5 %multiply_convert_fusion.1 = (bf16[2,512,1024]{2,1,0:T(8,128)(2,1)S(1)}, bf16[2,512,1024]{2,1,0:T(8,128)(2,1)S(1)}) fusion(f32[2,512,2048]{2,1,0:T(8,128)} %fusion, bf16[2,512,2048]{2,1,0:T(8,128)(2,1)S(1)} %bitcast.53, bf16[1,2048,1024]{2,1,0:T(8,128)(2,1)S(1)} %copy-done.6), kind=kOutput, calls=%fused_computation.12 | convolution fusion | flops 4308598784 | bytes 20971520 | tf_op jit(solution)/shard_map/srd,df->srf/dot_general | solution.py:53
  158.8 0.0 copy-start.10
  158.8 0.0 copy-start.12
  158.8 2.4 %fusion.15 = f32[512,2048]{1,0:T(8,128)S(1)} fusion(bf16[2,512,1024]{2,1,0:T(8,128)(2,1)S(1)} %get-tuple-element.7, s32[]{:T(128)S(6)} %select_n.29, bf16[1,2048,1024]{2,1,0:T(8,128)(2,1)S(1)} %copy-done.7), kind=kOutput, calls=%fused_computation.33 | convolution fusion | flops 2147483648 | bytes 9437188 | tf_op jit(solution)/shard_map/dot_general | solution.py:59
  161.2 0.0 copy-done.10
  161.2 0.0 copy-done.12
  161.2 3.8 %fusion.6 = bf16[64,8,2048]{2,1,0:T(8,128)(2,1)} fusion(f32[512,2048]{1,0:T(8,128)S(1)} %fusion.15, bf16[2,512,1024]{2,1,0:T(8,128)(2,1)S(1)} %get-tuple-element.6, s32[]{:T(128)S(6)} %select_n.29, bf16[1,2048,1024]{2,1,0:T(8,128)(2,1)S(1)} %copy-done.8), kind=kOutput, calls=%fused_computation.18 | convolution fusion | flops 2149580800 | bytes 11534340 | tf_op jit(solution)/shard_map/dot_general | solution.py:60
  165.0 12.5 %all-to-all-start.1 = ((bf16[64,8,2048]{2,1,0:T(8,128)(2,1)}), bf16[64,8,2048]{2,1,0:T(8,128)(2,1)S(1)}, u32[]{:S(2)}, u32[]{:S(2)}) async-start(bf16[64,8,2048]{2,1,0:T(8,128)(2,1)} %fusion.6), calls=%async_computation.1 | async-start | bytes 4194304 | tf_op jit(solution)/shard_map/all_to_all | solution.py:61
  177.5 0.9 fusion.12
  178.4 0.0 copy-start.5
  178.5 0.0 copy-start.11
  178.5 6.7 %reduce-precision_reduce_fusion.1 = bf16[1024,1024]{1,0:T(8,128)(2,1)} fusion(bf16[2,512,1024]{2,1,0:T(8,128)(2,1)} %copy-done.12, bf16[2,512,2048]{2,1,0:T(8,128)(2,1)} %bitcast.56, s32[]{:T(128)S(6)} %select_n.30), kind=kOutput, calls=%fused_computation.6 | convolution fusion | flops 2150629376 | bytes 6291460 | tf_op jit(solution)/shard_map/srd,srf->sdf/dot_general | solution.py:68
  185.2 0.0 copy-done.5
  185.2 0.0 copy-done.11
  185.2 0.0 copy-start.3
  185.2 4.0 %reduce-precision_reduce_fusion.2 = bf16[1024,1024]{1,0:T(8,128)(2,1)} fusion(bf16[2,512,1024]{2,1,0:T(8,128)(2,1)S(1)} %copy-done.11, bf16[2,512,2048]{2,1,0:T(8,128)(2,1)S(1)} %bitcast.57, s32[]{:T(128)S(6)} %select_n.30), kind=kOutput, calls=%fused_computation.7 | convolution fusion | flops 2150629376 | bytes 6291460 | tf_op jit(solution)/shard_map/srd,srf->sdf/dot_general | solution.py:68
  189.2 0.0 copy-done.3
  189.2 0.0 copy-start.1
  189.2 8.1 %reduce-precision_reduce_fusion = bf16[1024,1024]{1,0:T(8,128)(2,1)} fusion(f32[2,512,2048]{2,1,0:T(8,128)} %fusion, bf16[2,512,2048]{2,1,0:T(8,128)(2,1)S(1)} %bitcast.54, s32[]{:T(128)S(6)} %select_n.30), kind=kOutput, calls=%fused_computation.5 | convolution fusion | flops 2156920832 | bytes 12582916 | tf_op jit(solution)/shard_map/srd,srf->sdf/dot_general | solution.py:68
  197.3 8.7 %all-to-all-done.1 = bf16[64,8,2048]{2,1,0:T(8,128)(2,1)S(1)} async-done(((bf16[64,8,2048]{2,1,0:T(8,128)(2,1)}), bf16[64,8,2048]{2,1,0:T(8,128)(2,1)S(1)}, u32[]{:S(2)}, u32[]{:S(2)}) %all-to-all-start.1) | async-done | bytes 2097184 | tf_op jit(solution)/shard_map/all_to_all | solution.py:61
  206.0 1.7 convolution_convert_fusion
  207.7 0.0 copy-done.1
  (3 shorter events, 0.0 us)
Async XLA Ops:
  0.6 1.7 copy-start
  0.6 3.6 %copy-start.9 = (bf16[256,2048]{1,0:T(8,128)(2,1)S(1)}, bf16[256,2048]{1,0:T(8,128)(2,1)}, u32[]{:S(2)}) copy-start(bf16[256,2048]{1,0:T(8,128)(2,1)} %param.9) | copy-start | bytes 3145732
  13.9 117.0 %all-to-all-start = ((bf16[128,2,8,2048]{3,2,1,0:T(8,128)(2,1)}), bf16[128,2,8,2048]{3,2,1,0:T(8,128)(2,1)}, u32[]{:S(2)}, u32[]{:S(2)}) async-start(bf16[128,2,8,2048]{3,2,1,0:T(8,128)(2,1)} %pad_maximum_fusion), calls=%async_computation | async-start | bytes 16777216 | tf_op jit(solution)/shard_map/all_to_all | solution.py:39
  130.9 4.7 %copy-start.7 = (bf16[1,2048,1024]{2,1,0:T(8,128)(2,1)S(1)}, bf16[1,2048,1024]{2,1,0:T(8,128)(2,1)}, u32[]{:S(2)}) copy-start(bf16[1,2048,1024]{2,1,0:T(8,128)(2,1)} %param.13) | copy-start | bytes 12582916
  130.9 8.2 %copy-start.8 = (bf16[1,2048,1024]{2,1,0:T(8,128)(2,1)S(1)}, bf16[1,2048,1024]{2,1,0:T(8,128)(2,1)}, u32[]{:S(2)}) copy-start(bf16[1,2048,1024]{2,1,0:T(8,128)(2,1)} %param.14) | copy-start | bytes 12582916
  134.8 15.5 %copy-start.4 = (bf16[128,1,8,2048]{3,2,1,0:T(8,128)(2,1)}, bf16[128,1,8,2048]{3,2,1,0:T(8,128)(2,1)S(1)}, u32[]{:S(2)}) copy-start(bf16[128,1,8,2048]{3,2,1,0:T(8,128)(2,1)S(1)} %get-tuple-element.8) | copy-start | bytes 12582916
  134.8 15.4 %copy-start.2 = (bf16[128,1,8,2048]{3,2,1,0:T(8,128)(2,1)}, bf16[128,1,8,2048]{3,2,1,0:T(8,128)(2,1)S(1)}, u32[]{:S(2)}) copy-start(bf16[128,1,8,2048]{3,2,1,0:T(8,128)(2,1)S(1)} %get-tuple-element.9) | copy-start | bytes 12582916
  139.1 11.2 %copy-start.6 = (bf16[1,2048,1024]{2,1,0:T(8,128)(2,1)S(1)}, bf16[1,2048,1024]{2,1,0:T(8,128)(2,1)}, u32[]{:S(2)}) copy-start(bf16[1,2048,1024]{2,1,0:T(8,128)(2,1)} %param.15) | copy-start | bytes 12582916
  158.8 2.4 %copy-start.10 = (bf16[2,512,1024]{2,1,0:T(8,128)(2,1)}, bf16[2,512,1024]{2,1,0:T(8,128)(2,1)S(1)}, u32[]{:S(2)}) copy-start(bf16[2,512,1024]{2,1,0:T(8,128)(2,1)S(1)} %get-tuple-element.7) | copy-start | bytes 6291460
  158.8 2.4 %copy-start.12 = (bf16[2,512,1024]{2,1,0:T(8,128)(2,1)}, bf16[2,512,1024]{2,1,0:T(8,128)(2,1)S(1)}, u32[]{:S(2)}) copy-start(bf16[2,512,1024]{2,1,0:T(8,128)(2,1)S(1)} %get-tuple-element.6) | copy-start | bytes 6291460
  165.0 41.0 %all-to-all-start.1 = ((bf16[64,8,2048]{2,1,0:T(8,128)(2,1)}), bf16[64,8,2048]{2,1,0:T(8,128)(2,1)S(1)}, u32[]{:S(2)}, u32[]{:S(2)}) async-start(bf16[64,8,2048]{2,1,0:T(8,128)(2,1)} %fusion.6), calls=%async_computation.1 | async-start | bytes 4194304 | tf_op jit(solution)/shard_map/all_to_all | solution.py:61
  178.4 6.8 %copy-start.5 = (bf16[128,1,8,2048]{3,2,1,0:T(8,128)(2,1)S(1)}, bf16[128,1,8,2048]{3,2,1,0:T(8,128)(2,1)}, u32[]{:S(2)}) copy-start(bf16[128,1,8,2048]{3,2,1,0:T(8,128)(2,1)} %copy-done.4) | copy-start | bytes 12582916
  178.5 6.7 %copy-start.11 = (bf16[2,512,1024]{2,1,0:T(8,128)(2,1)S(1)}, bf16[2,512,1024]{2,1,0:T(8,128)(2,1)}, u32[]{:S(2)}) copy-start(bf16[2,512,1024]{2,1,0:T(8,128)(2,1)} %copy-done.10) | copy-start | bytes 6291460
  185.2 4.0 %copy-start.3 = (bf16[128,1,8,2048]{3,2,1,0:T(8,128)(2,1)S(1)}, bf16[128,1,8,2048]{3,2,1,0:T(8,128)(2,1)}, u32[]{:S(2)}) copy-start(bf16[128,1,8,2048]{3,2,1,0:T(8,128)(2,1)} %copy-done.2) | copy-start | bytes 12582916
  189.2 18.5 %copy-start.1 = (bf16[256,2048]{1,0:T(8,128)(2,1)S(1)}, bf16[256,2048]{1,0:T(8,128)(2,1)}, u32[]{:S(2)}) copy-start(bf16[256,2048]{1,0:T(8,128)(2,1)} %param.8) | copy-start | bytes 3145732

commit v9 on v7

--- a/solution.py
+++ b/solution.py
@@ -19,7 +19,8 @@
     me = lax.axis_index("dp")
     position = expert_ids * slot_count + route_slots
 
-    slots = lax.broadcasted_iota(jnp.int32, (dp_count * rows, cell_count), 0) % rows
+    order = lax.broadcasted_iota(jnp.int32, (dp_count * rows, cell_count), 0)
+    slots = order // (dp_count * slot_count) * slot_count + order % slot_count
     hit0 = slots == position[None, :, 0]
     hit1 = slots == position[None, :, 1]
     pick = (hit0 | hit1).astype(jnp.bfloat16)
@@ -28,13 +29,15 @@
     send_rg = jnp.dot(weigh.astype(jnp.bfloat16), grad_out, preferred_element_type=jnp.float32).astype(
         jnp.bfloat16
     )
-    axes = ("dp", "seq", "expert")
-    recv_x = lax.all_to_all(
-        send_x.reshape(dp_count * group, slot_count, width), axes, 0, 0, tiled=True
-    ).reshape(dp_count, group * slot_count, width)
-    recv_rg = lax.all_to_all(
-        send_rg.reshape(dp_count * group, slot_count, width), axes, 0, 0, tiled=True
-    ).reshape(dp_count, group * slot_count, width)
+    axes = ("seq", "expert", "dp")
+
+    def exchange(send):
+        recv = lax.all_to_all(send.reshape(group * dp_count, slot_count, width), axes, 0, 0, tiled=True)
+        recv = recv.reshape(group, dp_count, slot_count, width).transpose(1, 0, 2, 3)
+        return recv.reshape(dp_count, group * slot_count, width)
+
+    recv_x = exchange(send_x)
+    recv_rg = exchange(send_rg)
 
     wg, wu, wd = w_gate[0], w_up[0], w_down[0]
     ff = wg.shape[1]
@@ -72,8 +75,10 @@
     grad_up = wgrad(x_half, up_grad)
     grad_down = wgrad(rg_half, act)
 
+    back_slots = lax.broadcasted_iota(jnp.int32, (rows, cell_count), 0)
+    back_pick = (back_slots == position[None, :, 0]) | (back_slots == position[None, :, 1])
     grad_tokens = jnp.dot(
-        pick[:rows].T, returned, preferred_element_type=jnp.float32
+        back_pick.astype(jnp.bfloat16).T, returned, preferred_element_type=jnp.float32
     ).astype(jnp.bfloat16)
     return grad_tokens, grad_gate, grad_up, grad_down
 

time: 182 us -> 188 us (1.033)
  local copies, waits for them, and re-layouts: 11.3 us -> 22.6 us
  starting transfers between devices: 25.6 us -> 21.7 us
  matrix products: 50.9 us -> 48.1 us
  waiting for transfers between devices: 86.1 us -> 88.2 us
    unnamed x24 -> x34, local copies, waits for them, and re-layouts: 1.77 us -> 7.02 us
    reshape x0 -> x1, local copies, waits for them, and re-layouts: none -> 5.06 us  [exchange(): recv.reshape(group, dp_count, slot_count, width).transpose(1, 0, 2, 3)]
    dot_general x1, matrix products: 10.5 us -> 7.18 us  [per_device(): jnp.einsum('srd,df->srf', recv_rg, wd, preferred_element_type=jnp.float32)]
    transpose x0 -> x1, local copies, waits for them, and re-layouts: none -> 2.65 us  [exchange(): recv.reshape(group, dp_count, slot_count, width).transpose(1, 0, 2, 3)]
    all_to_all x2, starting transfers between devices: 19.2 us -> 17.2 us  [exchange(): lax.all_to_all(send.reshape(group * dp_count, slot_count, width), axes, 0...]
    all_to_all x1, starting transfers between devices: 6.4 us -> 4.48 us  [per_device(): lax.all_to_all(back.reshape(group, slot_count, width), ('seq', 'expert'),...]
  transfers between devices with their start and end apart: 3 -> 3, of which waited for: 3 -> 3; matrix products, arithmetic and copies ran while one was open for 25% -> 24% of each run, Pallas kernels for 0% -> 0%
where the time goes in v9:
time: 188 us; the launch traced here: 187 us
  waiting for transfers between devices  88.2 us (47%)
  matrix products  48.1 us (26%)
  local copies, waits for them, and re-layouts  22.6 us (12%)
  starting transfers between devices  21.7 us (12%)
  other arithmetic  5.75 us (3%)
    all_to_all x2, waiting for transfers between devices, exchange(): lax.all_to_all(send.reshape(group * dp_count, slot_count, width), axes, 0...  81.1 us
    all_to_all x2, starting transfers between devices, exchange(): lax.all_to_all(send.reshape(group * dp_count, slot_count, width), axes, 0...  17.2 us
    dot_general x3, matrix products, wgrad(): jnp.einsum('srd,srf->sdf', left, right, preferred_element_type=jnp.float32)  14.6 us
    dot_general x1, matrix products, per_device(): jnp.einsum('srd,df->srf', recv_x, wgu, preferred_element_type=jnp.float32)  10.8 us
    dot_general x1, matrix products, per_device(): jnp.einsum('srd,df->srf', recv_rg, wd, preferred_element_type=jnp.float32)  7.18 us
    all_to_all x1, waiting for transfers between devices, per_device(): lax.all_to_all(back.reshape(group, slot_count, width), ('seq', 'expert'),...  7.05 us
    unnamed x34, local copies, waits for them, and re-layouts  7.02 us
    optimization_barrier x1, local copies, waits for them, and re-layouts, per_device(): lax.optimization_barrier((recv_rg, gate_fac, silu_g, act, x_half))  6.28 us
  transfers between devices with their start and end apart: 3, of which 3 were waited for; matrix products, arithmetic and copies ran while one was open for 24% of the time, Pallas kernels for 0%

profile of v9, /device:TPU:1, one launch (start us, length us, event | category | flops | bytes accessed | tf_op | source)
XLA Modules:
  0.0 187.1 jit_solution(5403217177321574759)
XLA Ops:
  0.6 0.0 copy-start
  0.7 0.8 multiply_add_fusion
  1.5 0.4 copy-done
  1.9 3.8 %convert_bitcast_fusion = bf16[128,8,2048]{2,1,0:T(8,128)(2,1)} fusion(bf16[256,2048]{1,0:T(8,128)(2,1)S(1)} %copy-done, s32[256]{0:T(256)S(1)} %bitcast.68, s32[1024]{0:T(1024)S(1)} %get-tuple-element.23, s32[1024]{0:T(1024)S(1)} %get-tuple-element.25, s32[1024]{0:T(1024)S(1)} %get-tuple-element.24, s32[1024]{0:T(1024)S(1)} %get-tuple-element.26, ...), kind=kOutput, calls=%fused_computation.18 | convolution fusion | flops 1077673984 | bytes 5263360 | tf_op jit(solution)/shard_map/dot_general | solution.py:28
  5.7 0.0 copy-start.12
  5.7 12.0 %all-to-all-start.1 = ((bf16[128,8,2048]{2,1,0:T(8,128)(2,1)}), bf16[128,8,2048]{2,1,0:T(8,128)(2,1)}, u32[]{:S(2)}, u32[]{:S(2)}) async-start(bf16[128,8,2048]{2,1,0:T(8,128)(2,1)} %convert_bitcast_fusion), calls=%async_computation.1 | async-start | bytes 8388608 | tf_op jit(solution)/shard_map/all_to_all | solution.py:35
  17.7 0.0 copy-done.7
  17.7 0.0 copy-done.12
  17.7 3.8 %convert_bitcast_fusion.1 = bf16[128,8,2048]{2,1,0:T(8,128)(2,1)} fusion(bf16[256,2048]{1,0:T(8,128)(2,1)S(1)} %copy-done.12, bf16[256]{0:T(256)(128)(2,1)S(1)} %get-tuple-element.15, bf16[256]{0:T(256)(128)(2,1)S(1)} %get-tuple-element.14, s32[256]{0:T(256)S(1)} %bitcast.69, s32[1024]{0:T(1024)S(1)} %get-tuple-element.23, s32[1024]{0:T(1024)S(1)} %get-tuple-element.25, ...), kind=kOutput, calls=%fused_computation.19 | convolution fusion | flops 1077936128 | bytes 5264384 | tf_op jit(solution)/shard_map/dot_general | solution.py:29
  21.6 49.6 %all-to-all-done.1 = bf16[128,8,2048]{2,1,0:T(8,128)(2,1)} async-done(((bf16[128,8,2048]{2,1,0:T(8,128)(2,1)}), bf16[128,8,2048]{2,1,0:T(8,128)(2,1)}, u32[]{:S(2)}, u32[]{:S(2)}) %all-to-all-start.1) | async-done | bytes 4194336 | tf_op jit(solution)/shard_map/all_to_all | solution.py:35
  71.2 5.3 %all-to-all-start = ((bf16[128,8,2048]{2,1,0:T(8,128)(2,1)}), bf16[128,8,2048]{2,1,0:T(8,128)(2,1)}, u32[]{:S(2)}, u32[]{:S(2)}) async-start(bf16[128,8,2048]{2,1,0:T(8,128)(2,1)} %convert_bitcast_fusion.1), calls=%async_computation | async-start | bytes 8388608 | tf_op jit(solution)/shard_map/all_to_all | solution.py:35
  76.5 0.0 copy-start.8
  76.5 0.0 copy-start.10
  76.5 5.1 %copy.31 = bf16[64,2,8,2048]{3,2,0,1:T(8,128)(2,1)} copy(bf16[64,2,8,2048]{3,2,1,0:T(8,128)(2,1)} %bitcast.7) | data formatting | bytes 8388608 | tf_op jit(solution)/shard_map/reshape | solution.py:36
  81.6 0.0 copy-done.8
  81.6 1.2 copy-done.10
  82.7 10.8 %fusion = f32[2,512,2048]{2,1,0:T(8,128)S(1)} fusion(bf16[2048,1024]{1,0:T(8,128)(2,1)S(1)} %bitcast.72, bf16[2048,1024]{1,0:T(8,128)(2,1)S(1)} %bitcast.71, bf16[64,2,8,2048]{3,2,1,0:T(8,128)(2,1)} %bitcast.7), kind=kOutput, calls=%fused_computation.1 | convolution fusion | flops 8606711808 | bytes 20971520 | tf_op jit(solution)/shard_map/srd,df->srf/dot_general | solution.py:45
  93.5 5.0 %multiply_convert_fusion.2 = (bf16[2,512,1024]{2,1,0:T(8,128)(2,1)}, f32[2,512,1024]{2,1,0:T(8,128)}, f32[2,512,1024]{2,1,0:T(8,128)}) fusion(f32[2,512,2048]{2,1,0:T(8,128)S(1)} %fusion), kind=kLoop, calls=%fused_computation.14 | loop fusion | flops 11534336 | bytes 18874368 | tf_op jit(solution)/shard_map/convert_element_type | solution.py:49
  98.5 31.5 %all-to-all-done = bf16[128,8,2048]{2,1,0:T(8,128)(2,1)} async-done(((bf16[128,8,2048]{2,1,0:T(8,128)(2,1)}), bf16[128,8,2048]{2,1,0:T(8,128)(2,1)}, u32[]{:S(2)}, u32[]{:S(2)}) %all-to-all-start) | async-done | bytes 4194336 | tf_op jit(solution)/shard_map/all_to_all | solution.py:35
  130.0 2.7 %copy.32 = bf16[2,64,8,2048]{3,2,1,0:T(8,128)(2,1)S(1)} copy(bf16[2,64,8,2048]{3,2,0,1:T(8,128)(2,1)} %bitcast.4) | data formatting | bytes 8388608 | tf_op jit(solution)/shard_map/transpose | solution.py:36
  132.6 0.0 copy-start.2
  132.6 0.0 copy-start.4
  132.7 0.8 copy-done.3
  133.4 1.5 constant_dynamic-slice_fusion
  135.0 2.0 %copy-done.5 = f32[2,512,1024]{2,1,0:T(8,128)S(1)} copy-done((f32[2,512,1024]{2,1,0:T(8,128)S(1)}, f32[2,512,1024]{2,1,0:T(8,128)}, u32[]{:S(2)}) %copy-start.5) | copy-done | bytes 4194328
  136.9 1.4 copy-done.4
  138.3 7.2 %multiply_convert_fusion = (bf16[2,512,1024]{2,1,0:T(8,128)(2,1)S(1)}, bf16[2,512,1024]{2,1,0:T(8,128)(2,1)S(1)}) fusion(f32[2,512,1024]{2,1,0:T(8,128)S(1)} %copy-done.5, f32[2,512,1024]{2,1,0:T(8,128)S(1)} %copy-done.4, bf16[2,512,2048]{2,1,0:T(8,128)(2,1)S(1)} %bitcast.62, bf16[1,2048,1024]{2,1,0:T(8,128)(2,1)} %param.15), kind=kOutput, calls=%fused_computation.12 | convolution fusion | flops 4299161600 | bytes 20971520 | tf_op jit(solution)/shard_map/srd,df->srf/dot_general | solution.py:55
  145.5 0.0 copy-done.2
  145.5 0.0 copy-start.13
  145.5 0.0 copy-start.15
  145.5 0.0 copy-done.9
  145.5 0.0 copy-start.11
  145.5 2.4 %fusion.10 = f32[512,2048]{1,0:T(8,128)S(1)} fusion(bf16[2,512,1024]{2,1,0:T(8,128)(2,1)S(1)} %get-tuple-element.20, s32[]{:T(128)S(6)} %select_n.38, bf16[1,2048,1024]{2,1,0:T(8,128)(2,1)S(1)} %copy-done.9), kind=kOutput, calls=%fused_computation.28 | convolution fusion | flops 2147483648 | bytes 9437188 | tf_op jit(solution)/shard_map/dot_general | solution.py:61
  147.9 0.0 copy-done.13
  147.9 0.0 copy-done.15
  147.9 1.3 copy-done.11
  149.2 3.8 %fusion.6 = bf16[64,8,2048]{2,1,0:T(8,128)(2,1)} fusion(f32[512,2048]{1,0:T(8,128)S(1)} %fusion.10, bf16[2,512,1024]{2,1,0:T(8,128)(2,1)S(1)} %get-tuple-element.19, s32[]{:T(128)S(6)} %select_n.38, bf16[1,2048,1024]{2,1,0:T(8,128)(2,1)S(1)} %copy-done.11), kind=kOutput, calls=%fused_computation.20 | convolution fusion | flops 2149580800 | bytes 11534340 | tf_op jit(solution)/shard_map/dot_general | solution.py:62
  153.0 4.5 %all-to-all-start.2 = ((bf16[64,8,2048]{2,1,0:T(8,128)(2,1)}), bf16[64,8,2048]{2,1,0:T(8,128)(2,1)S(1)}, u32[]{:S(2)}, u32[]{:S(2)}) async-start(bf16[64,8,2048]{2,1,0:T(8,128)(2,1)} %fusion.6), calls=%async_computation.2 | async-start | bytes 4194304 | tf_op jit(solution)/shard_map/all_to_all | solution.py:63
  157.4 6.3 %copy.25 = bf16[2,512,2048]{1,2,0:T(8,128)(2,1)} copy(bf16[2,512,2048]{2,1,0:T(8,128)(2,1)} %bitcast.63) | data formatting | bytes 8388608 | tf_op jit(solution)/shard_map/optimization_barrier | solution.py:52
  163.7 6.6 %reduce-precision_reduce_fusion = bf16[1024,1024]{1,0:T(8,128)(2,1)} fusion(bf16[2,512,1024]{2,1,0:T(8,128)(2,1)} %get-tuple-element.13, bf16[2,512,2048]{1,2,0:T(8,128)(2,1)} %copy.25, s32[]{:T(128)S(6)} %select_n.37), kind=kOutput, calls=%fused_computation.4 | convolution fusion | flops 2150629376 | bytes 6291460 | tf_op jit(solution)/shard_map/srd,srf->sdf/dot_general | solution.py:70
  170.3 0.0 copy-done.6
  170.3 0.0 copy-done.16
  170.3 4.0 %reduce-precision_reduce_fusion.1 = bf16[1024,1024]{1,0:T(8,128)(2,1)} fusion(bf16[2,512,1024]{2,1,0:T(8,128)(2,1)S(1)} %copy-done.6, bf16[2,512,1024]{2,1,0:T(8,128)(2,1)S(1)} %copy-done.16), kind=kOutput, calls=%fused_computation.5 | convolution fusion | flops 2150629376 | bytes 6291456 | tf_op jit(solution)/shard_map/srd,srf->sdf/dot_general | solution.py:70
  174.3 0.0 copy-done.14
  174.3 4.0 %reduce-precision_reduce_fusion.2 = bf16[1024,1024]{1,0:T(8,128)(2,1)} fusion(bf16[2,512,1024]{2,1,0:T(8,128)(2,1)S(1)} %copy-done.6, bf16[2,512,1024]{2,1,0:T(8,128)(2,1)S(1)} %copy-done.14), kind=kOutput, calls=%fused_computation.6 | convolution fusion | flops 2150629376 | bytes 6291456 | tf_op jit(solution)/shard_map/srd,srf->sdf/dot_general | solution.py:70
  178.4 7.0 %all-to-all-done.2 = bf16[64,8,2048]{2,1,0:T(8,128)(2,1)S(1)} async-done(((bf16[64,8,2048]{2,1,0:T(8,128)(2,1)}), bf16[64,8,2048]{2,1,0:T(8,128)(2,1)S(1)}, u32[]{:S(2)}, u32[]{:S(2)}) %all-to-all-start.2) | async-done | bytes 2097184 | tf_op jit(solution)/shard_map/all_to_all | solution.py:63
  185.4 1.7 convolution_convert_fusion
  187.1 0.0 copy-done.1
  (13 shorter events, 0.1 us)
Async XLA Ops:
  0.6 1.3 copy-start
  5.7 12.0 %copy-start.7 = (bf16[256,2]{0,1:T(2,128)(2,1)S(1)}, bf16[256,2]{0,1:T(2,128)(2,1)}, u32[]{:S(2)}) copy-start(bf16[256,2]{0,1:T(2,128)(2,1)} %param.10) | copy-start | bytes 3076
  5.7 12.0 %copy-start.12 = (bf16[256,2048]{1,0:T(8,128)(2,1)S(1)}, bf16[256,2048]{1,0:T(8,128)(2,1)}, u32[]{:S(2)}) copy-start(bf16[256,2048]{1,0:T(8,128)(2,1)} %param.9) | copy-start | bytes 3145732
  5.7 65.5 %all-to-all-start.1 = ((bf16[128,8,2048]{2,1,0:T(8,128)(2,1)}), bf16[128,8,2048]{2,1,0:T(8,128)(2,1)}, u32[]{:S(2)}, u32[]{:S(2)}) async-start(bf16[128,8,2048]{2,1,0:T(8,128)(2,1)} %convert_bitcast_fusion), calls=%async_computation.1 | async-start | bytes 8388608 | tf_op jit(solution)/shard_map/all_to_all | solution.py:35
  71.2 58.8 %all-to-all-start = ((bf16[128,8,2048]{2,1,0:T(8,128)(2,1)}), bf16[128,8,2048]{2,1,0:T(8,128)(2,1)}, u32[]{:S(2)}, u32[]{:S(2)}) async-start(bf16[128,8,2048]{2,1,0:T(8,128)(2,1)} %convert_bitcast_fusion.1), calls=%async_computation | async-start | bytes 8388608 | tf_op jit(solution)/shard_map/all_to_all | solution.py:35
  76.5 5.1 %copy-start.8 = (bf16[1,2048,1024]{2,1,0:T(8,128)(2,1)S(1)}, bf16[1,2048,1024]{2,1,0:T(8,128)(2,1)}, u32[]{:S(2)}) copy-start(bf16[1,2048,1024]{2,1,0:T(8,128)(2,1)} %param.13) | copy-start | bytes 12582916
  76.5 6.2 %copy-start.10 = (bf16[1,2048,1024]{2,1,0:T(8,128)(2,1)S(1)}, bf16[1,2048,1024]{2,1,0:T(8,128)(2,1)}, u32[]{:S(2)}) copy-start(bf16[1,2048,1024]{2,1,0:T(8,128)(2,1)} %param.14) | copy-start | bytes 12582916
  130.0 3.4 %copy-start.3 = (bf16[64,2,8,2048]{3,2,0,1:T(8,128)(2,1)S(1)}, bf16[64,2,8,2048]{3,2,0,1:T(8,128)(2,1)}, u32[]{:S(2)}) copy-start(bf16[64,2,8,2048]{3,2,0,1:T(8,128)(2,1)} %copy.31) | copy-start | bytes 12582916
  130.0 6.9 %copy-start.5 = (f32[2,512,1024]{2,1,0:T(8,128)S(1)}, f32[2,512,1024]{2,1,0:T(8,128)}, u32[]{:S(2)}) copy-start(f32[2,512,1024]{2,1,0:T(8,128)} %get-tuple-element.11) | copy-start | bytes 12582916
  132.6 12.8 %copy-start.2 = (bf16[2,64,8,2048]{3,2,1,0:T(8,128)(2,1)}, bf16[2,64,8,2048]{3,2,1,0:T(8,128)(2,1)S(1)}, u32[]{:S(2)}) copy-start(bf16[2,64,8,2048]{3,2,1,0:T(8,128)(2,1)S(1)} %copy.32) | copy-start | bytes 12582916
  132.6 5.6 %copy-start.4 = (f32[2,512,1024]{2,1,0:T(8,128)S(1)}, f32[2,512,1024]{2,1,0:T(8,128)}, u32[]{:S(2)}) copy-start(f32[2,512,1024]{2,1,0:T(8,128)} %get-tuple-element.10) | copy-start | bytes 12582916
  138.3 7.2 %copy-start.9 = (bf16[1,2048,1024]{2,1,0:T(8,128)(2,1)S(1)}, bf16[1,2048,1024]{2,1,0:T(8,128)(2,1)}, u32[]{:S(2)}) copy-start(bf16[1,2048,1024]{2,1,0:T(8,128)(2,1)} %param.13) | copy-start | bytes 12582916
  145.5 2.4 %copy-start.13 = (bf16[2,512,1024]{2,1,0:T(8,128)(2,1)}, bf16[2,512,1024]{2,1,0:T(8,128)(2,1)S(1)}, u32[]{:S(2)}) copy-start(bf16[2,512,1024]{2,1,0:T(8,128)(2,1)S(1)} %get-tuple-element.20) | copy-start | bytes 6291460
  145.5 2.4 %copy-start.15 = (bf16[2,512,1024]{2,1,0:T(8,128)(2,1)}, bf16[2,512,1024]{2,1,0:T(8,128)(2,1)S(1)}, u32[]{:S(2)}) copy-start(bf16[2,512,1024]{2,1,0:T(8,128)(2,1)S(1)} %get-tuple-element.19) | copy-start | bytes 6291460
  145.5 3.7 %copy-start.11 = (bf16[1,2048,1024]{2,1,0:T(8,128)(2,1)S(1)}, bf16[1,2048,1024]{2,1,0:T(8,128)(2,1)}, u32[]{:S(2)}) copy-start(bf16[1,2048,1024]{2,1,0:T(8,128)(2,1)} %param.14) | copy-start | bytes 12582916
  153.0 32.4 %all-to-all-start.2 = ((bf16[64,8,2048]{2,1,0:T(8,128)(2,1)}), bf16[64,8,2048]{2,1,0:T(8,128)(2,1)S(1)}, u32[]{:S(2)}, u32[]{:S(2)}) async-start(bf16[64,8,2048]{2,1,0:T(8,128)(2,1)} %fusion.6), calls=%async_computation.2 | async-start | bytes 4194304 | tf_op jit(solution)/shard_map/all_to_all | solution.py:63
  163.7 6.6 %copy-start.6 = (bf16[2,512,1024]{2,1,0:T(8,128)(2,1)S(1)}, bf16[2,512,1024]{2,1,0:T(8,128)(2,1)}, u32[]{:S(2)}) copy-start(bf16[2,512,1024]{2,1,0:T(8,128)(2,1)} %constant_dynamic-slice_fusion) | copy-start | bytes 6291460
  163.7 6.6 %copy-start.16 = (bf16[2,512,1024]{2,1,0:T(8,128)(2,1)S(1)}, bf16[2,512,1024]{2,1,0:T(8,128)(2,1)}, u32[]{:S(2)}) copy-start(bf16[2,512,1024]{2,1,0:T(8,128)(2,1)} %copy-done.15) | copy-start | bytes 6291460
  170.3 4.0 %copy-start.14 = (bf16[2,512,1024]{2,1,0:T(8,128)(2,1)S(1)}, bf16[2,512,1024]{2,1,0:T(8,128)(2,1)}, u32[]{:S(2)}) copy-start(bf16[2,512,1024]{2,1,0:T(8,128)(2,1)} %copy-done.13) | copy-start | bytes 6291460
  174.3 12.8 %copy-start.1 = (bf16[256,2048]{1,0:T(8,128)(2,1)S(1)}, bf16[256,2048]{1,0:T(8,128)(2,1)}, u32[]{:S(2)}) copy-start(bf16[256,2048]{1,0:T(8,128)(2,1)} %param.8) | copy-start | bytes 3145732

commit v10 on v7

--- a/solution.py
+++ b/solution.py
@@ -44,14 +44,15 @@
     gate_sig = jax.nn.sigmoid(gate_pre)
     silu_g = gate_pre * gate_sig
     act = (silu_g * up_pre).astype(jnp.bfloat16)
-    gate_fac = up_pre * gate_sig * (1.0 + gate_pre * (1.0 - gate_sig))
+    gate_fac = (up_pre * gate_sig * (1.0 + gate_pre * (1.0 - gate_sig))).astype(jnp.bfloat16)
+    silu_g = silu_g.astype(jnp.bfloat16)
     x_half = lax.dynamic_slice_in_dim(recv_x, me * half, half, axis=2)
     recv_rg, gate_fac, silu_g, act, x_half = lax.optimization_barrier(
         (recv_rg, gate_fac, silu_g, act, x_half)
     )
     act_grad = jnp.einsum("srd,df->srf", recv_rg, wd, preferred_element_type=jnp.float32)
-    gate_grad = (act_grad * gate_fac).astype(jnp.bfloat16)
-    up_grad = (act_grad * silu_g).astype(jnp.bfloat16)
+    gate_grad = (act_grad * gate_fac.astype(jnp.float32)).astype(jnp.bfloat16)
+    up_grad = (act_grad * silu_g.astype(jnp.float32)).astype(jnp.bfloat16)
 
     gg_own = lax.dynamic_index_in_dim(gate_grad, me, 0, keepdims=False)
     ug_own = lax.dynamic_index_in_dim(up_grad, me, 0, keepdims=False)

time: 182 us -> 180 us (0.989)
  transfers between devices with their start and end apart: 3 -> 3, of which waited for: 3 -> 3; matrix products, arithmetic and copies ran while one was open for 25% -> 24% of each run, Pallas kernels for 0% -> 0%
where the time goes in v10:
time: 180 us
  waiting for transfers between devices  87.6 us (49%)
  matrix products  49.2 us (27%)
  starting transfers between devices  25.6 us (14%)
  local copies, waits for them, and re-layouts  11.3 us (6%)
  other arithmetic  5.13 us (3%)
    all_to_all x1, waiting for transfers between devices, per_device(): lax.all_to_all(send_x.reshape(dp_count * group, slot_count, width), axes,...  47.9 us
    all_to_all x1, waiting for transfers between devices, per_device(): lax.all_to_all(send_rg.reshape(dp_count * group, slot_count, width), axes...  33.1 us
    dot_general x3, matrix products, wgrad(): jnp.einsum('srd,srf->sdf', left, right, preferred_element_type=jnp.float32)  14.6 us
    all_to_all x1, starting transfers between devices, per_device(): lax.all_to_all(send_x.reshape(dp_count * group, slot_count, width), axes,...  12 us
    dot_general x1, matrix products, per_device(): jnp.einsum('srd,df->srf', recv_x, wgu, preferred_element_type=jnp.float32)  11.4 us
    dot_general x1, matrix products, per_device(): jnp.einsum('srd,df->srf', recv_rg, wd, preferred_element_type=jnp.float32)  8.84 us
    all_to_all x1, starting transfers between devices, per_device(): lax.all_to_all(send_rg.reshape(dp_count * group, slot_count, width), axes...  7.27 us
    all_to_all x1, waiting for transfers between devices, per_device(): lax.all_to_all(back.reshape(group, slot_count, width), ('seq', 'expert'),...  6.66 us
  transfers between devices with their start and end apart: 3, of which 3 were waited for; matrix products, arithmetic and copies ran while one was open for 24% of the time, Pallas kernels for 0%

profile of v10, /device:TPU:1, one launch (start us, length us, event | category | flops | bytes accessed | tf_op | source)
XLA Modules:
  0.0 179.7 jit_solution(5736518723267394660)
XLA Ops:
  0.6 0.0 copy-start
  0.7 0.8 multiply_add_fusion
  1.5 0.4 copy-done
  1.9 3.2 %convert_bitcast_fusion = bf16[128,8,2048]{2,1,0:T(8,128)(2,1)} fusion(bf16[256,2048]{1,0:T(8,128)(2,1)S(1)} %copy-done, s32[256]{0:T(256)S(1)} %bitcast.55, s32[256]{0:T(256)S(1)} %bitcast.52, s32[1024]{0:T(1024)S(1)} %get-tuple-element.23, s32[1024]{0:T(1024)S(1)} %get-tuple-element.24, pred[1024]{0:T(1024)(128)(4,1)S(1)} %fusion.31), kind=kOutput, calls=%fused_computation.16 | convolution fusion | flops 1076887552 | bytes 5254144 | tf_op jit(solution)/shard_map/dot_general | solution.py:27
  5.1 0.0 copy-start.3
  5.1 0.0 copy-start.7
  5.1 12.0 %all-to-all-start.1 = ((bf16[128,8,2048]{2,1,0:T(8,128)(2,1)}), bf16[128,8,2048]{2,1,0:T(8,128)(2,1)}, u32[]{:S(2)}, u32[]{:S(2)}) async-start(bf16[128,8,2048]{2,1,0:T(8,128)(2,1)} %convert_bitcast_fusion), calls=%async_computation.1 | async-start | bytes 8388608 | tf_op jit(solution)/shard_map/all_to_all | solution.py:32
  17.1 0.0 copy-done.3
  17.1 0.0 copy-done.7
  17.1 3.3 %convert_bitcast_fusion.1 = bf16[128,8,2048]{2,1,0:T(8,128)(2,1)} fusion(bf16[256,2048]{1,0:T(8,128)(2,1)S(1)} %copy-done.7, s32[256]{0:T(256)S(1)} %bitcast.56, s32[256]{0:T(256)S(1)} %bitcast.53, s32[1024]{0:T(1024)S(1)} %get-tuple-element.23, s32[1024]{0:T(1024)S(1)} %get-tuple-element.24, pred[1024]{0:T(1024)(128)(4,1)S(1)} %fusion.31, ...), kind=kOutput, calls=%fused_computation.17 | convolution fusion | flops 1077149696 | bytes 5255168 | tf_op jit(solution)/shard_map/dot_general | solution.py:28
  20.4 47.9 %all-to-all-done.1 = bf16[128,8,2048]{2,1,0:T(8,128)(2,1)} async-done(((bf16[128,8,2048]{2,1,0:T(8,128)(2,1)}), bf16[128,8,2048]{2,1,0:T(8,128)(2,1)}, u32[]{:S(2)}, u32[]{:S(2)}) %all-to-all-start.1) | async-done | bytes 4194336 | tf_op jit(solution)/shard_map/all_to_all | solution.py:32
  68.3 7.3 %all-to-all-start = ((bf16[128,8,2048]{2,1,0:T(8,128)(2,1)}), bf16[128,8,2048]{2,1,0:T(8,128)(2,1)}, u32[]{:S(2)}, u32[]{:S(2)}) async-start(bf16[128,8,2048]{2,1,0:T(8,128)(2,1)} %convert_bitcast_fusion.1), calls=%async_computation | async-start | bytes 8388608 | tf_op jit(solution)/shard_map/all_to_all | solution.py:35
  75.6 0.0 copy-start.4
  75.6 3.2 %constant_dynamic-slice_fusion = bf16[2,512,1024]{2,1,0:T(8,128)(2,1)} fusion(bf16[2,512,2048]{2,1,0:T(8,128)(2,1)} %bitcast.5, s32[]{:T(128)S(6)} %select_n.29), kind=kLoop, calls=%fused_computation.56 | loop fusion | bytes 4194308 | tf_op jit(solution)/shard_map/dynamic_slice | solution.py:49
  78.9 0.0 copy-done.4
  78.9 11.4 %fusion = f32[2,512,2048]{2,1,0:T(8,128)S(1)} fusion(bf16[2,512,2048]{2,1,0:T(8,128)(2,1)} %bitcast.5, bf16[2048,1024]{1,0:T(8,128)(2,1)} %bitcast.59, bf16[2048,1024]{1,0:T(8,128)(2,1)S(1)} %bitcast.58), kind=kOutput, calls=%fused_computation.1 | convolution fusion | flops 8606711808 | bytes 20971520 | tf_op jit(solution)/shard_map/srd,df->srf/dot_general | solution.py:42
  90.3 3.4 %multiply_convert_fusion.2 = (bf16[2,512,1024]{2,1,0:T(8,128)(2,1)}, bf16[2,512,1024]{2,1,0:T(8,128)(2,1)S(1)}, bf16[2,512,1024]{2,1,0:T(8,128)(2,1)}) fusion(f32[2,512,2048]{2,1,0:T(8,128)S(1)} %fusion), kind=kLoop, calls=%fused_computation.12 | loop fusion | flops 13631488 | bytes 14680064 | tf_op jit(solution)/shard_map/convert_element_type | solution.py:46
  93.7 33.1 %all-to-all-done = bf16[128,8,2048]{2,1,0:T(8,128)(2,1)} async-done(((bf16[128,8,2048]{2,1,0:T(8,128)(2,1)}), bf16[128,8,2048]{2,1,0:T(8,128)(2,1)}, u32[]{:S(2)}, u32[]{:S(2)}) %all-to-all-start) | async-done | bytes 4194336 | tf_op jit(solution)/shard_map/all_to_all | solution.py:35
  126.8 0.0 copy-start.5
  126.8 8.8 %multiply_convert_fusion = (bf16[2,512,1024]{2,1,0:T(8,128)(2,1)S(1)}, bf16[2,512,1024]{2,1,0:T(8,128)(2,1)S(1)}) fusion(bf16[2,512,1024]{2,1,0:T(8,128)(2,1)} %get-tuple-element.11, bf16[2,512,1024]{2,1,0:T(8,128)(2,1)S(1)} %get-tuple-element.10, bf16[2,512,2048]{2,1,0:T(8,128)(2,1)} %bitcast.3, bf16[1,2048,1024]{2,1,0:T(8,128)(2,1)} %param.15), kind=kOutput, calls=%fused_computation.10 | convolution fusion | flops 4301258752 | bytes 16777216 | tf_op jit(solution)/shard_map/srd,df->srf/dot_general | solution.py:53
  135.7 0.0 copy-start.8
  135.7 0.0 copy-start.10
  135.7 0.0 copy-done.5
  135.7 0.0 copy-start.6
  135.7 2.4 %fusion.13 = f32[512,2048]{1,0:T(8,128)S(1)} fusion(bf16[2,512,1024]{2,1,0:T(8,128)(2,1)S(1)} %get-tuple-element.20, s32[]{:T(128)S(6)} %select_n.30, bf16[1,2048,1024]{2,1,0:T(8,128)(2,1)S(1)} %copy-done.5), kind=kOutput, calls=%fused_computation.31 | convolution fusion | flops 2147483648 | bytes 9437188 | tf_op jit(solution)/shard_map/dot_general | solution.py:59
  138.1 0.0 copy-done.8
  138.1 0.0 copy-done.10
  138.1 1.3 copy-done.6
  139.4 3.7 %fusion.6 = bf16[64,8,2048]{2,1,0:T(8,128)(2,1)} fusion(f32[512,2048]{1,0:T(8,128)S(1)} %fusion.13, bf16[2,512,1024]{2,1,0:T(8,128)(2,1)S(1)} %get-tuple-element.19, s32[]{:T(128)S(6)} %select_n.30, bf16[1,2048,1024]{2,1,0:T(8,128)(2,1)S(1)} %copy-done.6), kind=kOutput, calls=%fused_computation.18 | convolution fusion | flops 2149580800 | bytes 11534340 | tf_op jit(solution)/shard_map/dot_general | solution.py:60
  143.1 6.4 %all-to-all-start.2 = ((bf16[64,8,2048]{2,1,0:T(8,128)(2,1)}), bf16[64,8,2048]{2,1,0:T(8,128)(2,1)S(1)}, u32[]{:S(2)}, u32[]{:S(2)}) async-start(bf16[64,8,2048]{2,1,0:T(8,128)(2,1)} %fusion.6), calls=%async_computation.2 | async-start | bytes 4194304 | tf_op jit(solution)/shard_map/all_to_all | solution.py:61
  149.5 0.9 fusion.10
  150.4 6.3 %copy.17 = bf16[2,512,2048]{1,2,0:T(8,128)(2,1)} copy(bf16[2,512,2048]{2,1,0:T(8,128)(2,1)} %bitcast.3) | data formatting | bytes 8388608 | tf_op jit(solution)/shard_map/optimization_barrier | solution.py:50
  156.7 0.0 copy-start.2
  156.7 0.0 copy-start.11
  156.7 6.6 %reduce-precision_reduce_fusion = bf16[1024,1024]{1,0:T(8,128)(2,1)} fusion(bf16[2,512,1024]{2,1,0:T(8,128)(2,1)} %get-tuple-element.13, bf16[2,512,2048]{1,2,0:T(8,128)(2,1)} %copy.17, s32[]{:T(128)S(6)} %select_n.29), kind=kOutput, calls=%fused_computation.4 | convolution fusion | flops 2150629376 | bytes 6291460 | tf_op jit(solution)/shard_map/srd,srf->sdf/dot_general | solution.py:68
  163.3 0.0 copy-done.2
  163.3 0.0 copy-done.11
  163.3 0.0 copy-start.9
  163.3 4.0 %reduce-precision_reduce_fusion.1 = bf16[1024,1024]{1,0:T(8,128)(2,1)} fusion(bf16[2,512,1024]{2,1,0:T(8,128)(2,1)S(1)} %copy-done.2, bf16[2,512,1024]{2,1,0:T(8,128)(2,1)S(1)} %copy-done.11), kind=kOutput, calls=%fused_computation.5 | convolution fusion | flops 2150629376 | bytes 6291456 | tf_op jit(solution)/shard_map/srd,srf->sdf/dot_general | solution.py:68
  167.3 0.0 copy-done.9
  167.3 0.0 copy-start.1
  167.3 4.0 %reduce-precision_reduce_fusion.2 = bf16[1024,1024]{1,0:T(8,128)(2,1)} fusion(bf16[2,512,1024]{2,1,0:T(8,128)(2,1)S(1)} %copy-done.2, bf16[2,512,1024]{2,1,0:T(8,128)(2,1)S(1)} %copy-done.9), kind=kOutput, calls=%fused_computation.6 | convolution fusion | flops 2150629376 | bytes 6291456 | tf_op jit(solution)/shard_map/srd,srf->sdf/dot_general | solution.py:68
  171.3 6.7 %all-to-all-done.2 = bf16[64,8,2048]{2,1,0:T(8,128)(2,1)S(1)} async-done(((bf16[64,8,2048]{2,1,0:T(8,128)(2,1)}), bf16[64,8,2048]{2,1,0:T(8,128)(2,1)S(1)}, u32[]{:S(2)}, u32[]{:S(2)}) %all-to-all-start.2) | async-done | bytes 2097184 | tf_op jit(solution)/shard_map/all_to_all | solution.py:61
  178.0 1.7 convolution_convert_fusion
  179.7 0.0 copy-done.1
  (4 shorter events, 0.0 us)
Async XLA Ops:
  0.6 1.3 copy-start
  5.1 12.0 %copy-start.3 = (bf16[256,2]{0,1:T(2,128)(2,1)S(1)}, bf16[256,2]{0,1:T(2,128)(2,1)}, u32[]{:S(2)}) copy-start(bf16[256,2]{0,1:T(2,128)(2,1)} %param.10) | copy-start | bytes 3076
  5.1 12.0 %copy-start.7 = (bf16[256,2048]{1,0:T(8,128)(2,1)S(1)}, bf16[256,2048]{1,0:T(8,128)(2,1)}, u32[]{:S(2)}) copy-start(bf16[256,2048]{1,0:T(8,128)(2,1)} %param.9) | copy-start | bytes 3145732
  5.1 63.2 %all-to-all-start.1 = ((bf16[128,8,2048]{2,1,0:T(8,128)(2,1)}), bf16[128,8,2048]{2,1,0:T(8,128)(2,1)}, u32[]{:S(2)}, u32[]{:S(2)}) async-start(bf16[128,8,2048]{2,1,0:T(8,128)(2,1)} %convert_bitcast_fusion), calls=%async_computation.1 | async-start | bytes 8388608 | tf_op jit(solution)/shard_map/all_to_all | solution.py:32
  68.3 58.5 %all-to-all-start = ((bf16[128,8,2048]{2,1,0:T(8,128)(2,1)}), bf16[128,8,2048]{2,1,0:T(8,128)(2,1)}, u32[]{:S(2)}, u32[]{:S(2)}) async-start(bf16[128,8,2048]{2,1,0:T(8,128)(2,1)} %convert_bitcast_fusion.1), calls=%async_computation | async-start | bytes 8388608 | tf_op jit(solution)/shard_map/all_to_all | solution.py:35
  75.6 3.3 %copy-start.4 = (bf16[1,2048,1024]{2,1,0:T(8,128)(2,1)S(1)}, bf16[1,2048,1024]{2,1,0:T(8,128)(2,1)}, u32[]{:S(2)}) copy-start(bf16[1,2048,1024]{2,1,0:T(8,128)(2,1)} %param.13) | copy-start | bytes 12582916
  126.8 8.9 %copy-start.5 = (bf16[1,2048,1024]{2,1,0:T(8,128)(2,1)S(1)}, bf16[1,2048,1024]{2,1,0:T(8,128)(2,1)}, u32[]{:S(2)}) copy-start(bf16[1,2048,1024]{2,1,0:T(8,128)(2,1)} %param.13) | copy-start | bytes 12582916
  135.7 2.4 %copy-start.8 = (bf16[2,512,1024]{2,1,0:T(8,128)(2,1)}, bf16[2,512,1024]{2,1,0:T(8,128)(2,1)S(1)}, u32[]{:S(2)}) copy-start(bf16[2,512,1024]{2,1,0:T(8,128)(2,1)S(1)} %get-tuple-element.20) | copy-start | bytes 6291460
  135.7 2.4 %copy-start.10 = (bf16[2,512,1024]{2,1,0:T(8,128)(2,1)}, bf16[2,512,1024]{2,1,0:T(8,128)(2,1)S(1)}, u32[]{:S(2)}) copy-start(bf16[2,512,1024]{2,1,0:T(8,128)(2,1)S(1)} %get-tuple-element.19) | copy-start | bytes 6291460
  135.7 3.7 %copy-start.6 = (bf16[1,2048,1024]{2,1,0:T(8,128)(2,1)S(1)}, bf16[1,2048,1024]{2,1,0:T(8,128)(2,1)}, u32[]{:S(2)}) copy-start(bf16[1,2048,1024]{2,1,0:T(8,128)(2,1)} %param.14) | copy-start | bytes 12582916
  143.1 34.9 %all-to-all-start.2 = ((bf16[64,8,2048]{2,1,0:T(8,128)(2,1)}), bf16[64,8,2048]{2,1,0:T(8,128)(2,1)S(1)}, u32[]{:S(2)}, u32[]{:S(2)}) async-start(bf16[64,8,2048]{2,1,0:T(8,128)(2,1)} %fusion.6), calls=%async_computation.2 | async-start | bytes 4194304 | tf_op jit(solution)/shard_map/all_to_all | solution.py:61
  156.7 6.6 %copy-start.2 = (bf16[2,512,1024]{2,1,0:T(8,128)(2,1)S(1)}, bf16[2,512,1024]{2,1,0:T(8,128)(2,1)}, u32[]{:S(2)}) copy-start(bf16[2,512,1024]{2,1,0:T(8,128)(2,1)} %constant_dynamic-slice_fusion) | copy-start | bytes 6291460
  156.7 6.6 %copy-start.11 = (bf16[2,512,1024]{2,1,0:T(8,128)(2,1)S(1)}, bf16[2,512,1024]{2,1,0:T(8,128)(2,1)}, u32[]{:S(2)}) copy-start(bf16[2,512,1024]{2,1,0:T(8,128)(2,1)} %copy-done.10) | copy-start | bytes 6291460
  163.3 4.0 %copy-start.9 = (bf16[2,512,1024]{2,1,0:T(8,128)(2,1)S(1)}, bf16[2,512,1024]{2,1,0:T(8,128)(2,1)}, u32[]{:S(2)}) copy-start(bf16[2,512,1024]{2,1,0:T(8,128)(2,1)} %copy-done.8) | copy-start | bytes 6291460
  167.3 12.4 %copy-start.1 = (bf16[256,2048]{1,0:T(8,128)(2,1)S(1)}, bf16[256,2048]{1,0:T(8,128)(2,1)}, u32[]{:S(2)}) copy-start(bf16[256,2048]{1,0:T(8,128)(2,1)} %param.8) | copy-start | bytes 3145732

commit v11 on v7

--- a/solution.py
+++ b/solution.py
@@ -45,13 +45,14 @@
     silu_g = gate_pre * gate_sig
     act = (silu_g * up_pre).astype(jnp.bfloat16)
     gate_fac = up_pre * gate_sig * (1.0 + gate_pre * (1.0 - gate_sig))
+    silu_g = silu_g.astype(jnp.bfloat16)
     x_half = lax.dynamic_slice_in_dim(recv_x, me * half, half, axis=2)
     recv_rg, gate_fac, silu_g, act, x_half = lax.optimization_barrier(
         (recv_rg, gate_fac, silu_g, act, x_half)
     )
     act_grad = jnp.einsum("srd,df->srf", recv_rg, wd, preferred_element_type=jnp.float32)
     gate_grad = (act_grad * gate_fac).astype(jnp.bfloat16)
-    up_grad = (act_grad * silu_g).astype(jnp.bfloat16)
+    up_grad = (act_grad * silu_g.astype(jnp.float32)).astype(jnp.bfloat16)
 
     gg_own = lax.dynamic_index_in_dim(gate_grad, me, 0, keepdims=False)
     ug_own = lax.dynamic_index_in_dim(up_grad, me, 0, keepdims=False)

time: 182 us -> 181 us (level)
  transfers between devices with their start and end apart: 3 -> 3, of which waited for: 3 -> 3; matrix products, arithmetic and copies ran while one was open for 25% -> 24% of each run, Pallas kernels for 0% -> 0%
where the time goes in v11:
time: 181 us; the launch traced here: 180 us
  waiting for transfers between devices  87 us (48%)
  matrix products  49.7 us (27%)
  starting transfers between devices  25.6 us (14%)
  local copies, waits for them, and re-layouts  11.3 us (6%)
  other arithmetic  5.71 us (3%)
    all_to_all x1, waiting for transfers between devices, per_device(): lax.all_to_all(send_x.reshape(dp_count * group, slot_count, width), axes,...  47.9 us
    all_to_all x1, waiting for transfers between devices, per_device(): lax.all_to_all(send_rg.reshape(dp_count * group, slot_count, width), axes...  32.5 us
    dot_general x3, matrix products, wgrad(): jnp.einsum('srd,srf->sdf', left, right, preferred_element_type=jnp.float32)  14.6 us
    all_to_all x1, starting transfers between devices, per_device(): lax.all_to_all(send_x.reshape(dp_count * group, slot_count, width), axes,...  12 us
    dot_general x1, matrix products, per_device(): jnp.einsum('srd,df->srf', recv_x, wgu, preferred_element_type=jnp.float32)  11.4 us
    dot_general x1, matrix products, per_device(): jnp.einsum('srd,df->srf', recv_rg, wd, preferred_element_type=jnp.float32)  9.32 us
    all_to_all x1, starting transfers between devices, per_device(): lax.all_to_all(send_rg.reshape(dp_count * group, slot_count, width), axes...  7.27 us
    all_to_all x1, waiting for transfers between devices, per_device(): lax.all_to_all(back.reshape(group, slot_count, width), ('seq', 'expert'),...  6.66 us
  transfers between devices with their start and end apart: 3, of which 3 were waited for; matrix products, arithmetic and copies ran while one was open for 24% of the time, Pallas kernels for 0%

profile of v11, /device:TPU:1, one launch (start us, length us, event | category | flops | bytes accessed | tf_op | source)
XLA Modules:
  0.0 180.2 jit_solution(3921840245088656648)
XLA Ops:
  0.6 0.0 copy-start
  0.7 0.8 multiply_add_fusion
  1.5 0.4 copy-done
  1.9 3.2 %convert_bitcast_fusion = bf16[128,8,2048]{2,1,0:T(8,128)(2,1)} fusion(bf16[256,2048]{1,0:T(8,128)(2,1)S(1)} %copy-done, s32[256]{0:T(256)S(1)} %bitcast.55, s32[256]{0:T(256)S(1)} %bitcast.52, s32[1024]{0:T(1024)S(1)} %get-tuple-element.23, s32[1024]{0:T(1024)S(1)} %get-tuple-element.24, pred[1024]{0:T(1024)(128)(4,1)S(1)} %fusion.31), kind=kOutput, calls=%fused_computation.16 | convolution fusion | flops 1076887552 | bytes 5254144 | tf_op jit(solution)/shard_map/dot_general | solution.py:27
  5.1 0.0 copy-start.3
  5.1 0.0 copy-start.7
  5.1 12.0 %all-to-all-start.1 = ((bf16[128,8,2048]{2,1,0:T(8,128)(2,1)}), bf16[128,8,2048]{2,1,0:T(8,128)(2,1)}, u32[]{:S(2)}, u32[]{:S(2)}) async-start(bf16[128,8,2048]{2,1,0:T(8,128)(2,1)} %convert_bitcast_fusion), calls=%async_computation.1 | async-start | bytes 8388608 | tf_op jit(solution)/shard_map/all_to_all | solution.py:32
  17.1 0.0 copy-done.3
  17.1 0.0 copy-done.7
  17.1 3.3 %convert_bitcast_fusion.1 = bf16[128,8,2048]{2,1,0:T(8,128)(2,1)} fusion(bf16[256,2048]{1,0:T(8,128)(2,1)S(1)} %copy-done.7, s32[256]{0:T(256)S(1)} %bitcast.56, s32[256]{0:T(256)S(1)} %bitcast.53, s32[1024]{0:T(1024)S(1)} %get-tuple-element.23, s32[1024]{0:T(1024)S(1)} %get-tuple-element.24, pred[1024]{0:T(1024)(128)(4,1)S(1)} %fusion.31, ...), kind=kOutput, calls=%fused_computation.17 | convolution fusion | flops 1077149696 | bytes 5255168 | tf_op jit(solution)/shard_map/dot_general | solution.py:28
  20.4 47.9 %all-to-all-done.1 = bf16[128,8,2048]{2,1,0:T(8,128)(2,1)} async-done(((bf16[128,8,2048]{2,1,0:T(8,128)(2,1)}), bf16[128,8,2048]{2,1,0:T(8,128)(2,1)}, u32[]{:S(2)}, u32[]{:S(2)}) %all-to-all-start.1) | async-done | bytes 4194336 | tf_op jit(solution)/shard_map/all_to_all | solution.py:32
  68.3 7.3 %all-to-all-start = ((bf16[128,8,2048]{2,1,0:T(8,128)(2,1)}), bf16[128,8,2048]{2,1,0:T(8,128)(2,1)}, u32[]{:S(2)}, u32[]{:S(2)}) async-start(bf16[128,8,2048]{2,1,0:T(8,128)(2,1)} %convert_bitcast_fusion.1), calls=%async_computation | async-start | bytes 8388608 | tf_op jit(solution)/shard_map/all_to_all | solution.py:35
  75.6 0.0 copy-start.4
  75.6 3.2 %constant_dynamic-slice_fusion = bf16[2,512,1024]{2,1,0:T(8,128)(2,1)} fusion(bf16[2,512,2048]{2,1,0:T(8,128)(2,1)} %bitcast.5, s32[]{:T(128)S(6)} %select_n.29), kind=kLoop, calls=%fused_computation.56 | loop fusion | bytes 4194308 | tf_op jit(solution)/shard_map/dynamic_slice | solution.py:49
  78.9 0.0 copy-done.4
  78.9 11.4 %fusion = f32[2,512,2048]{2,1,0:T(8,128)S(1)} fusion(bf16[2,512,2048]{2,1,0:T(8,128)(2,1)} %bitcast.5, bf16[2048,1024]{1,0:T(8,128)(2,1)} %bitcast.59, bf16[2048,1024]{1,0:T(8,128)(2,1)S(1)} %bitcast.58), kind=kOutput, calls=%fused_computation.1 | convolution fusion | flops 8606711808 | bytes 20971520 | tf_op jit(solution)/shard_map/srd,df->srf/dot_general | solution.py:42
  90.3 4.0 %multiply_convert_fusion.2 = (bf16[2,512,1024]{2,1,0:T(8,128)(2,1)}, f32[2,512,1024]{2,1,0:T(8,128)}, bf16[2,512,1024]{2,1,0:T(8,128)(2,1)S(1)}) fusion(f32[2,512,2048]{2,1,0:T(8,128)S(1)} %fusion), kind=kLoop, calls=%fused_computation.12 | loop fusion | flops 12582912 | bytes 16777216 | tf_op jit(solution)/shard_map/convert_element_type | solution.py:46
  94.3 32.5 %all-to-all-done = bf16[128,8,2048]{2,1,0:T(8,128)(2,1)} async-done(((bf16[128,8,2048]{2,1,0:T(8,128)(2,1)}), bf16[128,8,2048]{2,1,0:T(8,128)(2,1)}, u32[]{:S(2)}, u32[]{:S(2)}) %all-to-all-start) | async-done | bytes 4194336 | tf_op jit(solution)/shard_map/all_to_all | solution.py:35
  126.8 0.0 copy-start.5
  126.8 9.3 %multiply_convert_fusion = (bf16[2,512,1024]{2,1,0:T(8,128)(2,1)S(1)}, bf16[2,512,1024]{2,1,0:T(8,128)(2,1)S(1)}) fusion(bf16[2,512,1024]{2,1,0:T(8,128)(2,1)S(1)} %get-tuple-element.11, f32[2,512,1024]{2,1,0:T(8,128)} %get-tuple-element.10, bf16[2,512,2048]{2,1,0:T(8,128)(2,1)} %bitcast.3, bf16[1,2048,1024]{2,1,0:T(8,128)(2,1)} %param.15), kind=kOutput, calls=%fused_computation.10 | convolution fusion | flops 4300210176 | bytes 18874368 | tf_op jit(solution)/shard_map/srd,df->srf/dot_general | solution.py:53
  136.1 0.0 copy-start.8
  136.1 0.0 copy-start.10
  136.1 0.0 copy-done.5
  136.2 0.0 copy-start.6
  136.2 2.4 %fusion.13 = f32[512,2048]{1,0:T(8,128)S(1)} fusion(bf16[2,512,1024]{2,1,0:T(8,128)(2,1)S(1)} %get-tuple-element.20, s32[]{:T(128)S(6)} %select_n.30, bf16[1,2048,1024]{2,1,0:T(8,128)(2,1)S(1)} %copy-done.5), kind=kOutput, calls=%fused_computation.31 | convolution fusion | flops 2147483648 | bytes 9437188 | tf_op jit(solution)/shard_map/dot_general | solution.py:59
  138.6 0.0 copy-done.8
  138.6 0.0 copy-done.10
  138.6 1.3 copy-done.6
  139.9 3.7 %fusion.6 = bf16[64,8,2048]{2,1,0:T(8,128)(2,1)} fusion(f32[512,2048]{1,0:T(8,128)S(1)} %fusion.13, bf16[2,512,1024]{2,1,0:T(8,128)(2,1)S(1)} %get-tuple-element.19, s32[]{:T(128)S(6)} %select_n.30, bf16[1,2048,1024]{2,1,0:T(8,128)(2,1)S(1)} %copy-done.6), kind=kOutput, calls=%fused_computation.18 | convolution fusion | flops 2149580800 | bytes 11534340 | tf_op jit(solution)/shard_map/dot_general | solution.py:60
  143.6 6.4 %all-to-all-start.2 = ((bf16[64,8,2048]{2,1,0:T(8,128)(2,1)}), bf16[64,8,2048]{2,1,0:T(8,128)(2,1)S(1)}, u32[]{:S(2)}, u32[]{:S(2)}) async-start(bf16[64,8,2048]{2,1,0:T(8,128)(2,1)} %fusion.6), calls=%async_computation.2 | async-start | bytes 4194304 | tf_op jit(solution)/shard_map/all_to_all | solution.py:61
  150.0 0.9 fusion.10
  150.9 6.3 %copy.17 = bf16[2,512,2048]{1,2,0:T(8,128)(2,1)} copy(bf16[2,512,2048]{2,1,0:T(8,128)(2,1)} %bitcast.3) | data formatting | bytes 8388608 | tf_op jit(solution)/shard_map/optimization_barrier | solution.py:50
  157.2 0.0 copy-start.2
  157.2 0.0 copy-start.11
  157.2 6.6 %reduce-precision_reduce_fusion = bf16[1024,1024]{1,0:T(8,128)(2,1)} fusion(bf16[2,512,1024]{2,1,0:T(8,128)(2,1)} %get-tuple-element.13, bf16[2,512,2048]{1,2,0:T(8,128)(2,1)} %copy.17, s32[]{:T(128)S(6)} %select_n.29), kind=kOutput, calls=%fused_computation.4 | convolution fusion | flops 2150629376 | bytes 6291460 | tf_op jit(solution)/shard_map/srd,srf->sdf/dot_general | solution.py:68
  163.7 0.0 copy-done.2
  163.7 0.0 copy-done.11
  163.7 0.0 copy-start.9
  163.8 4.0 %reduce-precision_reduce_fusion.1 = bf16[1024,1024]{1,0:T(8,128)(2,1)} fusion(bf16[2,512,1024]{2,1,0:T(8,128)(2,1)S(1)} %copy-done.2, bf16[2,512,1024]{2,1,0:T(8,128)(2,1)S(1)} %copy-done.11), kind=kOutput, calls=%fused_computation.5 | convolution fusion | flops 2150629376 | bytes 6291456 | tf_op jit(solution)/shard_map/srd,srf->sdf/dot_general | solution.py:68
  167.8 0.0 copy-done.9
  167.8 0.0 copy-start.1
  167.8 4.0 %reduce-precision_reduce_fusion.2 = bf16[1024,1024]{1,0:T(8,128)(2,1)} fusion(bf16[2,512,1024]{2,1,0:T(8,128)(2,1)S(1)} %copy-done.2, bf16[2,512,1024]{2,1,0:T(8,128)(2,1)S(1)} %copy-done.9), kind=kOutput, calls=%fused_computation.6 | convolution fusion | flops 2150629376 | bytes 6291456 | tf_op jit(solution)/shard_map/srd,srf->sdf/dot_general | solution.py:68
  171.8 6.7 %all-to-all-done.2 = bf16[64,8,2048]{2,1,0:T(8,128)(2,1)S(1)} async-done(((bf16[64,8,2048]{2,1,0:T(8,128)(2,1)}), bf16[64,8,2048]{2,1,0:T(8,128)(2,1)S(1)}, u32[]{:S(2)}, u32[]{:S(2)}) %all-to-all-start.2) | async-done | bytes 2097184 | tf_op jit(solution)/shard_map/all_to_all | solution.py:61
  178.4 1.7 convolution_convert_fusion
  180.2 0.0 copy-done.1
  (4 shorter events, 0.0 us)
Async XLA Ops:
  0.6 1.3 copy-start
  5.1 12.0 %copy-start.3 = (bf16[256,2]{0,1:T(2,128)(2,1)S(1)}, bf16[256,2]{0,1:T(2,128)(2,1)}, u32[]{:S(2)}) copy-start(bf16[256,2]{0,1:T(2,128)(2,1)} %param.10) | copy-start | bytes 3076
  5.1 12.0 %copy-start.7 = (bf16[256,2048]{1,0:T(8,128)(2,1)S(1)}, bf16[256,2048]{1,0:T(8,128)(2,1)}, u32[]{:S(2)}) copy-start(bf16[256,2048]{1,0:T(8,128)(2,1)} %param.9) | copy-start | bytes 3145732
  5.1 63.2 %all-to-all-start.1 = ((bf16[128,8,2048]{2,1,0:T(8,128)(2,1)}), bf16[128,8,2048]{2,1,0:T(8,128)(2,1)}, u32[]{:S(2)}, u32[]{:S(2)}) async-start(bf16[128,8,2048]{2,1,0:T(8,128)(2,1)} %convert_bitcast_fusion), calls=%async_computation.1 | async-start | bytes 8388608 | tf_op jit(solution)/shard_map/all_to_all | solution.py:32
  68.3 58.5 %all-to-all-start = ((bf16[128,8,2048]{2,1,0:T(8,128)(2,1)}), bf16[128,8,2048]{2,1,0:T(8,128)(2,1)}, u32[]{:S(2)}, u32[]{:S(2)}) async-start(bf16[128,8,2048]{2,1,0:T(8,128)(2,1)} %convert_bitcast_fusion.1), calls=%async_computation | async-start | bytes 8388608 | tf_op jit(solution)/shard_map/all_to_all | solution.py:35
  75.6 3.3 %copy-start.4 = (bf16[1,2048,1024]{2,1,0:T(8,128)(2,1)S(1)}, bf16[1,2048,1024]{2,1,0:T(8,128)(2,1)}, u32[]{:S(2)}) copy-start(bf16[1,2048,1024]{2,1,0:T(8,128)(2,1)} %param.13) | copy-start | bytes 12582916
  126.8 9.3 %copy-start.5 = (bf16[1,2048,1024]{2,1,0:T(8,128)(2,1)S(1)}, bf16[1,2048,1024]{2,1,0:T(8,128)(2,1)}, u32[]{:S(2)}) copy-start(bf16[1,2048,1024]{2,1,0:T(8,128)(2,1)} %param.13) | copy-start | bytes 12582916
  136.1 2.4 %copy-start.8 = (bf16[2,512,1024]{2,1,0:T(8,128)(2,1)}, bf16[2,512,1024]{2,1,0:T(8,128)(2,1)S(1)}, u32[]{:S(2)}) copy-start(bf16[2,512,1024]{2,1,0:T(8,128)(2,1)S(1)} %get-tuple-element.20) | copy-start | bytes 6291460
  136.1 2.4 %copy-start.10 = (bf16[2,512,1024]{2,1,0:T(8,128)(2,1)}, bf16[2,512,1024]{2,1,0:T(8,128)(2,1)S(1)}, u32[]{:S(2)}) copy-start(bf16[2,512,1024]{2,1,0:T(8,128)(2,1)S(1)} %get-tuple-element.19) | copy-start | bytes 6291460
  136.2 3.7 %copy-start.6 = (bf16[1,2048,1024]{2,1,0:T(8,128)(2,1)S(1)}, bf16[1,2048,1024]{2,1,0:T(8,128)(2,1)}, u32[]{:S(2)}) copy-start(bf16[1,2048,1024]{2,1,0:T(8,128)(2,1)} %param.14) | copy-start | bytes 12582916
  143.6 34.9 %all-to-all-start.2 = ((bf16[64,8,2048]{2,1,0:T(8,128)(2,1)}), bf16[64,8,2048]{2,1,0:T(8,128)(2,1)S(1)}, u32[]{:S(2)}, u32[]{:S(2)}) async-start(bf16[64,8,2048]{2,1,0:T(8,128)(2,1)} %fusion.6), calls=%async_computation.2 | async-start | bytes 4194304 | tf_op jit(solution)/shard_map/all_to_all | solution.py:61
  157.2 6.6 %copy-start.2 = (bf16[2,512,1024]{2,1,0:T(8,128)(2,1)S(1)}, bf16[2,512,1024]{2,1,0:T(8,128)(2,1)}, u32[]{:S(2)}) copy-start(bf16[2,512,1024]{2,1,0:T(8,128)(2,1)} %constant_dynamic-slice_fusion) | copy-start | bytes 6291460
  157.2 6.6 %copy-start.11 = (bf16[2,512,1024]{2,1,0:T(8,128)(2,1)S(1)}, bf16[2,512,1024]{2,1,0:T(8,128)(2,1)}, u32[]{:S(2)}) copy-start(bf16[2,512,1024]{2,1,0:T(8,128)(2,1)} %copy-done.10) | copy-start | bytes 6291460
  163.7 4.0 %copy-start.9 = (bf16[2,512,1024]{2,1,0:T(8,128)(2,1)S(1)}, bf16[2,512,1024]{2,1,0:T(8,128)(2,1)}, u32[]{:S(2)}) copy-start(bf16[2,512,1024]{2,1,0:T(8,128)(2,1)} %copy-done.8) | copy-start | bytes 6291460
  167.8 12.4 %copy-start.1 = (bf16[256,2048]{1,0:T(8,128)(2,1)S(1)}, bf16[256,2048]{1,0:T(8,128)(2,1)}, u32[]{:S(2)}) copy-start(bf16[256,2048]{1,0:T(8,128)(2,1)} %param.8) | copy-start | bytes 3145732

commit v12 on v10

--- a/solution.py
+++ b/solution.py
@@ -45,14 +45,13 @@
     silu_g = gate_pre * gate_sig
     act = (silu_g * up_pre).astype(jnp.bfloat16)
     gate_fac = (up_pre * gate_sig * (1.0 + gate_pre * (1.0 - gate_sig))).astype(jnp.bfloat16)
-    silu_g = silu_g.astype(jnp.bfloat16)
     x_half = lax.dynamic_slice_in_dim(recv_x, me * half, half, axis=2)
     recv_rg, gate_fac, silu_g, act, x_half = lax.optimization_barrier(
         (recv_rg, gate_fac, silu_g, act, x_half)
     )
     act_grad = jnp.einsum("srd,df->srf", recv_rg, wd, preferred_element_type=jnp.float32)
     gate_grad = (act_grad * gate_fac.astype(jnp.float32)).astype(jnp.bfloat16)
-    up_grad = (act_grad * silu_g.astype(jnp.float32)).astype(jnp.bfloat16)
+    up_grad = (act_grad * silu_g).astype(jnp.bfloat16)
 
     gg_own = lax.dynamic_index_in_dim(gate_grad, me, 0, keepdims=False)
     ug_own = lax.dynamic_index_in_dim(up_grad, me, 0, keepdims=False)

time: 180 us -> 181 us (level)
  no operation moved by 1% of the time
where the time goes in v12:
time: 181 us; the launch traced here: 180 us
  waiting for transfers between devices  87.1 us (48%)
  matrix products  49.7 us (27%)
  starting transfers between devices  25.6 us (14%)
  local copies, waits for them, and re-layouts  11.3 us (6%)
  other arithmetic  5.58 us (3%)
    all_to_all x1, waiting for transfers between devices, per_device(): lax.all_to_all(send_x.reshape(dp_count * group, slot_count, width), axes,...  47.9 us
    all_to_all x1, waiting for transfers between devices, per_device(): lax.all_to_all(send_rg.reshape(dp_count * group, slot_count, width), axes...  32.6 us
    dot_general x3, matrix products, wgrad(): jnp.einsum('srd,srf->sdf', left, right, preferred_element_type=jnp.float32)  14.6 us
    all_to_all x1, starting transfers between devices, per_device(): lax.all_to_all(send_x.reshape(dp_count * group, slot_count, width), axes,...  12 us
    dot_general x1, matrix products, per_device(): jnp.einsum('srd,df->srf', recv_x, wgu, preferred_element_type=jnp.float32)  11.4 us
    dot_general x1, matrix products, per_device(): jnp.einsum('srd,df->srf', recv_rg, wd, preferred_element_type=jnp.float32)  9.32 us
    all_to_all x1, starting transfers between devices, per_device(): lax.all_to_all(send_rg.reshape(dp_count * group, slot_count, width), axes...  7.27 us
    all_to_all x1, waiting for transfers between devices, per_device(): lax.all_to_all(back.reshape(group, slot_count, width), ('seq', 'expert'),...  6.66 us
  transfers between devices with their start and end apart: 3, of which 3 were waited for; matrix products, arithmetic and copies ran while one was open for 24% of the time, Pallas kernels for 0%

profile of v12, /device:TPU:1, one launch (start us, length us, event | category | flops | bytes accessed | tf_op | source)
XLA Modules:
  0.0 180.2 jit_solution(10693655497480215245)
XLA Ops:
  0.6 0.0 copy-start
  0.7 0.8 multiply_add_fusion
  1.5 0.4 copy-done
  1.9 3.2 %convert_bitcast_fusion = bf16[128,8,2048]{2,1,0:T(8,128)(2,1)} fusion(bf16[256,2048]{1,0:T(8,128)(2,1)S(1)} %copy-done, s32[256]{0:T(256)S(1)} %bitcast.55, s32[256]{0:T(256)S(1)} %bitcast.52, s32[1024]{0:T(1024)S(1)} %get-tuple-element.23, s32[1024]{0:T(1024)S(1)} %get-tuple-element.24, pred[1024]{0:T(1024)(128)(4,1)S(1)} %fusion.30), kind=kOutput, calls=%fused_computation.16 | convolution fusion | flops 1076887552 | bytes 5254144 | tf_op jit(solution)/shard_map/dot_general | solution.py:27
  5.1 0.0 copy-start.3
  5.1 0.0 copy-start.7
  5.1 12.0 %all-to-all-start.1 = ((bf16[128,8,2048]{2,1,0:T(8,128)(2,1)}), bf16[128,8,2048]{2,1,0:T(8,128)(2,1)}, u32[]{:S(2)}, u32[]{:S(2)}) async-start(bf16[128,8,2048]{2,1,0:T(8,128)(2,1)} %convert_bitcast_fusion), calls=%async_computation.1 | async-start | bytes 8388608 | tf_op jit(solution)/shard_map/all_to_all | solution.py:32
  17.1 0.0 copy-done.3
  17.1 0.0 copy-done.7
  17.1 3.3 %convert_bitcast_fusion.1 = bf16[128,8,2048]{2,1,0:T(8,128)(2,1)} fusion(bf16[256,2048]{1,0:T(8,128)(2,1)S(1)} %copy-done.7, s32[256]{0:T(256)S(1)} %bitcast.56, s32[256]{0:T(256)S(1)} %bitcast.53, s32[1024]{0:T(1024)S(1)} %get-tuple-element.23, s32[1024]{0:T(1024)S(1)} %get-tuple-element.24, pred[1024]{0:T(1024)(128)(4,1)S(1)} %fusion.30, ...), kind=kOutput, calls=%fused_computation.17 | convolution fusion | flops 1077149696 | bytes 5255168 | tf_op jit(solution)/shard_map/dot_general | solution.py:28
  20.4 47.9 %all-to-all-done.1 = bf16[128,8,2048]{2,1,0:T(8,128)(2,1)} async-done(((bf16[128,8,2048]{2,1,0:T(8,128)(2,1)}), bf16[128,8,2048]{2,1,0:T(8,128)(2,1)}, u32[]{:S(2)}, u32[]{:S(2)}) %all-to-all-start.1) | async-done | bytes 4194336 | tf_op jit(solution)/shard_map/all_to_all | solution.py:32
  68.3 7.3 %all-to-all-start = ((bf16[128,8,2048]{2,1,0:T(8,128)(2,1)}), bf16[128,8,2048]{2,1,0:T(8,128)(2,1)}, u32[]{:S(2)}, u32[]{:S(2)}) async-start(bf16[128,8,2048]{2,1,0:T(8,128)(2,1)} %convert_bitcast_fusion.1), calls=%async_computation | async-start | bytes 8388608 | tf_op jit(solution)/shard_map/all_to_all | solution.py:35
  75.6 0.0 copy-start.4
  75.6 3.2 %constant_dynamic-slice_fusion = bf16[2,512,1024]{2,1,0:T(8,128)(2,1)} fusion(bf16[2,512,2048]{2,1,0:T(8,128)(2,1)} %bitcast.5, s32[]{:T(128)S(6)} %select_n.29), kind=kLoop, calls=%fused_computation.55 | loop fusion | bytes 4194308 | tf_op jit(solution)/shard_map/dynamic_slice | solution.py:48
  78.9 0.0 copy-done.4
  78.9 11.4 %fusion = f32[2,512,2048]{2,1,0:T(8,128)S(1)} fusion(bf16[2,512,2048]{2,1,0:T(8,128)(2,1)} %bitcast.5, bf16[2048,1024]{1,0:T(8,128)(2,1)} %bitcast.59, bf16[2048,1024]{1,0:T(8,128)(2,1)S(1)} %bitcast.58), kind=kOutput, calls=%fused_computation.1 | convolution fusion | flops 8606711808 | bytes 20971520 | tf_op jit(solution)/shard_map/srd,df->srf/dot_general | solution.py:42
  90.3 3.9 %multiply_convert_fusion.2 = (bf16[2,512,1024]{2,1,0:T(8,128)(2,1)}, bf16[2,512,1024]{2,1,0:T(8,128)(2,1)S(1)}, f32[2,512,1024]{2,1,0:T(8,128)}) fusion(f32[2,512,2048]{2,1,0:T(8,128)S(1)} %fusion), kind=kLoop, calls=%fused_computation.12 | loop fusion | flops 12582912 | bytes 16777216 | tf_op jit(solution)/shard_map/convert_element_type | solution.py:46
  94.2 32.6 %all-to-all-done = bf16[128,8,2048]{2,1,0:T(8,128)(2,1)} async-done(((bf16[128,8,2048]{2,1,0:T(8,128)(2,1)}), bf16[128,8,2048]{2,1,0:T(8,128)(2,1)}, u32[]{:S(2)}, u32[]{:S(2)}) %all-to-all-start) | async-done | bytes 4194336 | tf_op jit(solution)/shard_map/all_to_all | solution.py:35
  126.8 0.0 copy-start.5
  126.8 9.3 %multiply_convert_fusion = (bf16[2,512,1024]{2,1,0:T(8,128)(2,1)S(1)}, bf16[2,512,1024]{2,1,0:T(8,128)(2,1)S(1)}) fusion(f32[2,512,1024]{2,1,0:T(8,128)} %get-tuple-element.11, bf16[2,512,1024]{2,1,0:T(8,128)(2,1)S(1)} %get-tuple-element.10, bf16[2,512,2048]{2,1,0:T(8,128)(2,1)} %bitcast.3, bf16[1,2048,1024]{2,1,0:T(8,128)(2,1)} %param.15), kind=kOutput, calls=%fused_computation.10 | convolution fusion | flops 4300210176 | bytes 18874368 | tf_op jit(solution)/shard_map/srd,df->srf/dot_general | solution.py:52
  136.1 0.0 copy-start.8
  136.1 0.0 copy-start.10
  136.1 0.0 copy-done.5
  136.2 0.0 copy-start.6
  136.2 2.4 %fusion.13 = f32[512,2048]{1,0:T(8,128)S(1)} fusion(bf16[2,512,1024]{2,1,0:T(8,128)(2,1)S(1)} %get-tuple-element.20, s32[]{:T(128)S(6)} %select_n.30, bf16[1,2048,1024]{2,1,0:T(8,128)(2,1)S(1)} %copy-done.5), kind=kOutput, calls=%fused_computation.31 | convolution fusion | flops 2147483648 | bytes 9437188 | tf_op jit(solution)/shard_map/dot_general | solution.py:58
  138.6 0.0 copy-done.8
  138.6 0.0 copy-done.10
  138.6 1.3 copy-done.6
  139.9 3.7 %fusion.6 = bf16[64,8,2048]{2,1,0:T(8,128)(2,1)} fusion(f32[512,2048]{1,0:T(8,128)S(1)} %fusion.13, bf16[2,512,1024]{2,1,0:T(8,128)(2,1)S(1)} %get-tuple-element.19, s32[]{:T(128)S(6)} %select_n.30, bf16[1,2048,1024]{2,1,0:T(8,128)(2,1)S(1)} %copy-done.6), kind=kOutput, calls=%fused_computation.18 | convolution fusion | flops 2149580800 | bytes 11534340 | tf_op jit(solution)/shard_map/dot_general | solution.py:59
  143.6 6.4 %all-to-all-start.2 = ((bf16[64,8,2048]{2,1,0:T(8,128)(2,1)}), bf16[64,8,2048]{2,1,0:T(8,128)(2,1)S(1)}, u32[]{:S(2)}, u32[]{:S(2)}) async-start(bf16[64,8,2048]{2,1,0:T(8,128)(2,1)} %fusion.6), calls=%async_computation.2 | async-start | bytes 4194304 | tf_op jit(solution)/shard_map/all_to_all | solution.py:60
  150.0 0.9 fusion.10
  150.9 6.3 %copy.17 = bf16[2,512,2048]{1,2,0:T(8,128)(2,1)} copy(bf16[2,512,2048]{2,1,0:T(8,128)(2,1)} %bitcast.3) | data formatting | bytes 8388608 | tf_op jit(solution)/shard_map/optimization_barrier | solution.py:49
  157.2 0.0 copy-start.2
  157.2 0.0 copy-start.11
  157.2 6.6 %reduce-precision_reduce_fusion = bf16[1024,1024]{1,0:T(8,128)(2,1)} fusion(bf16[2,512,1024]{2,1,0:T(8,128)(2,1)} %get-tuple-element.13, bf16[2,512,2048]{1,2,0:T(8,128)(2,1)} %copy.17, s32[]{:T(128)S(6)} %select_n.29), kind=kOutput, calls=%fused_computation.4 | convolution fusion | flops 2150629376 | bytes 6291460 | tf_op jit(solution)/shard_map/srd,srf->sdf/dot_general | solution.py:67
  163.7 0.0 copy-done.2
  163.7 0.0 copy-done.11
  163.7 0.0 copy-start.9
  163.7 4.0 %reduce-precision_reduce_fusion.1 = bf16[1024,1024]{1,0:T(8,128)(2,1)} fusion(bf16[2,512,1024]{2,1,0:T(8,128)(2,1)S(1)} %copy-done.2, bf16[2,512,1024]{2,1,0:T(8,128)(2,1)S(1)} %copy-done.11), kind=kOutput, calls=%fused_computation.5 | convolution fusion | flops 2150629376 | bytes 6291456 | tf_op jit(solution)/shard_map/srd,srf->sdf/dot_general | solution.py:67
  167.8 0.0 copy-done.9
  167.8 0.0 copy-start.1
  167.8 4.0 %reduce-precision_reduce_fusion.2 = bf16[1024,1024]{1,0:T(8,128)(2,1)} fusion(bf16[2,512,1024]{2,1,0:T(8,128)(2,1)S(1)} %copy-done.2, bf16[2,512,1024]{2,1,0:T(8,128)(2,1)S(1)} %copy-done.9), kind=kOutput, calls=%fused_computation.6 | convolution fusion | flops 2150629376 | bytes 6291456 | tf_op jit(solution)/shard_map/srd,srf->sdf/dot_general | solution.py:67
  171.8 6.7 %all-to-all-done.2 = bf16[64,8,2048]{2,1,0:T(8,128)(2,1)S(1)} async-done(((bf16[64,8,2048]{2,1,0:T(8,128)(2,1)}), bf16[64,8,2048]{2,1,0:T(8,128)(2,1)S(1)}, u32[]{:S(2)}, u32[]{:S(2)}) %all-to-all-start.2) | async-done | bytes 2097184 | tf_op jit(solution)/shard_map/all_to_all | solution.py:60
  178.4 1.7 convolution_convert_fusion
  180.2 0.0 copy-done.1
  (4 shorter events, 0.0 us)
Async XLA Ops:
  0.6 1.3 copy-start
  5.1 12.0 %copy-start.3 = (bf16[256,2]{0,1:T(2,128)(2,1)S(1)}, bf16[256,2]{0,1:T(2,128)(2,1)}, u32[]{:S(2)}) copy-start(bf16[256,2]{0,1:T(2,128)(2,1)} %param.10) | copy-start | bytes 3076
  5.1 12.0 %copy-start.7 = (bf16[256,2048]{1,0:T(8,128)(2,1)S(1)}, bf16[256,2048]{1,0:T(8,128)(2,1)}, u32[]{:S(2)}) copy-start(bf16[256,2048]{1,0:T(8,128)(2,1)} %param.9) | copy-start | bytes 3145732
  5.1 63.2 %all-to-all-start.1 = ((bf16[128,8,2048]{2,1,0:T(8,128)(2,1)}), bf16[128,8,2048]{2,1,0:T(8,128)(2,1)}, u32[]{:S(2)}, u32[]{:S(2)}) async-start(bf16[128,8,2048]{2,1,0:T(8,128)(2,1)} %convert_bitcast_fusion), calls=%async_computation.1 | async-start | bytes 8388608 | tf_op jit(solution)/shard_map/all_to_all | solution.py:32
  68.3 58.5 %all-to-all-start = ((bf16[128,8,2048]{2,1,0:T(8,128)(2,1)}), bf16[128,8,2048]{2,1,0:T(8,128)(2,1)}, u32[]{:S(2)}, u32[]{:S(2)}) async-start(bf16[128,8,2048]{2,1,0:T(8,128)(2,1)} %convert_bitcast_fusion.1), calls=%async_computation | async-start | bytes 8388608 | tf_op jit(solution)/shard_map/all_to_all | solution.py:35
  75.6 3.3 %copy-start.4 = (bf16[1,2048,1024]{2,1,0:T(8,128)(2,1)S(1)}, bf16[1,2048,1024]{2,1,0:T(8,128)(2,1)}, u32[]{:S(2)}) copy-start(bf16[1,2048,1024]{2,1,0:T(8,128)(2,1)} %param.13) | copy-start | bytes 12582916
  126.8 9.3 %copy-start.5 = (bf16[1,2048,1024]{2,1,0:T(8,128)(2,1)S(1)}, bf16[1,2048,1024]{2,1,0:T(8,128)(2,1)}, u32[]{:S(2)}) copy-start(bf16[1,2048,1024]{2,1,0:T(8,128)(2,1)} %param.13) | copy-start | bytes 12582916
  136.1 2.4 %copy-start.8 = (bf16[2,512,1024]{2,1,0:T(8,128)(2,1)}, bf16[2,512,1024]{2,1,0:T(8,128)(2,1)S(1)}, u32[]{:S(2)}) copy-start(bf16[2,512,1024]{2,1,0:T(8,128)(2,1)S(1)} %get-tuple-element.20) | copy-start | bytes 6291460
  136.1 2.4 %copy-start.10 = (bf16[2,512,1024]{2,1,0:T(8,128)(2,1)}, bf16[2,512,1024]{2,1,0:T(8,128)(2,1)S(1)}, u32[]{:S(2)}) copy-start(bf16[2,512,1024]{2,1,0:T(8,128)(2,1)S(1)} %get-tuple-element.19) | copy-start | bytes 6291460
  136.2 3.7 %copy-start.6 = (bf16[1,2048,1024]{2,1,0:T(8,128)(2,1)S(1)}, bf16[1,2048,1024]{2,1,0:T(8,128)(2,1)}, u32[]{:S(2)}) copy-start(bf16[1,2048,1024]{2,1,0:T(8,128)(2,1)} %param.14) | copy-start | bytes 12582916
  143.6 34.9 %all-to-all-start.2 = ((bf16[64,8,2048]{2,1,0:T(8,128)(2,1)}), bf16[64,8,2048]{2,1,0:T(8,128)(2,1)S(1)}, u32[]{:S(2)}, u32[]{:S(2)}) async-start(bf16[64,8,2048]{2,1,0:T(8,128)(2,1)} %fusion.6), calls=%async_computation.2 | async-start | bytes 4194304 | tf_op jit(solution)/shard_map/all_to_all | solution.py:60
  157.2 6.6 %copy-start.2 = (bf16[2,512,1024]{2,1,0:T(8,128)(2,1)S(1)}, bf16[2,512,1024]{2,1,0:T(8,128)(2,1)}, u32[]{:S(2)}) copy-start(bf16[2,512,1024]{2,1,0:T(8,128)(2,1)} %constant_dynamic-slice_fusion) | copy-start | bytes 6291460
  157.2 6.6 %copy-start.11 = (bf16[2,512,1024]{2,1,0:T(8,128)(2,1)S(1)}, bf16[2,512,1024]{2,1,0:T(8,128)(2,1)}, u32[]{:S(2)}) copy-start(bf16[2,512,1024]{2,1,0:T(8,128)(2,1)} %copy-done.10) | copy-start | bytes 6291460
  163.7 4.0 %copy-start.9 = (bf16[2,512,1024]{2,1,0:T(8,128)(2,1)S(1)}, bf16[2,512,1024]{2,1,0:T(8,128)(2,1)}, u32[]{:S(2)}) copy-start(bf16[2,512,1024]{2,1,0:T(8,128)(2,1)} %copy-done.8) | copy-start | bytes 6291460
  167.8 12.4 %copy-start.1 = (bf16[256,2048]{1,0:T(8,128)(2,1)S(1)}, bf16[256,2048]{1,0:T(8,128)(2,1)}, u32[]{:S(2)}) copy-start(bf16[256,2048]{1,0:T(8,128)(2,1)} %param.8) | copy-start | bytes 3145732

commit v13 on v7

--- a/solution.py
+++ b/solution.py
@@ -53,10 +53,10 @@
     gate_grad = (act_grad * gate_fac).astype(jnp.bfloat16)
     up_grad = (act_grad * silu_g).astype(jnp.bfloat16)
 
-    gg_own = lax.dynamic_index_in_dim(gate_grad, me, 0, keepdims=False)
-    ug_own = lax.dynamic_index_in_dim(up_grad, me, 0, keepdims=False)
-    back = jnp.dot(gg_own, wg.T, preferred_element_type=jnp.float32)
-    back = (back + jnp.dot(ug_own, wu.T, preferred_element_type=jnp.float32)).astype(jnp.bfloat16)
+    gu_own = lax.dynamic_index_in_dim(
+        jnp.concatenate([gate_grad, up_grad], axis=-1), me, 0, keepdims=False
+    )
+    back = jnp.dot(gu_own, wgu.T, preferred_element_type=jnp.float32).astype(jnp.bfloat16)
     returned = lax.all_to_all(
         back.reshape(group, slot_count, width), ("seq", "expert"), 0, 0, tiled=True
     ).reshape(rows, width)

time: 182 us -> 182 us (level)
    dot_general x2 -> x1, matrix products: 6.09 us -> 5.88 us  [per_device(): jnp.dot(gu_own, wgu.T, preferred_element_type=jnp.float32)]
where the time goes in v13:
time: 182 us
  waiting for transfers between devices  85.6 us (47%)
  matrix products  51.1 us (28%)
  starting transfers between devices  25.6 us (14%)
  local copies, waits for them, and re-layouts  12 us (7%)
  other arithmetic  6.66 us (4%)
    all_to_all x1, waiting for transfers between devices, per_device(): lax.all_to_all(send_x.reshape(dp_count * group, slot_count, width), axes,...  47.9 us
    all_to_all x1, waiting for transfers between devices, per_device(): lax.all_to_all(send_rg.reshape(dp_count * group, slot_count, width), axes...  31 us
    dot_general x3, matrix products, wgrad(): jnp.einsum('srd,srf->sdf', left, right, preferred_element_type=jnp.float32)  14.6 us
    all_to_all x1, starting transfers between devices, per_device(): lax.all_to_all(send_x.reshape(dp_count * group, slot_count, width), axes,...  12 us
    dot_general x1, matrix products, per_device(): jnp.einsum('srd,df->srf', recv_x, wgu, preferred_element_type=jnp.float32)  11.9 us
    dot_general x1, matrix products, per_device(): jnp.einsum('srd,df->srf', recv_rg, wd, preferred_element_type=jnp.float32)  10.5 us
    all_to_all x1, starting transfers between devices, per_device(): lax.all_to_all(send_rg.reshape(dp_count * group, slot_count, width), axes...  7.29 us
    all_to_all x1, waiting for transfers between devices, per_device(): lax.all_to_all(back.reshape(group, slot_count, width), ('seq', 'expert'),...  6.67 us
  transfers between devices with their start and end apart: 3, of which 3 were waited for; matrix products, arithmetic and copies ran while one was open for 25% of the time, Pallas kernels for 0%

profile of v13, /device:TPU:1, one launch (start us, length us, event | category | flops | bytes accessed | tf_op | source)
XLA Modules:
  0.0 181.7 jit_solution(10451492975995047524)
XLA Ops:
  0.6 0.0 copy-start
  0.7 0.8 multiply_add_fusion
  1.5 0.4 copy-done
  1.9 3.2 %convert_bitcast_fusion = bf16[128,8,2048]{2,1,0:T(8,128)(2,1)} fusion(bf16[256,2048]{1,0:T(8,128)(2,1)S(1)} %copy-done, s32[256]{0:T(256)S(1)} %bitcast.48, s32[256]{0:T(256)S(1)} %bitcast.45, s32[1024]{0:T(1024)S(1)} %get-tuple-element.23, s32[1024]{0:T(1024)S(1)} %get-tuple-element.24, pred[1024]{0:T(1024)(128)(4,1)S(1)} %fusion.29), kind=kOutput, calls=%fused_computation.17 | convolution fusion | flops 1076887552 | bytes 5254144 | tf_op jit(solution)/shard_map/dot_general | solution.py:27
  5.1 0.0 copy-start.3
  5.1 0.0 copy-start.7
  5.1 12.0 %all-to-all-start.1 = ((bf16[128,8,2048]{2,1,0:T(8,128)(2,1)}), bf16[128,8,2048]{2,1,0:T(8,128)(2,1)}, u32[]{:S(2)}, u32[]{:S(2)}) async-start(bf16[128,8,2048]{2,1,0:T(8,128)(2,1)} %convert_bitcast_fusion), calls=%async_computation.1 | async-start | bytes 8388608 | tf_op jit(solution)/shard_map/all_to_all | solution.py:32
  17.1 0.0 copy-done.3
  17.1 0.0 copy-done.7
  17.1 3.3 %convert_bitcast_fusion.1 = bf16[128,8,2048]{2,1,0:T(8,128)(2,1)} fusion(bf16[256,2048]{1,0:T(8,128)(2,1)S(1)} %copy-done.7, s32[256]{0:T(256)S(1)} %bitcast.49, s32[256]{0:T(256)S(1)} %bitcast.46, s32[1024]{0:T(1024)S(1)} %get-tuple-element.23, s32[1024]{0:T(1024)S(1)} %get-tuple-element.24, pred[1024]{0:T(1024)(128)(4,1)S(1)} %fusion.29, ...), kind=kOutput, calls=%fused_computation.18 | convolution fusion | flops 1077149696 | bytes 5255168 | tf_op jit(solution)/shard_map/dot_general | solution.py:28
  20.4 47.9 %all-to-all-done.1 = bf16[128,8,2048]{2,1,0:T(8,128)(2,1)} async-done(((bf16[128,8,2048]{2,1,0:T(8,128)(2,1)}), bf16[128,8,2048]{2,1,0:T(8,128)(2,1)}, u32[]{:S(2)}, u32[]{:S(2)}) %all-to-all-start.1) | async-done | bytes 4194336 | tf_op jit(solution)/shard_map/all_to_all | solution.py:32
  68.3 7.3 %all-to-all-start = ((bf16[128,8,2048]{2,1,0:T(8,128)(2,1)}), bf16[128,8,2048]{2,1,0:T(8,128)(2,1)}, u32[]{:S(2)}, u32[]{:S(2)}) async-start(bf16[128,8,2048]{2,1,0:T(8,128)(2,1)} %convert_bitcast_fusion.1), calls=%async_computation | async-start | bytes 8388608 | tf_op jit(solution)/shard_map/all_to_all | solution.py:35
  75.6 0.0 copy-start.4
  75.6 3.2 %constant_dynamic-slice_fusion = bf16[2,512,1024]{2,1,0:T(8,128)(2,1)} fusion(bf16[2,512,2048]{2,1,0:T(8,128)(2,1)} %bitcast.5, s32[]{:T(128)S(6)} %select_n.28), kind=kLoop, calls=%fused_computation.53 | loop fusion | bytes 4194308 | tf_op jit(solution)/shard_map/dynamic_slice | solution.py:48
  78.9 0.0 copy-done.4
  78.9 11.9 %fusion = f32[2,512,2048]{2,1,0:T(8,128)S(1)} fusion(bf16[2,512,2048]{2,1,0:T(8,128)(2,1)} %bitcast.5, bf16[2048,1024]{1,0:T(8,128)(2,1)S(1)} %bitcast.51, bf16[2048,1024]{1,0:T(8,128)(2,1)} %bitcast.53), kind=kOutput, calls=%fused_computation.1 | convolution fusion | flops 8606711808 | bytes 20971520 | tf_op jit(solution)/shard_map/srd,df->srf/dot_general | solution.py:42
  90.8 5.0 %multiply_convert_fusion.2 = (bf16[2,512,1024]{2,1,0:T(8,128)(2,1)}, f32[2,512,1024]{2,1,0:T(8,128)}, f32[2,512,1024]{2,1,0:T(8,128)}) fusion(f32[2,512,2048]{2,1,0:T(8,128)S(1)} %fusion), kind=kLoop, calls=%fused_computation.13 | loop fusion | flops 11534336 | bytes 18874368 | tf_op jit(solution)/shard_map/convert_element_type | solution.py:46
  95.8 31.0 %all-to-all-done = bf16[128,8,2048]{2,1,0:T(8,128)(2,1)} async-done(((bf16[128,8,2048]{2,1,0:T(8,128)(2,1)}), bf16[128,8,2048]{2,1,0:T(8,128)(2,1)}, u32[]{:S(2)}, u32[]{:S(2)}) %all-to-all-start) | async-done | bytes 4194336 | tf_op jit(solution)/shard_map/all_to_all | solution.py:35
  126.8 0.0 copy-start.5
  126.8 0.0 copy-start.6
  126.8 10.5 %multiply_convert_fusion = (bf16[2,512,1024]{2,1,0:T(8,128)(2,1)S(1)}, bf16[2,512,1024]{2,1,0:T(8,128)(2,1)S(1)}) fusion(f32[2,512,1024]{2,1,0:T(8,128)} %get-tuple-element.11, f32[2,512,1024]{2,1,0:T(8,128)} %get-tuple-element.10, bf16[2,512,2048]{2,1,0:T(8,128)(2,1)} %bitcast.3, bf16[1,2048,1024]{2,1,0:T(8,128)(2,1)} %param.15), kind=kOutput, calls=%fused_computation.11 | convolution fusion | flops 4299161600 | bytes 20971520 | tf_op jit(solution)/shard_map/srd,df->srf/dot_general | solution.py:52
  137.3 0.0 copy-start.8
  137.3 0.0 copy-start.10
  137.3 1.3 copy-done.8
  138.7 0.6 copy-done.10
  139.2 0.0 copy-done.5
  139.2 0.0 copy-done.6
  139.2 5.9 %fusion.7 = bf16[64,8,2048]{2,1,0:T(8,128)(2,1)} fusion(bf16[2048,1024]{1,0:T(8,128)(2,1)S(1)} %bitcast.52, bf16[2048,1024]{1,0:T(8,128)(2,1)S(1)} %bitcast.54, s32[]{:T(128)S(6)} %select_n.29, bf16[2,512,1024]{2,1,0:T(8,128)(2,1)S(1)} %get-tuple-element.20, bf16[2,512,1024]{2,1,0:T(8,128)(2,1)S(1)} %get-tuple-element.19), kind=kOutput, calls=%fused_computation.20 | convolution fusion | flops 4316987392 | bytes 14680068 | tf_op jit(solution)/shard_map/dot_general | solution.py:59
  145.1 6.4 %all-to-all-start.2 = ((bf16[64,8,2048]{2,1,0:T(8,128)(2,1)}), bf16[64,8,2048]{2,1,0:T(8,128)(2,1)S(1)}, u32[]{:S(2)}, u32[]{:S(2)}) async-start(bf16[64,8,2048]{2,1,0:T(8,128)(2,1)} %fusion.7), calls=%async_computation.2 | async-start | bytes 4194304 | tf_op jit(solution)/shard_map/all_to_all | solution.py:60
  151.5 0.9 fusion.14
  152.4 6.3 %copy.17 = bf16[2,512,2048]{1,2,0:T(8,128)(2,1)} copy(bf16[2,512,2048]{2,1,0:T(8,128)(2,1)} %bitcast.3) | data formatting | bytes 8388608 | tf_op jit(solution)/shard_map/optimization_barrier | solution.py:49
  158.7 0.0 copy-start.2
  158.7 0.0 copy-start.11
  158.7 6.6 %reduce-precision_reduce_fusion = bf16[1024,1024]{1,0:T(8,128)(2,1)} fusion(bf16[2,512,1024]{2,1,0:T(8,128)(2,1)} %get-tuple-element.13, bf16[2,512,2048]{1,2,0:T(8,128)(2,1)} %copy.17, s32[]{:T(128)S(6)} %select_n.28), kind=kOutput, calls=%fused_computation.3 | convolution fusion | flops 2150629376 | bytes 6291460 | tf_op jit(solution)/shard_map/srd,srf->sdf/dot_general | solution.py:67
  165.3 0.0 copy-done.2
  165.3 0.0 copy-done.11
  165.3 0.0 copy-start.9
  165.3 4.0 %reduce-precision_reduce_fusion.1 = bf16[1024,1024]{1,0:T(8,128)(2,1)} fusion(bf16[2,512,1024]{2,1,0:T(8,128)(2,1)S(1)} %copy-done.2, bf16[2,512,1024]{2,1,0:T(8,128)(2,1)S(1)} %copy-done.11), kind=kOutput, calls=%fused_computation.4 | convolution fusion | flops 2150629376 | bytes 6291456 | tf_op jit(solution)/shard_map/srd,srf->sdf/dot_general | solution.py:67
  169.3 0.0 copy-done.9
  169.3 0.0 copy-start.1
  169.3 4.0 %reduce-precision_reduce_fusion.2 = bf16[1024,1024]{1,0:T(8,128)(2,1)} fusion(bf16[2,512,1024]{2,1,0:T(8,128)(2,1)S(1)} %copy-done.2, bf16[2,512,1024]{2,1,0:T(8,128)(2,1)S(1)} %copy-done.9), kind=kOutput, calls=%fused_computation.5 | convolution fusion | flops 2150629376 | bytes 6291456 | tf_op jit(solution)/shard_map/srd,srf->sdf/dot_general | solution.py:67
  173.3 6.7 %all-to-all-done.2 = bf16[64,8,2048]{2,1,0:T(8,128)(2,1)S(1)} async-done(((bf16[64,8,2048]{2,1,0:T(8,128)(2,1)}), bf16[64,8,2048]{2,1,0:T(8,128)(2,1)S(1)}, u32[]{:S(2)}, u32[]{:S(2)}) %all-to-all-start.2) | async-done | bytes 2097184 | tf_op jit(solution)/shard_map/all_to_all | solution.py:60
  180.0 1.7 convolution_convert_fusion
  181.7 0.0 copy-done.1
  (4 shorter events, 0.0 us)
Async XLA Ops:
  0.6 1.3 copy-start
  5.1 12.0 %copy-start.3 = (bf16[256,2]{0,1:T(2,128)(2,1)S(1)}, bf16[256,2]{0,1:T(2,128)(2,1)}, u32[]{:S(2)}) copy-start(bf16[256,2]{0,1:T(2,128)(2,1)} %param.10) | copy-start | bytes 3076
  5.1 12.0 %copy-start.7 = (bf16[256,2048]{1,0:T(8,128)(2,1)S(1)}, bf16[256,2048]{1,0:T(8,128)(2,1)}, u32[]{:S(2)}) copy-start(bf16[256,2048]{1,0:T(8,128)(2,1)} %param.9) | copy-start | bytes 3145732
  5.1 63.2 %all-to-all-start.1 = ((bf16[128,8,2048]{2,1,0:T(8,128)(2,1)}), bf16[128,8,2048]{2,1,0:T(8,128)(2,1)}, u32[]{:S(2)}, u32[]{:S(2)}) async-start(bf16[128,8,2048]{2,1,0:T(8,128)(2,1)} %convert_bitcast_fusion), calls=%async_computation.1 | async-start | bytes 8388608 | tf_op jit(solution)/shard_map/all_to_all | solution.py:32
  68.3 58.5 %all-to-all-start = ((bf16[128,8,2048]{2,1,0:T(8,128)(2,1)}), bf16[128,8,2048]{2,1,0:T(8,128)(2,1)}, u32[]{:S(2)}, u32[]{:S(2)}) async-start(bf16[128,8,2048]{2,1,0:T(8,128)(2,1)} %convert_bitcast_fusion.1), calls=%async_computation | async-start | bytes 8388608 | tf_op jit(solution)/shard_map/all_to_all | solution.py:35
  75.6 3.3 %copy-start.4 = (bf16[1,2048,1024]{2,1,0:T(8,128)(2,1)S(1)}, bf16[1,2048,1024]{2,1,0:T(8,128)(2,1)}, u32[]{:S(2)}) copy-start(bf16[1,2048,1024]{2,1,0:T(8,128)(2,1)} %param.14) | copy-start | bytes 12582916
  126.8 12.4 %copy-start.5 = (bf16[1,2048,1024]{2,1,0:T(8,128)(2,1)S(1)}, bf16[1,2048,1024]{2,1,0:T(8,128)(2,1)}, u32[]{:S(2)}) copy-start(bf16[1,2048,1024]{2,1,0:T(8,128)(2,1)} %param.14) | copy-start | bytes 12582916
  126.8 12.4 %copy-start.6 = (bf16[1,2048,1024]{2,1,0:T(8,128)(2,1)S(1)}, bf16[1,2048,1024]{2,1,0:T(8,128)(2,1)}, u32[]{:S(2)}) copy-start(bf16[1,2048,1024]{2,1,0:T(8,128)(2,1)} %param.13) | copy-start | bytes 12582916
  137.3 1.4 copy-start.8
  137.3 1.9 %copy-start.10 = (bf16[2,512,1024]{2,1,0:T(8,128)(2,1)}, bf16[2,512,1024]{2,1,0:T(8,128)(2,1)S(1)}, u32[]{:S(2)}) copy-start(bf16[2,512,1024]{2,1,0:T(8,128)(2,1)S(1)} %get-tuple-element.19) | copy-start | bytes 6291460
  145.1 34.9 %all-to-all-start.2 = ((bf16[64,8,2048]{2,1,0:T(8,128)(2,1)}), bf16[64,8,2048]{2,1,0:T(8,128)(2,1)S(1)}, u32[]{:S(2)}, u32[]{:S(2)}) async-start(bf16[64,8,2048]{2,1,0:T(8,128)(2,1)} %fusion.7), calls=%async_computation.2 | async-start | bytes 4194304 | tf_op jit(solution)/shard_map/all_to_all | solution.py:60
  158.7 6.6 %copy-start.2 = (bf16[2,512,1024]{2,1,0:T(8,128)(2,1)S(1)}, bf16[2,512,1024]{2,1,0:T(8,128)(2,1)}, u32[]{:S(2)}) copy-start(bf16[2,512,1024]{2,1,0:T(8,128)(2,1)} %constant_dynamic-slice_fusion) | copy-start | bytes 6291460
  158.7 6.6 %copy-start.11 = (bf16[2,512,1024]{2,1,0:T(8,128)(2,1)S(1)}, bf16[2,512,1024]{2,1,0:T(8,128)(2,1)}, u32[]{:S(2)}) copy-start(bf16[2,512,1024]{2,1,0:T(8,128)(2,1)} %copy-done.10) | copy-start | bytes 6291460
  165.3 4.0 %copy-start.9 = (bf16[2,512,1024]{2,1,0:T(8,128)(2,1)S(1)}, bf16[2,512,1024]{2,1,0:T(8,128)(2,1)}, u32[]{:S(2)}) copy-start(bf16[2,512,1024]{2,1,0:T(8,128)(2,1)} %copy-done.8) | copy-start | bytes 6291460
  169.3 12.4 %copy-start.1 = (bf16[256,2048]{1,0:T(8,128)(2,1)S(1)}, bf16[256,2048]{1,0:T(8,128)(2,1)}, u32[]{:S(2)}) copy-start(bf16[256,2048]{1,0:T(8,128)(2,1)} %param.8) | copy-start | bytes 3145732

commit v14 on v7

--- a/solution.py
+++ b/solution.py
@@ -24,7 +24,8 @@
     hit1 = slots == position[None, :, 1]
     pick = (hit0 | hit1).astype(jnp.bfloat16)
     weigh = jnp.where(hit0, route_weights[None, :, 0], jnp.where(hit1, route_weights[None, :, 1], 0))
-    send_x = jnp.dot(pick, tokens, preferred_element_type=jnp.float32).astype(jnp.bfloat16)
+    rows_x = jnp.dot(pick[:rows], tokens, preferred_element_type=jnp.float32).astype(jnp.bfloat16)
+    send_x = jnp.broadcast_to(rows_x[None], (dp_count, rows, width))
     send_rg = jnp.dot(weigh.astype(jnp.bfloat16), grad_out, preferred_element_type=jnp.float32).astype(
         jnp.bfloat16
     )

time: 182 us -> 186 us (1.022)
  local copies, waits for them, and re-layouts: 11.3 us -> 14.1 us
  waiting for transfers between devices: 86.1 us -> 88.2 us
    broadcast_in_dim x0 -> x1, local copies, waits for them, and re-layouts: none -> 2.48 us  [per_device(): send_x = jnp.broadcast_to(rows_x[None], (dp_count, rows, width))]
  transfers between devices with their start and end apart: 3 -> 3, of which waited for: 3 -> 3; matrix products, arithmetic and copies ran while one was open for 25% -> 23% of each run, Pallas kernels for 0% -> 0%
where the time goes in v14:
time: 186 us
  waiting for transfers between devices  88.2 us (47%)
  matrix products  50.7 us (27%)
  starting transfers between devices  25.8 us (14%)
  local copies, waits for them, and re-layouts  14.1 us (8%)
  other arithmetic  6.04 us (3%)
    all_to_all x1, waiting for transfers between devices, per_device(): lax.all_to_all(send_x.reshape(dp_count * group, slot_count, width), axes,...  47.9 us
    all_to_all x1, waiting for transfers between devices, per_device(): lax.all_to_all(send_rg.reshape(dp_count * group, slot_count, width), axes...  32.2 us
    dot_general x3, matrix products, wgrad(): jnp.einsum('srd,srf->sdf', left, right, preferred_element_type=jnp.float32)  14 us
    all_to_all x1, starting transfers between devices, per_device(): lax.all_to_all(send_x.reshape(dp_count * group, slot_count, width), axes,...  12 us
    dot_general x1, matrix products, per_device(): jnp.einsum('srd,df->srf', recv_x, wgu, preferred_element_type=jnp.float32)  11.4 us
    dot_general x1, matrix products, per_device(): jnp.einsum('srd,df->srf', recv_rg, wd, preferred_element_type=jnp.float32)  10.5 us
    all_to_all x1, waiting for transfers between devices, per_device(): lax.all_to_all(back.reshape(group, slot_count, width), ('seq', 'expert'),...  8.1 us
    all_to_all x1, starting transfers between devices, per_device(): lax.all_to_all(send_rg.reshape(dp_count * group, slot_count, width), axes...  7.27 us
  transfers between devices with their start and end apart: 3, of which 3 were waited for; matrix products, arithmetic and copies ran while one was open for 23% of the time, Pallas kernels for 0%

profile of v14, /device:TPU:1, one launch (start us, length us, event | category | flops | bytes accessed | tf_op | source)
XLA Modules:
  0.0 185.6 jit_solution(15169866657020601367)
XLA Ops:
  0.6 0.0 copy-start
  0.7 0.8 multiply_add_fusion
  1.5 0.9 select_compare_fusion.1
  2.4 0.0 copy-start.3
  2.4 0.7 copy-done.3
  3.1 2.0 %convolution_convert_fusion = bf16[512,2048]{1,0:T(8,128)(2,1)S(1)} fusion(bf16[256,2048]{1,0:T(8,128)(2,1)} %param.8, pred[1024,256]{1,0:T(32,128)(4,1)S(1)} %get-tuple-element.22, pred[1024,256]{1,0:T(32,128)(4,1)S(1)} %get-tuple-element.21), kind=kOutput, calls=%fused_computation.17 | convolution fusion | flops 538050560 | bytes 3407872 | tf_op jit(solution)/shard_map/dot_general | solution.py:27
  5.1 2.5 %broadcast_in_dim.38 = bf16[2,512,2048]{2,1,0:T(8,128)(2,1)} broadcast(bf16[512,2048]{1,0:T(8,128)(2,1)S(1)} %convolution_convert_fusion), dimensions={1,2} | broadcast | bytes 6291456 | tf_op jit(solution)/shard_map/broadcast_in_dim | solution.py:28
  7.6 0.0 copy-start.5
  7.6 12.0 %all-to-all-start.1 = ((bf16[128,8,2048]{2,1,0:T(8,128)(2,1)}), bf16[128,8,2048]{2,1,0:T(8,128)(2,1)}, u32[]{:S(2)}, u32[]{:S(2)}) async-start(bf16[128,8,2048]{2,1,0:T(8,128)(2,1)} %bitcast.51), calls=%async_computation.1 | async-start | bytes 8388608 | tf_op jit(solution)/shard_map/all_to_all | solution.py:33
  19.6 0.0 copy-done.5
  19.6 0.0 copy-done
  19.6 3.3 %convert_bitcast_fusion = bf16[128,8,2048]{2,1,0:T(8,128)(2,1)} fusion(bf16[256,2048]{1,0:T(8,128)(2,1)S(1)} %copy-done, bf16[256]{0:T(256)(128)(2,1)S(1)} %get-tuple-element.15, bf16[256]{0:T(256)(128)(2,1)S(1)} %get-tuple-element.14, s32[256]{0:T(256)S(1)} %bitcast.55, s32[1024]{0:T(1024)S(1)} %get-tuple-element.25, s32[1024]{0:T(1024)S(1)} %get-tuple-element.26, ...), kind=kOutput, calls=%fused_computation.16 | convolution fusion | flops 1077149696 | bytes 5255168 | tf_op jit(solution)/shard_map/dot_general | solution.py:29
  22.9 47.9 %all-to-all-done.1 = bf16[128,8,2048]{2,1,0:T(8,128)(2,1)} async-done(((bf16[128,8,2048]{2,1,0:T(8,128)(2,1)}), bf16[128,8,2048]{2,1,0:T(8,128)(2,1)}, u32[]{:S(2)}, u32[]{:S(2)}) %all-to-all-start.1) | async-done | bytes 4194336 | tf_op jit(solution)/shard_map/all_to_all | solution.py:33
  70.8 7.3 %all-to-all-start = ((bf16[128,8,2048]{2,1,0:T(8,128)(2,1)}), bf16[128,8,2048]{2,1,0:T(8,128)(2,1)}, u32[]{:S(2)}, u32[]{:S(2)}) async-start(bf16[128,8,2048]{2,1,0:T(8,128)(2,1)} %convert_bitcast_fusion), calls=%async_computation | async-start | bytes 8388608 | tf_op jit(solution)/shard_map/all_to_all | solution.py:36
  78.1 0.0 copy-start.6
  78.1 3.2 %constant_dynamic-slice_fusion = bf16[2,512,1024]{2,1,0:T(8,128)(2,1)} fusion(bf16[2,512,2048]{2,1,0:T(8,128)(2,1)} %bitcast.5, s32[]{:T(128)S(6)} %select_n.29), kind=kLoop, calls=%fused_computation.49 | loop fusion | bytes 4194308 | tf_op jit(solution)/shard_map/dynamic_slice | solution.py:49
  81.3 0.0 copy-done.6
  81.3 11.4 %fusion = f32[2,512,2048]{2,1,0:T(8,128)S(1)} fusion(bf16[2,512,2048]{2,1,0:T(8,128)(2,1)} %bitcast.5, bf16[2048,1024]{1,0:T(8,128)(2,1)} %bitcast.57, bf16[2048,1024]{1,0:T(8,128)(2,1)S(1)} %bitcast.56), kind=kOutput, calls=%fused_computation.1 | convolution fusion | flops 8606711808 | bytes 20971520 | tf_op jit(solution)/shard_map/srd,df->srf/dot_general | solution.py:43
  92.8 4.3 %multiply_convert_fusion.2 = (bf16[2,512,1024]{2,1,0:T(8,128)(2,1)S(1)}, f32[2,512,1024]{2,1,0:T(8,128)}, f32[2,512,1024]{2,1,0:T(8,128)}) fusion(f32[2,512,2048]{2,1,0:T(8,128)S(1)} %fusion), kind=kLoop, calls=%fused_computation.12 | loop fusion | flops 11534336 | bytes 18874368 | tf_op jit(solution)/shard_map/convert_element_type | solution.py:47
  97.1 32.2 %all-to-all-done = bf16[128,8,2048]{2,1,0:T(8,128)(2,1)} async-done(((bf16[128,8,2048]{2,1,0:T(8,128)(2,1)}), bf16[128,8,2048]{2,1,0:T(8,128)(2,1)}, u32[]{:S(2)}, u32[]{:S(2)}) %all-to-all-start) | async-done | bytes 4194336 | tf_op jit(solution)/shard_map/all_to_all | solution.py:36
  129.3 0.0 copy-start.7
  129.3 10.5 %multiply_convert_fusion = (bf16[2,512,1024]{2,1,0:T(8,128)(2,1)S(1)}, bf16[2,512,1024]{2,1,0:T(8,128)(2,1)S(1)}) fusion(f32[2,512,1024]{2,1,0:T(8,128)} %get-tuple-element.11, f32[2,512,1024]{2,1,0:T(8,128)} %get-tuple-element.10, bf16[2,512,2048]{2,1,0:T(8,128)(2,1)} %bitcast.3, bf16[1,2048,1024]{2,1,0:T(8,128)(2,1)} %param.15), kind=kOutput, calls=%fused_computation.10 | convolution fusion | flops 4299161600 | bytes 20971520 | tf_op jit(solution)/shard_map/srd,df->srf/dot_general | solution.py:53
  139.7 0.0 copy-start.9
  139.8 0.0 copy-start.11
  139.8 0.0 copy-done.7
  139.8 0.0 copy-start.8
  139.8 2.4 %fusion.10 = f32[512,2048]{1,0:T(8,128)S(1)} fusion(bf16[2,512,1024]{2,1,0:T(8,128)(2,1)S(1)} %get-tuple-element.20, s32[]{:T(128)S(6)} %select_n.30, bf16[1,2048,1024]{2,1,0:T(8,128)(2,1)S(1)} %copy-done.7), kind=kOutput, calls=%fused_computation.28 | convolution fusion | flops 2147483648 | bytes 9437188 | tf_op jit(solution)/shard_map/dot_general | solution.py:59
  142.2 0.0 copy-done.9
  142.2 0.0 copy-done.11
  142.2 1.3 copy-done.8
  143.5 3.7 %fusion.6 = bf16[64,8,2048]{2,1,0:T(8,128)(2,1)} fusion(f32[512,2048]{1,0:T(8,128)S(1)} %fusion.10, bf16[2,512,1024]{2,1,0:T(8,128)(2,1)S(1)} %get-tuple-element.19, s32[]{:T(128)S(6)} %select_n.30, bf16[1,2048,1024]{2,1,0:T(8,128)(2,1)S(1)} %copy-done.8), kind=kOutput, calls=%fused_computation.18 | convolution fusion | flops 2149580800 | bytes 11534340 | tf_op jit(solution)/shard_map/dot_general | solution.py:60
  147.2 6.6 %all-to-all-start.2 = ((bf16[64,8,2048]{2,1,0:T(8,128)(2,1)}), bf16[64,8,2048]{2,1,0:T(8,128)(2,1)}, u32[]{:S(2)}, u32[]{:S(2)}) async-start(bf16[64,8,2048]{2,1,0:T(8,128)(2,1)} %fusion.6), calls=%async_computation.2 | async-start | bytes 4194304 | tf_op jit(solution)/shard_map/all_to_all | solution.py:61
  153.8 6.3 %copy.17 = bf16[2,512,2048]{1,2,0:T(8,128)(2,1)} copy(bf16[2,512,2048]{2,1,0:T(8,128)(2,1)} %bitcast.3) | data formatting | bytes 8388608 | tf_op jit(solution)/shard_map/optimization_barrier | solution.py:50
  160.1 0.0 copy-start.2
  160.1 0.0 copy-start.12
  160.1 6.0 %reduce-precision_reduce_fusion = bf16[1024,1024]{1,0:T(8,128)(2,1)} fusion(bf16[2,512,1024]{2,1,0:T(8,128)(2,1)S(1)} %get-tuple-element.13, bf16[2,512,2048]{1,2,0:T(8,128)(2,1)} %copy.17, s32[]{:T(128)S(6)} %select_n.29), kind=kOutput, calls=%fused_computation.4 | convolution fusion | flops 2150629376 | bytes 6291460 | tf_op jit(solution)/shard_map/srd,srf->sdf/dot_general | solution.py:68
  166.0 0.0 copy-done.2
  166.0 0.0 copy-done.12
  166.0 0.0 copy-start.10
  166.0 4.0 %reduce-precision_reduce_fusion.1 = bf16[1024,1024]{1,0:T(8,128)(2,1)} fusion(bf16[2,512,1024]{2,1,0:T(8,128)(2,1)S(1)} %copy-done.2, bf16[2,512,1024]{2,1,0:T(8,128)(2,1)S(1)} %copy-done.12), kind=kOutput, calls=%fused_computation.5 | convolution fusion | flops 2150629376 | bytes 6291456 | tf_op jit(solution)/shard_map/srd,srf->sdf/dot_general | solution.py:68
  170.1 0.0 copy-done.10
  170.1 0.0 copy-start.4
  170.1 0.0 copy-start.1
  170.1 4.0 %reduce-precision_reduce_fusion.2 = bf16[1024,1024]{1,0:T(8,128)(2,1)} fusion(bf16[2,512,1024]{2,1,0:T(8,128)(2,1)S(1)} %copy-done.2, bf16[2,512,1024]{2,1,0:T(8,128)(2,1)S(1)} %copy-done.10), kind=kOutput, calls=%fused_computation.6 | convolution fusion | flops 2150629376 | bytes 6291456 | tf_op jit(solution)/shard_map/srd,srf->sdf/dot_general | solution.py:68
  174.1 8.1 %all-to-all-done.2 = bf16[64,8,2048]{2,1,0:T(8,128)(2,1)} async-done(((bf16[64,8,2048]{2,1,0:T(8,128)(2,1)}), bf16[64,8,2048]{2,1,0:T(8,128)(2,1)}, u32[]{:S(2)}, u32[]{:S(2)}) %all-to-all-start.2) | async-done | bytes 2097184 | tf_op jit(solution)/shard_map/all_to_all | solution.py:61
  182.2 0.0 copy-done.4
  182.2 3.4 %convolution_convert_fusion.1 = bf16[256,2048]{1,0:T(8,128)(2,1)} fusion(bf16[64,8,2048]{2,1,0:T(8,128)(2,1)} %all-to-all-done.2, pred[1024,256]{1,0:T(32,128)(4,1)S(1)} %copy-done.4, pred[1024,256]{1,0:T(32,128)(4,1)S(1)} %get-tuple-element.21), kind=kOutput, calls=%fused_computation.19 | convolution fusion | flops 537526272 | bytes 3407872 | tf_op jit(solution)/shard_map/dot_general | solution.py:76
  185.6 0.0 copy-done.1
  (4 shorter events, 0.0 us)
Async XLA Ops:
  0.6 19.0 %copy-start = (bf16[256,2048]{1,0:T(8,128)(2,1)S(1)}, bf16[256,2048]{1,0:T(8,128)(2,1)}, u32[]{:S(2)}) copy-start(bf16[256,2048]{1,0:T(8,128)(2,1)} %param.9) | copy-start | bytes 3145732
  2.4 0.7 copy-start.3
  7.6 12.0 %copy-start.5 = (bf16[256,2]{0,1:T(2,128)(2,1)S(1)}, bf16[256,2]{0,1:T(2,128)(2,1)}, u32[]{:S(2)}) copy-start(bf16[256,2]{0,1:T(2,128)(2,1)} %param.10) | copy-start | bytes 3076
  7.6 63.2 %all-to-all-start.1 = ((bf16[128,8,2048]{2,1,0:T(8,128)(2,1)}), bf16[128,8,2048]{2,1,0:T(8,128)(2,1)}, u32[]{:S(2)}, u32[]{:S(2)}) async-start(bf16[128,8,2048]{2,1,0:T(8,128)(2,1)} %bitcast.51), calls=%async_computation.1 | async-start | bytes 8388608 | tf_op jit(solution)/shard_map/all_to_all | solution.py:33
  70.8 58.5 %all-to-all-start = ((bf16[128,8,2048]{2,1,0:T(8,128)(2,1)}), bf16[128,8,2048]{2,1,0:T(8,128)(2,1)}, u32[]{:S(2)}, u32[]{:S(2)}) async-start(bf16[128,8,2048]{2,1,0:T(8,128)(2,1)} %convert_bitcast_fusion), calls=%async_computation | async-start | bytes 8388608 | tf_op jit(solution)/shard_map/all_to_all | solution.py:36
  78.1 3.3 %copy-start.6 = (bf16[1,2048,1024]{2,1,0:T(8,128)(2,1)S(1)}, bf16[1,2048,1024]{2,1,0:T(8,128)(2,1)}, u32[]{:S(2)}) copy-start(bf16[1,2048,1024]{2,1,0:T(8,128)(2,1)} %param.13) | copy-start | bytes 12582916
  129.3 10.5 %copy-start.7 = (bf16[1,2048,1024]{2,1,0:T(8,128)(2,1)S(1)}, bf16[1,2048,1024]{2,1,0:T(8,128)(2,1)}, u32[]{:S(2)}) copy-start(bf16[1,2048,1024]{2,1,0:T(8,128)(2,1)} %param.13) | copy-start | bytes 12582916
  139.7 2.4 %copy-start.9 = (bf16[2,512,1024]{2,1,0:T(8,128)(2,1)}, bf16[2,512,1024]{2,1,0:T(8,128)(2,1)S(1)}, u32[]{:S(2)}) copy-start(bf16[2,512,1024]{2,1,0:T(8,128)(2,1)S(1)} %get-tuple-element.20) | copy-start | bytes 6291460
  139.8 2.4 %copy-start.11 = (bf16[2,512,1024]{2,1,0:T(8,128)(2,1)}, bf16[2,512,1024]{2,1,0:T(8,128)(2,1)S(1)}, u32[]{:S(2)}) copy-start(bf16[2,512,1024]{2,1,0:T(8,128)(2,1)S(1)} %get-tuple-element.19) | copy-start | bytes 6291460
  139.8 3.7 %copy-start.8 = (bf16[1,2048,1024]{2,1,0:T(8,128)(2,1)S(1)}, bf16[1,2048,1024]{2,1,0:T(8,128)(2,1)}, u32[]{:S(2)}) copy-start(bf16[1,2048,1024]{2,1,0:T(8,128)(2,1)} %param.14) | copy-start | bytes 12582916
  147.2 35.0 %all-to-all-start.2 = ((bf16[64,8,2048]{2,1,0:T(8,128)(2,1)}), bf16[64,8,2048]{2,1,0:T(8,128)(2,1)}, u32[]{:S(2)}, u32[]{:S(2)}) async-start(bf16[64,8,2048]{2,1,0:T(8,128)(2,1)} %fusion.6), calls=%async_computation.2 | async-start | bytes 4194304 | tf_op jit(solution)/shard_map/all_to_all | solution.py:61
  160.1 6.0 %copy-start.2 = (bf16[2,512,1024]{2,1,0:T(8,128)(2,1)S(1)}, bf16[2,512,1024]{2,1,0:T(8,128)(2,1)}, u32[]{:S(2)}) copy-start(bf16[2,512,1024]{2,1,0:T(8,128)(2,1)} %constant_dynamic-slice_fusion) | copy-start | bytes 6291460
  160.1 6.0 %copy-start.12 = (bf16[2,512,1024]{2,1,0:T(8,128)(2,1)S(1)}, bf16[2,512,1024]{2,1,0:T(8,128)(2,1)}, u32[]{:S(2)}) copy-start(bf16[2,512,1024]{2,1,0:T(8,128)(2,1)} %copy-done.11) | copy-start | bytes 6291460
  166.0 4.0 %copy-start.10 = (bf16[2,512,1024]{2,1,0:T(8,128)(2,1)S(1)}, bf16[2,512,1024]{2,1,0:T(8,128)(2,1)}, u32[]{:S(2)}) copy-start(bf16[2,512,1024]{2,1,0:T(8,128)(2,1)} %copy-done.9) | copy-start | bytes 6291460
  170.1 12.1 %copy-start.4 = (pred[1024,256]{1,0:T(32,128)(4,1)S(1)}, pred[1024,256]{1,0:T(32,128)(4,1)}, u32[]{:S(2)}) copy-start(pred[1024,256]{1,0:T(32,128)(4,1)} %copy-done.3) | copy-start | bytes 786436
  170.1 15.5 %copy-start.1 = (bf16[256,2048]{1,0:T(8,128)(2,1)S(1)}, bf16[256,2048]{1,0:T(8,128)(2,1)}, u32[]{:S(2)}) copy-start(bf16[256,2048]{1,0:T(8,128)(2,1)} %param.9) | copy-start | bytes 3145732

commit v15 on v7

--- a/solution.py
+++ b/solution.py
@@ -72,8 +72,10 @@
     grad_up = wgrad(x_half, up_grad)
     grad_down = wgrad(rg_half, act)
 
+    cols = lax.broadcasted_iota(jnp.int32, (cell_count, rows), 1)
+    gather = (cols == position[:, 0:1]) | (cols == position[:, 1:2])
     grad_tokens = jnp.dot(
-        pick[:rows].T, returned, preferred_element_type=jnp.float32
+        gather.astype(jnp.bfloat16), returned, preferred_element_type=jnp.float32
     ).astype(jnp.bfloat16)
     return grad_tokens, grad_gate, grad_up, grad_down
 

time: 182 us -> 182 us (level)
  transfers between devices with their start and end apart: 3 -> 3, of which waited for: 3 -> 3; matrix products, arithmetic and copies ran while one was open for 25% -> 24% of each run, Pallas kernels for 0% -> 0%
where the time goes in v15:
time: 182 us; the launch traced here: 181 us
  waiting for transfers between devices  87 us (48%)
  matrix products  50.9 us (28%)
  starting transfers between devices  25.6 us (14%)
  local copies, waits for them, and re-layouts  11.3 us (6%)
  other arithmetic  5.77 us (3%)
    all_to_all x1, waiting for transfers between devices, per_device(): lax.all_to_all(send_x.reshape(dp_count * group, slot_count, width), axes,...  47.9 us
    all_to_all x1, waiting for transfers between devices, per_device(): lax.all_to_all(send_rg.reshape(dp_count * group, slot_count, width), axes...  31.5 us
    dot_general x3, matrix products, wgrad(): jnp.einsum('srd,srf->sdf', left, right, preferred_element_type=jnp.float32)  14.6 us
    all_to_all x1, starting transfers between devices, per_device(): lax.all_to_all(send_x.reshape(dp_count * group, slot_count, width), axes,...  12 us
    dot_general x1, matrix products, per_device(): jnp.einsum('srd,df->srf', recv_x, wgu, preferred_element_type=jnp.float32)  11.4 us
    dot_general x1, matrix products, per_device(): jnp.einsum('srd,df->srf', recv_rg, wd, preferred_element_type=jnp.float32)  10.5 us
    all_to_all x1, waiting for transfers between devices, per_device(): lax.all_to_all(back.reshape(group, slot_count, width), ('seq', 'expert'),...  7.55 us
    all_to_all x1, starting transfers between devices, per_device(): lax.all_to_all(send_rg.reshape(dp_count * group, slot_count, width), axes...  7.27 us
  transfers between devices with their start and end apart: 3, of which 3 were waited for; matrix products, arithmetic and copies ran while one was open for 24% of the time, Pallas kernels for 0%

profile of v15, /device:TPU:1, one launch (start us, length us, event | category | flops | bytes accessed | tf_op | source)
XLA Modules:
  0.0 181.4 jit_solution(11262809799502400545)
XLA Ops:
  0.6 0.0 copy-start
  0.7 0.8 multiply_add_fusion
  1.5 0.4 copy-done
  1.9 3.2 %convert_bitcast_fusion = bf16[128,8,2048]{2,1,0:T(8,128)(2,1)} fusion(bf16[256,2048]{1,0:T(8,128)(2,1)S(1)} %copy-done, s32[256]{0:T(256)S(1)} %bitcast.55, s32[256]{0:T(256)S(1)} %bitcast.52, s32[1024]{0:T(1024)S(1)} %get-tuple-element.23, s32[1024]{0:T(1024)S(1)} %get-tuple-element.24, pred[1024]{0:T(1024)(128)(4,1)S(1)} %fusion.39), kind=kOutput, calls=%fused_computation.16 | convolution fusion | flops 1076887552 | bytes 5254144 | tf_op jit(solution)/shard_map/dot_general | solution.py:27
  5.1 0.0 copy-start.3
  5.1 0.0 copy-start.7
  5.1 12.0 %all-to-all-start.1 = ((bf16[128,8,2048]{2,1,0:T(8,128)(2,1)}), bf16[128,8,2048]{2,1,0:T(8,128)(2,1)}, u32[]{:S(2)}, u32[]{:S(2)}) async-start(bf16[128,8,2048]{2,1,0:T(8,128)(2,1)} %convert_bitcast_fusion), calls=%async_computation.1 | async-start | bytes 8388608 | tf_op jit(solution)/shard_map/all_to_all | solution.py:32
  17.1 0.0 copy-done.3
  17.1 0.0 copy-done.7
  17.1 3.3 %convert_bitcast_fusion.1 = bf16[128,8,2048]{2,1,0:T(8,128)(2,1)} fusion(bf16[256,2048]{1,0:T(8,128)(2,1)S(1)} %copy-done.7, s32[256]{0:T(256)S(1)} %bitcast.56, s32[256]{0:T(256)S(1)} %bitcast.53, s32[1024]{0:T(1024)S(1)} %get-tuple-element.23, s32[1024]{0:T(1024)S(1)} %get-tuple-element.24, pred[1024]{0:T(1024)(128)(4,1)S(1)} %fusion.39, ...), kind=kOutput, calls=%fused_computation.17 | convolution fusion | flops 1077149696 | bytes 5255168 | tf_op jit(solution)/shard_map/dot_general | solution.py:28
  20.4 47.9 %all-to-all-done.1 = bf16[128,8,2048]{2,1,0:T(8,128)(2,1)} async-done(((bf16[128,8,2048]{2,1,0:T(8,128)(2,1)}), bf16[128,8,2048]{2,1,0:T(8,128)(2,1)}, u32[]{:S(2)}, u32[]{:S(2)}) %all-to-all-start.1) | async-done | bytes 4194336 | tf_op jit(solution)/shard_map/all_to_all | solution.py:32
  68.3 7.3 %all-to-all-start = ((bf16[128,8,2048]{2,1,0:T(8,128)(2,1)}), bf16[128,8,2048]{2,1,0:T(8,128)(2,1)}, u32[]{:S(2)}, u32[]{:S(2)}) async-start(bf16[128,8,2048]{2,1,0:T(8,128)(2,1)} %convert_bitcast_fusion.1), calls=%async_computation | async-start | bytes 8388608 | tf_op jit(solution)/shard_map/all_to_all | solution.py:35
  75.6 0.0 copy-start.4
  75.6 3.2 %constant_dynamic-slice_fusion = bf16[2,512,1024]{2,1,0:T(8,128)(2,1)} fusion(bf16[2,512,2048]{2,1,0:T(8,128)(2,1)} %bitcast.5, s32[]{:T(128)S(6)} %select_n.29), kind=kLoop, calls=%fused_computation.64 | loop fusion | bytes 4194308 | tf_op jit(solution)/shard_map/dynamic_slice | solution.py:48
  78.9 0.0 copy-done.4
  78.9 11.4 %fusion = f32[2,512,2048]{2,1,0:T(8,128)S(1)} fusion(bf16[2,512,2048]{2,1,0:T(8,128)(2,1)} %bitcast.5, bf16[2048,1024]{1,0:T(8,128)(2,1)} %bitcast.59, bf16[2048,1024]{1,0:T(8,128)(2,1)S(1)} %bitcast.58), kind=kOutput, calls=%fused_computation.1 | convolution fusion | flops 8606711808 | bytes 20971520 | tf_op jit(solution)/shard_map/srd,df->srf/dot_general | solution.py:42
  90.3 5.0 %multiply_convert_fusion.2 = (bf16[2,512,1024]{2,1,0:T(8,128)(2,1)}, f32[2,512,1024]{2,1,0:T(8,128)}, f32[2,512,1024]{2,1,0:T(8,128)}) fusion(f32[2,512,2048]{2,1,0:T(8,128)S(1)} %fusion), kind=kLoop, calls=%fused_computation.12 | loop fusion | flops 11534336 | bytes 18874368 | tf_op jit(solution)/shard_map/convert_element_type | solution.py:46
  95.3 31.5 %all-to-all-done = bf16[128,8,2048]{2,1,0:T(8,128)(2,1)} async-done(((bf16[128,8,2048]{2,1,0:T(8,128)(2,1)}), bf16[128,8,2048]{2,1,0:T(8,128)(2,1)}, u32[]{:S(2)}, u32[]{:S(2)}) %all-to-all-start) | async-done | bytes 4194336 | tf_op jit(solution)/shard_map/all_to_all | solution.py:35
  126.8 0.0 copy-start.5
  126.8 10.5 %multiply_convert_fusion = (bf16[2,512,1024]{2,1,0:T(8,128)(2,1)S(1)}, bf16[2,512,1024]{2,1,0:T(8,128)(2,1)S(1)}) fusion(f32[2,512,1024]{2,1,0:T(8,128)} %get-tuple-element.11, f32[2,512,1024]{2,1,0:T(8,128)} %get-tuple-element.10, bf16[2,512,2048]{2,1,0:T(8,128)(2,1)} %bitcast.3, bf16[1,2048,1024]{2,1,0:T(8,128)(2,1)} %param.15), kind=kOutput, calls=%fused_computation.10 | convolution fusion | flops 4299161600 | bytes 20971520 | tf_op jit(solution)/shard_map/srd,df->srf/dot_general | solution.py:52
  137.3 0.0 copy-start.8
  137.3 0.0 copy-start.10
  137.3 0.0 copy-done.5
  137.3 0.0 copy-start.6
  137.3 2.4 %fusion.13 = f32[512,2048]{1,0:T(8,128)S(1)} fusion(bf16[2,512,1024]{2,1,0:T(8,128)(2,1)S(1)} %get-tuple-element.20, s32[]{:T(128)S(6)} %select_n.30, bf16[1,2048,1024]{2,1,0:T(8,128)(2,1)S(1)} %copy-done.5), kind=kOutput, calls=%fused_computation.31 | convolution fusion | flops 2147483648 | bytes 9437188 | tf_op jit(solution)/shard_map/dot_general | solution.py:58
  139.7 0.0 copy-done.8
  139.7 0.0 copy-done.10
  139.7 1.3 copy-done.6
  141.0 3.7 %fusion.6 = bf16[64,8,2048]{2,1,0:T(8,128)(2,1)} fusion(f32[512,2048]{1,0:T(8,128)S(1)} %fusion.13, bf16[2,512,1024]{2,1,0:T(8,128)(2,1)S(1)} %get-tuple-element.19, s32[]{:T(128)S(6)} %select_n.30, bf16[1,2048,1024]{2,1,0:T(8,128)(2,1)S(1)} %copy-done.6), kind=kOutput, calls=%fused_computation.18 | convolution fusion | flops 2149580800 | bytes 11534340 | tf_op jit(solution)/shard_map/dot_general | solution.py:59
  144.7 6.4 %all-to-all-start.2 = ((bf16[64,8,2048]{2,1,0:T(8,128)(2,1)}), bf16[64,8,2048]{2,1,0:T(8,128)(2,1)S(1)}, u32[]{:S(2)}, u32[]{:S(2)}) async-start(bf16[64,8,2048]{2,1,0:T(8,128)(2,1)} %fusion.6), calls=%async_computation.2 | async-start | bytes 4194304 | tf_op jit(solution)/shard_map/all_to_all | solution.py:60
  151.1 6.3 %copy.17 = bf16[2,512,2048]{1,2,0:T(8,128)(2,1)} copy(bf16[2,512,2048]{2,1,0:T(8,128)(2,1)} %bitcast.3) | data formatting | bytes 8388608 | tf_op jit(solution)/shard_map/optimization_barrier | solution.py:49
  157.4 0.0 copy-start.2
  157.4 0.0 copy-start.11
  157.4 6.6 %reduce-precision_reduce_fusion = bf16[1024,1024]{1,0:T(8,128)(2,1)} fusion(bf16[2,512,1024]{2,1,0:T(8,128)(2,1)} %get-tuple-element.13, bf16[2,512,2048]{1,2,0:T(8,128)(2,1)} %copy.17, s32[]{:T(128)S(6)} %select_n.29), kind=kOutput, calls=%fused_computation.4 | convolution fusion | flops 2150629376 | bytes 6291460 | tf_op jit(solution)/shard_map/srd,srf->sdf/dot_general | solution.py:67
  164.0 0.0 copy-done.2
  164.0 0.0 copy-done.11
  164.0 0.0 copy-start.9
  164.0 4.0 %reduce-precision_reduce_fusion.1 = bf16[1024,1024]{1,0:T(8,128)(2,1)} fusion(bf16[2,512,1024]{2,1,0:T(8,128)(2,1)S(1)} %copy-done.2, bf16[2,512,1024]{2,1,0:T(8,128)(2,1)S(1)} %copy-done.11), kind=kOutput, calls=%fused_computation.5 | convolution fusion | flops 2150629376 | bytes 6291456 | tf_op jit(solution)/shard_map/srd,srf->sdf/dot_general | solution.py:67
  168.0 0.0 copy-done.9
  168.0 0.0 copy-start.1
  168.0 4.0 %reduce-precision_reduce_fusion.2 = bf16[1024,1024]{1,0:T(8,128)(2,1)} fusion(bf16[2,512,1024]{2,1,0:T(8,128)(2,1)S(1)} %copy-done.2, bf16[2,512,1024]{2,1,0:T(8,128)(2,1)S(1)} %copy-done.9), kind=kOutput, calls=%fused_computation.6 | convolution fusion | flops 2150629376 | bytes 6291456 | tf_op jit(solution)/shard_map/srd,srf->sdf/dot_general | solution.py:67
  172.0 7.6 %all-to-all-done.2 = bf16[64,8,2048]{2,1,0:T(8,128)(2,1)S(1)} async-done(((bf16[64,8,2048]{2,1,0:T(8,128)(2,1)}), bf16[64,8,2048]{2,1,0:T(8,128)(2,1)S(1)}, u32[]{:S(2)}, u32[]{:S(2)}) %all-to-all-start.2) | async-done | bytes 2097184 | tf_op jit(solution)/shard_map/all_to_all | solution.py:60
  179.6 1.8 convolution_convert_fusion
  181.4 0.0 copy-done.1
  (4 shorter events, 0.0 us)
Async XLA Ops:
  0.6 1.3 copy-start
  5.1 12.0 %copy-start.3 = (bf16[256,2]{0,1:T(2,128)(2,1)S(1)}, bf16[256,2]{0,1:T(2,128)(2,1)}, u32[]{:S(2)}) copy-start(bf16[256,2]{0,1:T(2,128)(2,1)} %param.10) | copy-start | bytes 3076
  5.1 12.0 %copy-start.7 = (bf16[256,2048]{1,0:T(8,128)(2,1)S(1)}, bf16[256,2048]{1,0:T(8,128)(2,1)}, u32[]{:S(2)}) copy-start(bf16[256,2048]{1,0:T(8,128)(2,1)} %param.9) | copy-start | bytes 3145732
  5.1 63.2 %all-to-all-start.1 = ((bf16[128,8,2048]{2,1,0:T(8,128)(2,1)}), bf16[128,8,2048]{2,1,0:T(8,128)(2,1)}, u32[]{:S(2)}, u32[]{:S(2)}) async-start(bf16[128,8,2048]{2,1,0:T(8,128)(2,1)} %convert_bitcast_fusion), calls=%async_computation.1 | async-start | bytes 8388608 | tf_op jit(solution)/shard_map/all_to_all | solution.py:32
  68.3 58.5 %all-to-all-start = ((bf16[128,8,2048]{2,1,0:T(8,128)(2,1)}), bf16[128,8,2048]{2,1,0:T(8,128)(2,1)}, u32[]{:S(2)}, u32[]{:S(2)}) async-start(bf16[128,8,2048]{2,1,0:T(8,128)(2,1)} %convert_bitcast_fusion.1), calls=%async_computation | async-start | bytes 8388608 | tf_op jit(solution)/shard_map/all_to_all | solution.py:35
  75.6 3.3 %copy-start.4 = (bf16[1,2048,1024]{2,1,0:T(8,128)(2,1)S(1)}, bf16[1,2048,1024]{2,1,0:T(8,128)(2,1)}, u32[]{:S(2)}) copy-start(bf16[1,2048,1024]{2,1,0:T(8,128)(2,1)} %param.13) | copy-start | bytes 12582916
  126.8 10.5 %copy-start.5 = (bf16[1,2048,1024]{2,1,0:T(8,128)(2,1)S(1)}, bf16[1,2048,1024]{2,1,0:T(8,128)(2,1)}, u32[]{:S(2)}) copy-start(bf16[1,2048,1024]{2,1,0:T(8,128)(2,1)} %param.13) | copy-start | bytes 12582916
  137.3 2.4 %copy-start.8 = (bf16[2,512,1024]{2,1,0:T(8,128)(2,1)}, bf16[2,512,1024]{2,1,0:T(8,128)(2,1)S(1)}, u32[]{:S(2)}) copy-start(bf16[2,512,1024]{2,1,0:T(8,128)(2,1)S(1)} %get-tuple-element.20) | copy-start | bytes 6291460
  137.3 2.4 %copy-start.10 = (bf16[2,512,1024]{2,1,0:T(8,128)(2,1)}, bf16[2,512,1024]{2,1,0:T(8,128)(2,1)S(1)}, u32[]{:S(2)}) copy-start(bf16[2,512,1024]{2,1,0:T(8,128)(2,1)S(1)} %get-tuple-element.19) | copy-start | bytes 6291460
  137.3 3.7 %copy-start.6 = (bf16[1,2048,1024]{2,1,0:T(8,128)(2,1)S(1)}, bf16[1,2048,1024]{2,1,0:T(8,128)(2,1)}, u32[]{:S(2)}) copy-start(bf16[1,2048,1024]{2,1,0:T(8,128)(2,1)} %param.14) | copy-start | bytes 12582916
  144.7 34.9 %all-to-all-start.2 = ((bf16[64,8,2048]{2,1,0:T(8,128)(2,1)}), bf16[64,8,2048]{2,1,0:T(8,128)(2,1)S(1)}, u32[]{:S(2)}, u32[]{:S(2)}) async-start(bf16[64,8,2048]{2,1,0:T(8,128)(2,1)} %fusion.6), calls=%async_computation.2 | async-start | bytes 4194304 | tf_op jit(solution)/shard_map/all_to_all | solution.py:60
  157.4 6.6 %copy-start.2 = (bf16[2,512,1024]{2,1,0:T(8,128)(2,1)S(1)}, bf16[2,512,1024]{2,1,0:T(8,128)(2,1)}, u32[]{:S(2)}) copy-start(bf16[2,512,1024]{2,1,0:T(8,128)(2,1)} %constant_dynamic-slice_fusion) | copy-start | bytes 6291460
  157.4 6.6 %copy-start.11 = (bf16[2,512,1024]{2,1,0:T(8,128)(2,1)S(1)}, bf16[2,512,1024]{2,1,0:T(8,128)(2,1)}, u32[]{:S(2)}) copy-start(bf16[2,512,1024]{2,1,0:T(8,128)(2,1)} %copy-done.10) | copy-start | bytes 6291460
  164.0 4.0 %copy-start.9 = (bf16[2,512,1024]{2,1,0:T(8,128)(2,1)S(1)}, bf16[2,512,1024]{2,1,0:T(8,128)(2,1)}, u32[]{:S(2)}) copy-start(bf16[2,512,1024]{2,1,0:T(8,128)(2,1)} %copy-done.8) | copy-start | bytes 6291460
  168.0 13.3 %copy-start.1 = (bf16[256,2048]{1,0:T(8,128)(2,1)S(1)}, bf16[256,2048]{1,0:T(8,128)(2,1)}, u32[]{:S(2)}) copy-start(bf16[256,2048]{1,0:T(8,128)(2,1)} %param.8) | copy-start | bytes 3145732

commit v16 on v13

--- a/solution.py
+++ b/solution.py
@@ -72,8 +72,10 @@
     grad_up = wgrad(x_half, up_grad)
     grad_down = wgrad(rg_half, act)
 
+    cols = lax.broadcasted_iota(jnp.int32, (cell_count, rows), 1)
+    gather = (cols == position[:, 0:1]) | (cols == position[:, 1:2])
     grad_tokens = jnp.dot(
-        pick[:rows].T, returned, preferred_element_type=jnp.float32
+        gather.astype(jnp.bfloat16), returned, preferred_element_type=jnp.float32
     ).astype(jnp.bfloat16)
     return grad_tokens, grad_gate, grad_up, grad_down
 

time: 182 us -> 182 us (level)
  transfers between devices with their start and end apart: 3 -> 3, of which waited for: 3 -> 3; matrix products, arithmetic and copies ran while one was open for 25% -> 24% of each run, Pallas kernels for 0% -> 0%
where the time goes in v16:
time: 182 us
  waiting for transfers between devices  86.5 us (48%)
  matrix products  51.2 us (28%)
  starting transfers between devices  25.6 us (14%)
  local copies, waits for them, and re-layouts  12 us (7%)
  other arithmetic  5.77 us (3%)
    all_to_all x1, waiting for transfers between devices, per_device(): lax.all_to_all(send_x.reshape(dp_count * group, slot_count, width), axes,...  47.9 us
    all_to_all x1, waiting for transfers between devices, per_device(): lax.all_to_all(send_rg.reshape(dp_count * group, slot_count, width), axes...  31 us
    dot_general x3, matrix products, wgrad(): jnp.einsum('srd,srf->sdf', left, right, preferred_element_type=jnp.float32)  14.6 us
    all_to_all x1, starting transfers between devices, per_device(): lax.all_to_all(send_x.reshape(dp_count * group, slot_count, width), axes,...  12 us
    dot_general x1, matrix products, per_device(): jnp.einsum('srd,df->srf', recv_x, wgu, preferred_element_type=jnp.float32)  11.9 us
    dot_general x1, matrix products, per_device(): jnp.einsum('srd,df->srf', recv_rg, wd, preferred_element_type=jnp.float32)  10.5 us
    all_to_all x1, waiting for transfers between devices, per_device(): lax.all_to_all(back.reshape(group, slot_count, width), ('seq', 'expert'),...  7.56 us
    all_to_all x1, starting transfers between devices, per_device(): lax.all_to_all(send_rg.reshape(dp_count * group, slot_count, width), axes...  7.29 us
  transfers between devices with their start and end apart: 3, of which 3 were waited for; matrix products, arithmetic and copies ran while one was open for 24% of the time, Pallas kernels for 0%

profile of v16, /device:TPU:1, one launch (start us, length us, event | category | flops | bytes accessed | tf_op | source)
XLA Modules:
  0.0 181.7 jit_solution(10059455478639233127)
XLA Ops:
  0.6 0.0 copy-start
  0.7 0.8 multiply_add_fusion
  1.5 0.4 copy-done
  1.9 3.2 %convert_bitcast_fusion = bf16[128,8,2048]{2,1,0:T(8,128)(2,1)} fusion(bf16[256,2048]{1,0:T(8,128)(2,1)S(1)} %copy-done, s32[256]{0:T(256)S(1)} %bitcast.48, s32[256]{0:T(256)S(1)} %bitcast.45, s32[1024]{0:T(1024)S(1)} %get-tuple-element.23, s32[1024]{0:T(1024)S(1)} %get-tuple-element.24, pred[1024]{0:T(1024)(128)(4,1)S(1)} %fusion.38), kind=kOutput, calls=%fused_computation.17 | convolution fusion | flops 1076887552 | bytes 5254144 | tf_op jit(solution)/shard_map/dot_general | solution.py:27
  5.1 0.0 copy-start.3
  5.1 0.0 copy-start.7
  5.1 12.0 %all-to-all-start.1 = ((bf16[128,8,2048]{2,1,0:T(8,128)(2,1)}), bf16[128,8,2048]{2,1,0:T(8,128)(2,1)}, u32[]{:S(2)}, u32[]{:S(2)}) async-start(bf16[128,8,2048]{2,1,0:T(8,128)(2,1)} %convert_bitcast_fusion), calls=%async_computation.1 | async-start | bytes 8388608 | tf_op jit(solution)/shard_map/all_to_all | solution.py:32
  17.1 0.0 copy-done.3
  17.1 0.0 copy-done.7
  17.1 3.3 %convert_bitcast_fusion.1 = bf16[128,8,2048]{2,1,0:T(8,128)(2,1)} fusion(bf16[256,2048]{1,0:T(8,128)(2,1)S(1)} %copy-done.7, s32[256]{0:T(256)S(1)} %bitcast.49, s32[256]{0:T(256)S(1)} %bitcast.46, s32[1024]{0:T(1024)S(1)} %get-tuple-element.23, s32[1024]{0:T(1024)S(1)} %get-tuple-element.24, pred[1024]{0:T(1024)(128)(4,1)S(1)} %fusion.38, ...), kind=kOutput, calls=%fused_computation.18 | convolution fusion | flops 1077149696 | bytes 5255168 | tf_op jit(solution)/shard_map/dot_general | solution.py:28
  20.4 47.9 %all-to-all-done.1 = bf16[128,8,2048]{2,1,0:T(8,128)(2,1)} async-done(((bf16[128,8,2048]{2,1,0:T(8,128)(2,1)}), bf16[128,8,2048]{2,1,0:T(8,128)(2,1)}, u32[]{:S(2)}, u32[]{:S(2)}) %all-to-all-start.1) | async-done | bytes 4194336 | tf_op jit(solution)/shard_map/all_to_all | solution.py:32
  68.3 7.3 %all-to-all-start = ((bf16[128,8,2048]{2,1,0:T(8,128)(2,1)}), bf16[128,8,2048]{2,1,0:T(8,128)(2,1)}, u32[]{:S(2)}, u32[]{:S(2)}) async-start(bf16[128,8,2048]{2,1,0:T(8,128)(2,1)} %convert_bitcast_fusion.1), calls=%async_computation | async-start | bytes 8388608 | tf_op jit(solution)/shard_map/all_to_all | solution.py:35
  75.6 0.0 copy-start.4
  75.6 3.2 %constant_dynamic-slice_fusion = bf16[2,512,1024]{2,1,0:T(8,128)(2,1)} fusion(bf16[2,512,2048]{2,1,0:T(8,128)(2,1)} %bitcast.5, s32[]{:T(128)S(6)} %select_n.28), kind=kLoop, calls=%fused_computation.62 | loop fusion | bytes 4194308 | tf_op jit(solution)/shard_map/dynamic_slice | solution.py:48
  78.9 0.0 copy-done.4
  78.9 11.9 %fusion = f32[2,512,2048]{2,1,0:T(8,128)S(1)} fusion(bf16[2,512,2048]{2,1,0:T(8,128)(2,1)} %bitcast.5, bf16[2048,1024]{1,0:T(8,128)(2,1)S(1)} %bitcast.51, bf16[2048,1024]{1,0:T(8,128)(2,1)} %bitcast.53), kind=kOutput, calls=%fused_computation.1 | convolution fusion | flops 8606711808 | bytes 20971520 | tf_op jit(solution)/shard_map/srd,df->srf/dot_general | solution.py:42
  90.8 5.0 %multiply_convert_fusion.2 = (bf16[2,512,1024]{2,1,0:T(8,128)(2,1)}, f32[2,512,1024]{2,1,0:T(8,128)}, f32[2,512,1024]{2,1,0:T(8,128)}) fusion(f32[2,512,2048]{2,1,0:T(8,128)S(1)} %fusion), kind=kLoop, calls=%fused_computation.13 | loop fusion | flops 11534336 | bytes 18874368 | tf_op jit(solution)/shard_map/convert_element_type | solution.py:46
  95.8 31.0 %all-to-all-done = bf16[128,8,2048]{2,1,0:T(8,128)(2,1)} async-done(((bf16[128,8,2048]{2,1,0:T(8,128)(2,1)}), bf16[128,8,2048]{2,1,0:T(8,128)(2,1)}, u32[]{:S(2)}, u32[]{:S(2)}) %all-to-all-start) | async-done | bytes 4194336 | tf_op jit(solution)/shard_map/all_to_all | solution.py:35
  126.8 0.0 copy-start.5
  126.8 0.0 copy-start.6
  126.8 10.5 %multiply_convert_fusion = (bf16[2,512,1024]{2,1,0:T(8,128)(2,1)S(1)}, bf16[2,512,1024]{2,1,0:T(8,128)(2,1)S(1)}) fusion(f32[2,512,1024]{2,1,0:T(8,128)} %get-tuple-element.11, f32[2,512,1024]{2,1,0:T(8,128)} %get-tuple-element.10, bf16[2,512,2048]{2,1,0:T(8,128)(2,1)} %bitcast.3, bf16[1,2048,1024]{2,1,0:T(8,128)(2,1)} %param.15), kind=kOutput, calls=%fused_computation.11 | convolution fusion | flops 4299161600 | bytes 20971520 | tf_op jit(solution)/shard_map/srd,df->srf/dot_general | solution.py:52
  137.3 0.0 copy-start.8
  137.3 0.0 copy-start.10
  137.3 1.3 copy-done.8
  138.7 0.6 copy-done.10
  139.2 0.0 copy-done.5
  139.2 0.0 copy-done.6
  139.2 5.9 %fusion.7 = bf16[64,8,2048]{2,1,0:T(8,128)(2,1)} fusion(bf16[2048,1024]{1,0:T(8,128)(2,1)S(1)} %bitcast.52, bf16[2048,1024]{1,0:T(8,128)(2,1)S(1)} %bitcast.54, s32[]{:T(128)S(6)} %select_n.29, bf16[2,512,1024]{2,1,0:T(8,128)(2,1)S(1)} %get-tuple-element.20, bf16[2,512,1024]{2,1,0:T(8,128)(2,1)S(1)} %get-tuple-element.19), kind=kOutput, calls=%fused_computation.20 | convolution fusion | flops 4316987392 | bytes 14680068 | tf_op jit(solution)/shard_map/dot_general | solution.py:59
  145.1 6.4 %all-to-all-start.2 = ((bf16[64,8,2048]{2,1,0:T(8,128)(2,1)}), bf16[64,8,2048]{2,1,0:T(8,128)(2,1)S(1)}, u32[]{:S(2)}, u32[]{:S(2)}) async-start(bf16[64,8,2048]{2,1,0:T(8,128)(2,1)} %fusion.7), calls=%async_computation.2 | async-start | bytes 4194304 | tf_op jit(solution)/shard_map/all_to_all | solution.py:60
  151.5 6.3 %copy.17 = bf16[2,512,2048]{1,2,0:T(8,128)(2,1)} copy(bf16[2,512,2048]{2,1,0:T(8,128)(2,1)} %bitcast.3) | data formatting | bytes 8388608 | tf_op jit(solution)/shard_map/optimization_barrier | solution.py:49
  157.8 0.0 copy-start.2
  157.8 0.0 copy-start.11
  157.8 6.6 %reduce-precision_reduce_fusion = bf16[1024,1024]{1,0:T(8,128)(2,1)} fusion(bf16[2,512,1024]{2,1,0:T(8,128)(2,1)} %get-tuple-element.13, bf16[2,512,2048]{1,2,0:T(8,128)(2,1)} %copy.17, s32[]{:T(128)S(6)} %select_n.28), kind=kOutput, calls=%fused_computation.3 | convolution fusion | flops 2150629376 | bytes 6291460 | tf_op jit(solution)/shard_map/srd,srf->sdf/dot_general | solution.py:67
  164.4 0.0 copy-done.2
  164.4 0.0 copy-done.11
  164.4 0.0 copy-start.9
  164.4 4.0 %reduce-precision_reduce_fusion.1 = bf16[1024,1024]{1,0:T(8,128)(2,1)} fusion(bf16[2,512,1024]{2,1,0:T(8,128)(2,1)S(1)} %copy-done.2, bf16[2,512,1024]{2,1,0:T(8,128)(2,1)S(1)} %copy-done.11), kind=kOutput, calls=%fused_computation.4 | convolution fusion | flops 2150629376 | bytes 6291456 | tf_op jit(solution)/shard_map/srd,srf->sdf/dot_general | solution.py:67
  168.4 0.0 copy-done.9
  168.4 0.0 copy-start.1
  168.4 4.0 %reduce-precision_reduce_fusion.2 = bf16[1024,1024]{1,0:T(8,128)(2,1)} fusion(bf16[2,512,1024]{2,1,0:T(8,128)(2,1)S(1)} %copy-done.2, bf16[2,512,1024]{2,1,0:T(8,128)(2,1)S(1)} %copy-done.9), kind=kOutput, calls=%fused_computation.5 | convolution fusion | flops 2150629376 | bytes 6291456 | tf_op jit(solution)/shard_map/srd,srf->sdf/dot_general | solution.py:67
  172.4 7.6 %all-to-all-done.2 = bf16[64,8,2048]{2,1,0:T(8,128)(2,1)S(1)} async-done(((bf16[64,8,2048]{2,1,0:T(8,128)(2,1)}), bf16[64,8,2048]{2,1,0:T(8,128)(2,1)S(1)}, u32[]{:S(2)}, u32[]{:S(2)}) %all-to-all-start.2) | async-done | bytes 2097184 | tf_op jit(solution)/shard_map/all_to_all | solution.py:60
  180.0 1.8 convolution_convert_fusion
  181.7 0.0 copy-done.1
  (4 shorter events, 0.0 us)
Async XLA Ops:
  0.6 1.3 copy-start
  5.1 12.0 %copy-start.3 = (bf16[256,2]{0,1:T(2,128)(2,1)S(1)}, bf16[256,2]{0,1:T(2,128)(2,1)}, u32[]{:S(2)}) copy-start(bf16[256,2]{0,1:T(2,128)(2,1)} %param.10) | copy-start | bytes 3076
  5.1 12.0 %copy-start.7 = (bf16[256,2048]{1,0:T(8,128)(2,1)S(1)}, bf16[256,2048]{1,0:T(8,128)(2,1)}, u32[]{:S(2)}) copy-start(bf16[256,2048]{1,0:T(8,128)(2,1)} %param.9) | copy-start | bytes 3145732
  5.1 63.2 %all-to-all-start.1 = ((bf16[128,8,2048]{2,1,0:T(8,128)(2,1)}), bf16[128,8,2048]{2,1,0:T(8,128)(2,1)}, u32[]{:S(2)}, u32[]{:S(2)}) async-start(bf16[128,8,2048]{2,1,0:T(8,128)(2,1)} %convert_bitcast_fusion), calls=%async_computation.1 | async-start | bytes 8388608 | tf_op jit(solution)/shard_map/all_to_all | solution.py:32
  68.3 58.5 %all-to-all-start = ((bf16[128,8,2048]{2,1,0:T(8,128)(2,1)}), bf16[128,8,2048]{2,1,0:T(8,128)(2,1)}, u32[]{:S(2)}, u32[]{:S(2)}) async-start(bf16[128,8,2048]{2,1,0:T(8,128)(2,1)} %convert_bitcast_fusion.1), calls=%async_computation | async-start | bytes 8388608 | tf_op jit(solution)/shard_map/all_to_all | solution.py:35
  75.6 3.3 %copy-start.4 = (bf16[1,2048,1024]{2,1,0:T(8,128)(2,1)S(1)}, bf16[1,2048,1024]{2,1,0:T(8,128)(2,1)}, u32[]{:S(2)}) copy-start(bf16[1,2048,1024]{2,1,0:T(8,128)(2,1)} %param.14) | copy-start | bytes 12582916
  126.8 12.4 %copy-start.5 = (bf16[1,2048,1024]{2,1,0:T(8,128)(2,1)S(1)}, bf16[1,2048,1024]{2,1,0:T(8,128)(2,1)}, u32[]{:S(2)}) copy-start(bf16[1,2048,1024]{2,1,0:T(8,128)(2,1)} %param.14) | copy-start | bytes 12582916
  126.8 12.4 %copy-start.6 = (bf16[1,2048,1024]{2,1,0:T(8,128)(2,1)S(1)}, bf16[1,2048,1024]{2,1,0:T(8,128)(2,1)}, u32[]{:S(2)}) copy-start(bf16[1,2048,1024]{2,1,0:T(8,128)(2,1)} %param.13) | copy-start | bytes 12582916
  137.3 1.4 copy-start.8
  137.3 1.9 %copy-start.10 = (bf16[2,512,1024]{2,1,0:T(8,128)(2,1)}, bf16[2,512,1024]{2,1,0:T(8,128)(2,1)S(1)}, u32[]{:S(2)}) copy-start(bf16[2,512,1024]{2,1,0:T(8,128)(2,1)S(1)} %get-tuple-element.19) | copy-start | bytes 6291460
  145.1 34.9 %all-to-all-start.2 = ((bf16[64,8,2048]{2,1,0:T(8,128)(2,1)}), bf16[64,8,2048]{2,1,0:T(8,128)(2,1)S(1)}, u32[]{:S(2)}, u32[]{:S(2)}) async-start(bf16[64,8,2048]{2,1,0:T(8,128)(2,1)} %fusion.7), calls=%async_computation.2 | async-start | bytes 4194304 | tf_op jit(solution)/shard_map/all_to_all | solution.py:60
  157.8 6.6 %copy-start.2 = (bf16[2,512,1024]{2,1,0:T(8,128)(2,1)S(1)}, bf16[2,512,1024]{2,1,0:T(8,128)(2,1)}, u32[]{:S(2)}) copy-start(bf16[2,512,1024]{2,1,0:T(8,128)(2,1)} %constant_dynamic-slice_fusion) | copy-start | bytes 6291460
  157.8 6.6 %copy-start.11 = (bf16[2,512,1024]{2,1,0:T(8,128)(2,1)S(1)}, bf16[2,512,1024]{2,1,0:T(8,128)(2,1)}, u32[]{:S(2)}) copy-start(bf16[2,512,1024]{2,1,0:T(8,128)(2,1)} %copy-done.10) | copy-start | bytes 6291460
  164.4 4.0 %copy-start.9 = (bf16[2,512,1024]{2,1,0:T(8,128)(2,1)S(1)}, bf16[2,512,1024]{2,1,0:T(8,128)(2,1)}, u32[]{:S(2)}) copy-start(bf16[2,512,1024]{2,1,0:T(8,128)(2,1)} %copy-done.8) | copy-start | bytes 6291460
  168.4 13.3 %copy-start.1 = (bf16[256,2048]{1,0:T(8,128)(2,1)S(1)}, bf16[256,2048]{1,0:T(8,128)(2,1)}, u32[]{:S(2)}) copy-start(bf16[256,2048]{1,0:T(8,128)(2,1)} %param.8) | copy-start | bytes 3145732
